TPU v7x, 256 devices: a whole 4x4x8 slice. The times are simulated.
256 devices in a mesh: depth: 8 (over x, core), tile: 32 (over y, z).
Axes of the slice: x: 4, y: 4, z: 8, core: 2. Of those that a mesh axis runs over, the one named last changes fastest.
Arguments:
- volume: bfloat16 [512, 512, 1024], P('depth', 'tile'), may hold values from -6 to 6
- knot_pos: int32 [16], replicated, may hold values from 0 to 255, as said below
- knot_color: int32 [4, 16], replicated, may hold values from 0 to 255
Outputs:
- image: float32 [4, 512, 1024], P(None, 'tile', 'depth')
Inputs may be any that keep to these rules, and one draw needn't show every extreme that they name: `knot_pos`: strictly increasing with neighbouring breakpoints 9 or more apart; the first is 0 and the last 255.
All inputs are finite; a program needn't handle non-finite values.
Results may differ from a plain program's by a relative error of at most 0.0003.
Values may be sent and summed in bfloat16 or wider, within the bound.
No kernel may reach another device: no remote copies, remote signals or barrier semaphores. Data moves between devices by JAX's collectives and lax.ppermute only.
A program may use at most 128 MiB of HBM per device.

v0:
```python
import jax
import jax.numpy as jnp
from jax import lax
from jax.sharding import PartitionSpec as P


def padded(block, sides, width):
    for axis, dim in sides:
        count = lax.axis_size(axis)
        forward = [(i, i + 1) for i in range(count - 1)]
        backward = [(target, source) for source, target in forward]
        low = lax.ppermute(
            lax.slice_in_dim(block, block.shape[dim] - width, None, axis=dim), axis, forward
        )
        high = lax.ppermute(lax.slice_in_dim(block, 0, width, axis=dim), axis, backward)
        block = jnp.concatenate([low, block, high], axis=dim)
    return block


def carried_in(value, axis, join, neutral):
    count, mine = (lax.axis_size(axis), lax.axis_index(axis))
    pieces = lax.all_gather(value, axis)
    subtotal = jnp.full_like(value, 0) + jnp.asarray(neutral, value.dtype)

    def hop(position, subtotal):
        longer = join(subtotal, pieces[position])
        return jnp.where(position < mine, longer, subtotal)

    return lax.fori_loop(0, count - 1, hop, subtotal)


def next_along(center):
    return jnp.pad(center[:, :, 1:], ((0, 0), (0, 0), (0, 1)))


def prior_along(center):
    return jnp.pad(center[:, :, :-1], ((0, 0), (0, 0), (1, 0)))


def smooth_block(extended):
    field = extended.astype(jnp.float32)
    center = field[1:-1, 1:-1]
    neighbours = field[2:, 1:-1] + field[:-2, 1:-1] + field[1:-1, 2:] + field[1:-1, :-2]
    neighbours = neighbours + next_along(center) + prior_along(center)
    return 0.4 * center + 0.1 * neighbours


def hat_colors(lookup, knot_pos, knot_color):
    knot_float = knot_pos.astype(jnp.float32)
    palette = knot_color.astype(jnp.float32) / 255.0
    count = knot_pos.shape[0]
    colors = [jnp.zeros_like(lookup) for c in range(3)]
    extinction = jnp.zeros_like(lookup)
    for k in range(count):
        if k == 0:
            weight = jnp.clip((knot_float[1] - lookup) / (knot_float[1] - knot_float[0]), 0.0, 1.0)
        elif k == count - 1:
            weight = jnp.clip(
                (lookup - knot_float[k - 1]) / (knot_float[k] - knot_float[k - 1]), 0.0, 1.0
            )
        else:
            rising = (lookup - knot_float[k - 1]) / (knot_float[k] - knot_float[k - 1])
            falling = (knot_float[k + 1] - lookup) / (knot_float[k + 1] - knot_float[k])
            weight = jnp.maximum(0.0, jnp.minimum(rising, falling))
        colors = [colors[c] + weight * palette[c, k] for c in range(3)]
        extinction = extinction + weight * palette[3, k]
    return (colors, extinction)


def shade_classify(smooth_ext, knot_pos, knot_color, sigma_scale):
    field = smooth_ext.astype(jnp.float32)
    center = field[1:-1, 1:-1]
    slope_z = 0.5 * (field[2:, 1:-1] - field[:-2, 1:-1])
    slope_x = 0.5 * (field[1:-1, 2:] - field[1:-1, :-2])
    slope_y = 0.5 * (next_along(center) - prior_along(center))
    facing = jnp.abs(0.6 * slope_z + 0.8 * slope_x)
    shading = 0.3 + 0.7 * facing / jnp.sqrt(
        slope_z * slope_z + slope_x * slope_x + slope_y * slope_y + 0.1
    )
    knot_float = knot_pos.astype(jnp.float32)
    lookup = jnp.clip(127.5 + 70.0 * center, knot_float[0], knot_float[-1])
    colors, extinction = hat_colors(lookup, knot_pos, knot_color)
    return (shading, colors, extinction * sigma_scale)


def composite(shading, colors, extinction):
    before = jnp.cumsum(extinction, axis=0) - extinction
    weight = shading * (1.0 - jnp.exp(-extinction)) * jnp.exp(-before)
    brick_color = jnp.stack([jnp.sum(weight * colors[c], axis=0) for c in range(3)])
    return (brick_color, jnp.sum(extinction, axis=0))


def add_terms(earlier, later):
    return earlier + later


def body(volume, knot_pos, knot_color):
    depth_count = lax.axis_size("depth")
    brick_depth, brick_rows, row_width = volume.shape
    sigma_scale = 4.0 / (brick_depth * depth_count)
    extended = padded(volume, (("depth", 0), ("tile", 1)), 1)
    smoothed = smooth_block(extended).astype(jnp.bfloat16)
    smooth_ext = padded(smoothed, (("depth", 0), ("tile", 1)), 1)
    shading, colors, extinction = shade_classify(smooth_ext, knot_pos, knot_color, sigma_scale)
    brick_color, optical_depth = composite(shading, colors, extinction)
    optical_ahead = carried_in(optical_depth, "depth", add_terms, jnp.zeros_like(optical_depth))
    attenuation = jnp.exp(-optical_ahead)
    weighted = jnp.concatenate([brick_color * attenuation[None], optical_depth[None]], axis=0)
    merged = lax.psum_scatter(weighted, "depth", scatter_dimension=2, tiled=True)
    return jnp.concatenate([merged[:3], 1.0 - jnp.exp(-merged[3:])], axis=0)


def solution(mesh):
    in_specs = (P("depth", "tile", None), P(), P())
    out_specs = P(None, "tile", "depth")
    return jax.shard_map(body, mesh=mesh, in_specs=in_specs, out_specs=out_specs, check_vma=False)
```

profile of v0, /device:TPU:24, one launch (start us, length us, event | category | flops | bytes accessed | tf_op | source)
XLA Modules:
  0.0 314.6 jit_solution(5360344120375077640)
XLA Ops:
  6.5 0.0 copy-start.4
  6.5 0.0 reduce-scatter.2.cloned.1.call-start
  6.5 0.8 fusion.15
  7.3 1.7 collective-permute-start
  9.1 1.3 collective-permute-start.1
  10.4 0.7 convert_multiply_fusion
  11.1 0.0 collective-permute-done
  11.1 1.8 constant_dynamic-update-slice_fusion.1
  12.9 0.5 collective-permute-done.1
  13.4 0.5 fusion.13
  13.9 7.9 %collective-permute-start.3 = (bf16[66,1,1024]{2,1,0:T(2,128)(2,1)S(1)}, bf16[66,1,1024]{2,1,0:T(2,128)(2,1)S(1)}, u32[]{:S(2)}, u32[]{:S(2)}) collective-permute-start(bf16[66,1,1024]{2,1,0:T(2,128)(2,1)S(1)} %get-tuple-element.119), channel_id=1, source_target_pairs={{1,0},{2,1},{3,2},{4,3},{5,4},{6,5},{7,6},{8,7},{9,8},{10,9},{11,1... | collective-permute-start | bytes 405512 | tf_op jit(solution)/shard_map/ppermute | solution.py:15
  21.9 1.9 collective-permute-start.2
  23.8 0.7 fusion.18
  24.5 0.0 copy-done.4
  24.5 0.7 fusion.17
  25.3 1.8 collective-permute-done.3
  27.1 6.8 %collective-permute-done.2 = bf16[66,1,1024]{2,1,0:T(2,128)(2,1)S(1)} collective-permute-done((bf16[66,1,1024]{2,1,0:T(2,128)(2,1)S(1)}, bf16[66,1,1024]{2,1,0:T(2,128)(2,1)S(1)}, u32[]{:S(2)}, u32[]{:S(2)}) %collective-permute-start.2) | collective-permute-done | bytes 135200 | tf_op jit(solution)/shard_map/ppermute | solution.py:12
  33.8 1.7 maximum_convert_fusion
  35.5 4.3 %fusion.12 = (f32[64,16,1023]{2,1,0:T(8,128)S(1)}, f32[64,16,1023]{2,1,0:T(8,128)}) fusion(f32[66,18,1024]{2,1,0:T(8,128)S(1)} %maximum_convert_fusion), kind=kLoop, calls=%fused_computation.56 | loop fusion | bytes 16760832 | tf_op jit(solution)/shard_map/slice | solution.py:33
  39.8 6.0 %fusion.7 = bf16[64,16,1024]{2,1,0:T(8,128)(2,1)S(1)} fusion(f32[66,18,1024]{2,1,0:T(8,128)S(1)} %maximum_convert_fusion, f32[64,16,1023]{2,1,0:T(8,128)} %get-tuple-element.115, f32[64,16,1023]{2,1,0:T(8,128)S(1)} %get-tuple-element.114), kind=kLoop, calls=%fused_computation.12 | loop fusion | flops 9437184 | bytes 31449088 | tf_op jit(solution)/shard_map/convert_element_type | solution.py:102
  45.8 1.3 collective-permute-start.5
  47.1 3.7 %collective-permute-start.4 = (bf16[1,16,1024]{2,1,0:T(8,128)(2,1)S(1)}, bf16[1,16,1024]{2,1,0:T(8,128)(2,1)S(1)}, u32[]{:S(2)}, u32[]{:S(2)}) collective-permute-start(bf16[1,16,1024]{2,1,0:T(8,128)(2,1)S(1)} %get-tuple-element.120), channel_id=1, source_target_pairs={{0,32},{32,64},{64,96},{96,128},{128,160},{160,192},{192,224},{1,3... | collective-permute-start | bytes 98312 | tf_op jit(solution)/shard_map/ppermute | solution.py:12
  50.8 0.7 fusion.20
  51.6 0.0 collective-permute-done.5
  51.6 0.1 collective-permute-done.4
  51.7 0.5 pad_maximum_fusion.2
  52.2 1.9 collective-permute-start.7
  54.1 4.1 %collective-permute-start.6 = (bf16[66,1,1024]{2,1,0:T(2,128)(2,1)S(1)}, bf16[66,1,1024]{2,1,0:T(2,128)(2,1)S(1)}, u32[]{:S(2)}, u32[]{:S(2)}) collective-permute-start(bf16[66,1,1024]{2,1,0:T(2,128)(2,1)S(1)} %get-tuple-element.116), channel_id=1, source_target_pairs={{0,1},{1,2},{2,3},{3,4},{4,5},{5,6},{6,7},{7,8},{8,9},{9,10},{10,1... | collective-permute-start | bytes 405512 | tf_op jit(solution)/shard_map/ppermute | solution.py:12
  58.2 0.7 fusion.19
  77.8 0.7 fusion.16
  78.5 0.0 collective-permute-done.7
  78.5 0.0 collective-permute-done.6
  78.5 1.8 maximum_convert_fusion.1
  80.4 0.0 copy-start
  80.4 5.4 %fusion.11 = (f32[64,16,1023]{2,1,0:T(8,128)}, f32[64,16,1023]{2,1,0:T(8,128)}) fusion(f32[66,18,1024]{2,1,0:T(8,128)S(1)} %maximum_convert_fusion.1), kind=kLoop, calls=%fused_computation.55 | loop fusion | bytes 16760832 | tf_op jit(solution)/shard_map/slice | solution.py:33
  85.8 0.0 copy-done
  85.8 37.9 %fusion.10 = (f32[16,1024]{1,0:T(8,128)S(1)}, f32[64,16,1024]{2,1,0:T(8,128)S(1)}) fusion(f32[]{:T(128)} %bitcast.31, f32[]{:T(128)} %bitcast.30, f32[]{:T(128)S(6)} %sub.293, f32[]{:T(128)} %bitcast.29, f32[]{:T(128)S(6)} %sub.290, f32[]{:T(128)} %bitcast.28, f32[]{:T(128)} %bitcast.27, f32[]{:T(128)S(6)} %sub.286, f32[]{:T(128)} %bitcast.26, f32[]{:T(128)} %bitcast.25, ...), kind=kLoop, calls=%fused_computation.54 | loop fusion | flops 133152768 | bytes 8454332 | tf_op jit(solution)/shard_map/reduce_sum | solution.py:90
  123.7 0.0 copy-start.1
  123.7 2.5 fusion.21
  126.2 0.8 copy-done.1
  126.9 17.4 %all-gather = f32[128,1024]{1,0:T(8,128)S(1)} all-gather(f32[16,1024]{1,0:T(8,128)S(1)} %get-tuple-element.110), channel_id=2, replica_groups=mesh['depth'=8,'tile'=32] {'depth'}, dimensions={0}, use_global_device_ids=true | all-gather | bytes 589824 | tf_op jit(solution)/shard_map/all_gather | solution.py:22
  144.3 0.0 slice-start
  144.3 0.3 while.14
  144.6 0.0 slice-start.1
  144.6 0.0 copy-start.2
  144.7 0.0 copy-start.3
  144.7 50.6 %multiply_reduce_fusion.2 = (f32[16,1024]{1,0:T(8,128)S(1)}, f32[64,16,1024]{2,1,0:T(8,128)S(1)}) fusion(f32[64,16,1024]{2,1,0:T(8,128)} %fusion.21, f32[64,16,1024]{2,1,0:T(8,128)} %copy-done.1, f32[]{:T(128)} %bitcast.47, f32[]{:T(128)} %bitcast.46, f32[]{:T(128)} %bitcast.45, f32[]{:T(128)} %bitcast.44, f32[]{:T(128)} %bitcast.43, f32[]{:T(128)} %bitcast.42, ...), kind=kLoop, calls=%fused_computation.18 | loop fusion | flops 159367168 | bytes 42000572 | tf_op jit(solution)/shard_map/reduce_sum | solution.py:89
  195.3 0.0 slice-done
  195.3 0.0 slice-done.1
  195.3 0.0 copy-done.2
  195.3 0.0 copy-done.3
  195.3 39.8 %multiply_reduce_fusion = f32[16,1024]{1,0:T(8,128)S(1)} fusion(f32[64,16,1024]{2,1,0:T(8,128)S(1)} %copy-done.3, f32[64,16,1024]{2,1,0:T(8,128)S(1)} %copy-done.2, f32[64,16,1024]{2,1,0:T(8,128)S(1)} %get-tuple-element.109, f32[]{:T(128)} %bitcast.81, f32[]{:T(128)} %bitcast.80, f32[]{:T(128)} %bitcast.79, f32[]{:T(128)} %bitcast.78, f32[]{:T(128)} %bitcast.77, ...), kind=kLoop, calls=%fused_computation.16 | loop fusion | flops 140492800 | bytes 16842940 | tf_op jit(solution)/shard_map/reduce_sum | solution.py:89
  235.2 39.8 %multiply_reduce_fusion.1 = f32[16,1024]{1,0:T(8,128)S(1)} fusion(f32[64,16,1024]{2,1,0:T(8,128)S(1)} %copy-done.3, f32[64,16,1024]{2,1,0:T(8,128)S(1)} %copy-done.2, f32[64,16,1024]{2,1,0:T(8,128)S(1)} %get-tuple-element.109, f32[]{:T(128)} %bitcast.64, f32[]{:T(128)} %bitcast.63, f32[]{:T(128)} %bitcast.62, f32[]{:T(128)} %bitcast.61, f32[]{:T(128)} %bitcast.60, ...), kind=kLoop, calls=%fused_computation.17 | loop fusion | flops 140492800 | bytes 16842940 | tf_op jit(solution)/shard_map/reduce_sum | solution.py:89
  275.0 0.7 pad_maximum_fusion.3
  275.7 0.0 reduce-scatter.2.cloned.1.call-update
  275.7 30.0 %reduce-scatter.2.cloned.1.call-done = f32[4,16,128]{2,1,0:T(8,128)} async-done(((f32[4,16,1024]{2,1,0:T(8,128)}), f32[4,16,128]{2,1,0:T(8,128)}) %reduce-scatter.2.cloned.1.call-update) | async-done | bytes 32784 | tf_op jit(solution)/shard_map/reduce_scatter | solution.py:109
  305.7 0.7 fusion.9
  306.4 0.7 slice.514
  307.2 0.6 pad_maximum_fusion.4
  (15 shorter events, 0.1 us)
Async XLA Ops:
  6.5 18.0 %copy-start.4 = (s32[16]{0:T(128)S(1)}, s32[16]{0:T(128)}, u32[]{:S(2)}) copy-start(s32[16]{0:T(128)} %param.6) | copy-start | bytes 196
  6.5 299.2 %reduce-scatter.2.cloned.1.call-start = ((), (), s32[]{:S(2)}) async-start(), calls=%async_computation.1 | async-start | bytes 294912 | tf_op jit(solution)/shard_map/reduce_scatter | solution.py:109
  7.3 3.7 %collective-permute-start = (bf16[1,16,1024]{2,1,0:T(8,128)(2,1)S(1)}, bf16[1,16,1024]{2,1,0:T(8,128)(2,1)S(1)}, u32[]{:S(2)}, u32[]{:S(2)}) collective-permute-start(bf16[1,16,1024]{2,1,0:T(8,128)(2,1)S(1)} %get-tuple-element.123), channel_id=1, source_target_pairs={{0,32},{32,64},{64,96},{96,128},{128,160},{160,192},{192,224},{1,3... | collective-permute-start | bytes 98312 | tf_op jit(solution)/shard_map/ppermute | solution.py:12
  9.1 4.4 %collective-permute-start.1 = (bf16[1,16,1024]{2,1,0:T(8,128)(2,1)S(1)}, bf16[1,16,1024]{2,1,0:T(8,128)(2,1)S(1)}, u32[]{:S(2)}, u32[]{:S(2)}) collective-permute-start(bf16[1,16,1024]{2,1,0:T(8,128)(2,1)S(1)} %get-tuple-element.122), channel_id=1, source_target_pairs={{32,0},{64,32},{96,64},{128,96},{160,128},{192,160},{224,192},{33,... | collective-permute-start | bytes 98312 | tf_op jit(solution)/shard_map/ppermute | solution.py:15
  13.9 13.1 %collective-permute-start.3 = (bf16[66,1,1024]{2,1,0:T(2,128)(2,1)S(1)}, bf16[66,1,1024]{2,1,0:T(2,128)(2,1)S(1)}, u32[]{:S(2)}, u32[]{:S(2)}) collective-permute-start(bf16[66,1,1024]{2,1,0:T(2,128)(2,1)S(1)} %get-tuple-element.119), channel_id=1, source_target_pairs={{1,0},{2,1},{3,2},{4,3},{5,4},{6,5},{7,6},{8,7},{9,8},{10,9},{11,1... | collective-permute-start | bytes 405512 | tf_op jit(solution)/shard_map/ppermute | solution.py:15
  21.9 12.0 %collective-permute-start.2 = (bf16[66,1,1024]{2,1,0:T(2,128)(2,1)S(1)}, bf16[66,1,1024]{2,1,0:T(2,128)(2,1)S(1)}, u32[]{:S(2)}, u32[]{:S(2)}) collective-permute-start(bf16[66,1,1024]{2,1,0:T(2,128)(2,1)S(1)} %get-tuple-element.118), channel_id=1, source_target_pairs={{0,1},{1,2},{2,3},{3,4},{4,5},{5,6},{6,7},{7,8},{8,9},{9,10},{10,1... | collective-permute-start | bytes 405512 | tf_op jit(solution)/shard_map/ppermute | solution.py:12
  45.8 5.8 %collective-permute-start.5 = (bf16[1,16,1024]{2,1,0:T(8,128)(2,1)S(1)}, bf16[1,16,1024]{2,1,0:T(8,128)(2,1)S(1)}, u32[]{:S(2)}, u32[]{:S(2)}) collective-permute-start(bf16[1,16,1024]{2,1,0:T(8,128)(2,1)S(1)} %get-tuple-element.121), channel_id=1, source_target_pairs={{32,0},{64,32},{96,64},{128,96},{160,128},{192,160},{224,192},{33,... | collective-permute-start | bytes 98312 | tf_op jit(solution)/shard_map/ppermute | solution.py:15
  47.1 4.6 %collective-permute-start.4 = (bf16[1,16,1024]{2,1,0:T(8,128)(2,1)S(1)}, bf16[1,16,1024]{2,1,0:T(8,128)(2,1)S(1)}, u32[]{:S(2)}, u32[]{:S(2)}) collective-permute-start(bf16[1,16,1024]{2,1,0:T(8,128)(2,1)S(1)} %get-tuple-element.120), channel_id=1, source_target_pairs={{0,32},{32,64},{64,96},{96,128},{128,160},{160,192},{192,224},{1,3... | collective-permute-start | bytes 98312 | tf_op jit(solution)/shard_map/ppermute | solution.py:12
  52.2 26.4 %collective-permute-start.7 = (bf16[66,1,1024]{2,1,0:T(2,128)(2,1)S(1)}, bf16[66,1,1024]{2,1,0:T(2,128)(2,1)S(1)}, u32[]{:S(2)}, u32[]{:S(2)}) collective-permute-start(bf16[66,1,1024]{2,1,0:T(2,128)(2,1)S(1)} %get-tuple-element.117), channel_id=1, source_target_pairs={{1,0},{2,1},{3,2},{4,3},{5,4},{6,5},{7,6},{8,7},{9,8},{10,9},{11,1... | collective-permute-start | bytes 405512 | tf_op jit(solution)/shard_map/ppermute | solution.py:15
  54.1 24.4 %collective-permute-start.6 = (bf16[66,1,1024]{2,1,0:T(2,128)(2,1)S(1)}, bf16[66,1,1024]{2,1,0:T(2,128)(2,1)S(1)}, u32[]{:S(2)}, u32[]{:S(2)}) collective-permute-start(bf16[66,1,1024]{2,1,0:T(2,128)(2,1)S(1)} %get-tuple-element.116), channel_id=1, source_target_pairs={{0,1},{1,2},{2,3},{3,4},{4,5},{5,6},{6,7},{7,8},{8,9},{9,10},{10,1... | collective-permute-start | bytes 405512 | tf_op jit(solution)/shard_map/ppermute | solution.py:12
  80.4 5.4 %copy-start = (f32[66,18,1024]{2,1,0:T(8,128)}, f32[66,18,1024]{2,1,0:T(8,128)S(1)}, u32[]{:S(2)}) copy-start(f32[66,18,1024]{2,1,0:T(8,128)S(1)} %maximum_convert_fusion.1) | copy-start | bytes 14598148
  123.7 3.2 %copy-start.1 = (f32[64,16,1024]{2,1,0:T(8,128)}, f32[64,16,1024]{2,1,0:T(8,128)S(1)}, u32[]{:S(2)}) copy-start(f32[64,16,1024]{2,1,0:T(8,128)S(1)} %get-tuple-element.111) | copy-start | bytes 12582916
  144.3 51.0 %slice-start = ((s8[6488064]{0:T(1024)(128)(4,1)}), s8[2293760]{0:T(1024)(128)(4,1)S(1)}, s32[]{:S(2)}) async-start(s8[6488064]{0:T(1024)(128)(4,1)} %bitcast.90), calls=%async_computation.2 | async-start | bytes 4587520
  144.6 50.7 %slice-start.1 = ((s8[6488064]{0:T(1024)(128)(4,1)}), s8[4194304]{0:T(1024)(128)(4,1)S(1)}, s32[]{:S(2)}) async-start(s8[6488064]{0:T(1024)(128)(4,1)} %bitcast.90), calls=%async_computation.3 | async-start | bytes 8388608
  144.6 50.7 %copy-start.2 = (f32[64,16,1024]{2,1,0:T(8,128)S(1)}, f32[64,16,1024]{2,1,0:T(8,128)}, u32[]{:S(2)}) copy-start(f32[64,16,1024]{2,1,0:T(8,128)} %copy-done.1) | copy-start | bytes 12582916
  144.7 50.7 %copy-start.3 = (f32[64,16,1024]{2,1,0:T(8,128)S(1)}, f32[64,16,1024]{2,1,0:T(8,128)}, u32[]{:S(2)}) copy-start(f32[64,16,1024]{2,1,0:T(8,128)} %fusion.21) | copy-start | bytes 12582916
Sparse Core Ops, SparseCore 0:
  275.9 29.8 reduce-scatter.1
where the time goes:
time: 317 us; the launch traced here: 315 us
  other arithmetic  183 us (58%)
  waiting for transfers between devices  39.2 us (12%)
  between operations  32.6 us (10%)
  starting transfers between devices  23.9 us (8%)
  local copies, waits for them, and re-layouts  17.9 us (6%)
  blocking collectives  17.4 us (5%)
    reduce_sum x3, other arithmetic, composite(): jnp.sum(weight * colors[c], axis=0)  130 us
    reduce_sum x1, other arithmetic, composite(): return (brick_color, jnp.sum(extinction, axis=0))  37.9 us
    reduce_scatter x1, waiting for transfers between devices, body(): lax.psum_scatter(weighted, 'depth', scatter_dimension=2, tiled=True)  30 us
    all_gather x1, blocking collectives, carried_in(): pieces = lax.all_gather(value, axis)  17.4 us
    ppermute x4, starting transfers between devices, padded(): lax.ppermute(lax.slice_in_dim(block, 0, width, axis=dim), axis, backward)  12.4 us
    ppermute x4, starting transfers between devices, padded(): lax.ppermute(lax.slice_in_dim(block, block.shape[dim] - width, None, axis...  11.5 us
    slice x2, local copies, waits for them, and re-layouts, next_along(): return jnp.pad(center[:, :, 1:], ((0, 0), (0, 0), (0, 1)))  9.69 us
    ppermute x4, waiting for transfers between devices, padded(): lax.ppermute(lax.slice_in_dim(block, block.shape[dim] - width, None, axis...  6.9 us
  transfers between devices with their start and end apart: 9, of which 5 were waited for; matrix products, arithmetic and copies ran while one was open for 2% of the time, Pallas kernels for 0%

commit v1 on v0

v1 whole, which is shorter than its diff:
```python
import jax
import jax.numpy as jnp
from jax import lax
from jax.experimental import pallas as pl
from jax.experimental.pallas import tpu as pltpu
from jax.sharding import PartitionSpec as P


def padded(block, sides, width):
    for axis, dim in sides:
        count = lax.axis_size(axis)
        forward = [(i, i + 1) for i in range(count - 1)]
        backward = [(target, source) for source, target in forward]
        low = lax.ppermute(
            lax.slice_in_dim(block, block.shape[dim] - width, None, axis=dim), axis, forward
        )
        high = lax.ppermute(lax.slice_in_dim(block, 0, width, axis=dim), axis, backward)
        block = jnp.concatenate([low, block, high], axis=dim)
    return block


def next_along(center):
    return jnp.pad(center[:, :, 1:], ((0, 0), (0, 0), (0, 1)))


def prior_along(center):
    return jnp.pad(center[:, :, :-1], ((0, 0), (0, 0), (1, 0)))


def smooth_block(extended):
    field = extended.astype(jnp.float32)
    center = field[1:-1, 1:-1]
    neighbours = field[2:, 1:-1] + field[:-2, 1:-1] + field[1:-1, 2:] + field[1:-1, :-2]
    neighbours = neighbours + next_along(center) + prior_along(center)
    return 0.4 * center + 0.1 * neighbours


def shade_lookup(smooth_ext, knot_pos):
    field = smooth_ext.astype(jnp.float32)
    center = field[1:-1, 1:-1]
    slope_z = 0.5 * (field[2:, 1:-1] - field[:-2, 1:-1])
    slope_x = 0.5 * (field[1:-1, 2:] - field[1:-1, :-2])
    slope_y = 0.5 * (next_along(center) - prior_along(center))
    facing = jnp.abs(0.6 * slope_z + 0.8 * slope_x)
    shading = 0.3 + 0.7 * facing / jnp.sqrt(
        slope_z * slope_z + slope_x * slope_x + slope_y * slope_y + 0.1
    )
    knot_float = knot_pos.astype(jnp.float32)
    lookup = jnp.clip(127.5 + 70.0 * center, knot_float[0], knot_float[-1])
    return shading, lookup


def ramp_table(knot_pos, knot_color, sigma_scale):
    knot_float = knot_pos.astype(jnp.float32)
    palette = knot_color.astype(jnp.float32) / 255.0
    palette = palette.at[3].multiply(sigma_scale)
    gaps = knot_float[1:] - knot_float[:-1]
    slopes = (palette[:, 1:] - palette[:, :-1]) / gaps[None]
    count = knot_pos.shape[0] - 1
    table = jnp.zeros((8, 128), jnp.float32)
    table = table.at[0, :count].set(knot_float[:-1])
    table = table.at[1, :count].set(gaps)
    table = table.at[2:6, :count].set(slopes)
    table = table.at[6, :4].set(palette[:, 0])
    return table


def composite_kernel(table, lookup_ref, shade_ref, color_ref, depth_ref, *, segments, rows):
    depth_len = lookup_ref.shape[0]
    width = lookup_ref.shape[2]
    knots = [table[0, k] for k in range(segments)]
    gaps = [table[1, k] for k in range(segments)]
    slopes = [[table[2 + c, k] for k in range(segments)] for c in range(4)]
    base = [table[6, c] for c in range(4)]
    for half in range(lookup_ref.shape[1] // rows):
        sl = pl.ds(half * rows, rows)

        def step(z, carry):
            trans, acc0, acc1, acc2, total = carry
            lookup = lookup_ref[z, sl, :]
            shade = shade_ref[z, sl, :]
            chan = [jnp.full_like(lookup, base[c]) for c in range(4)]
            for k in range(segments):
                t = jnp.minimum(jnp.maximum(lookup - knots[k], 0.0), gaps[k])
                chan = [chan[c] + t * slopes[c][k] for c in range(4)]
            ext = chan[3]
            fade = jnp.exp(-ext)
            weight = shade * (1.0 - fade) * trans
            acc0 = acc0 + weight * chan[0]
            acc1 = acc1 + weight * chan[1]
            acc2 = acc2 + weight * chan[2]
            return (trans * fade, acc0, acc1, acc2, total + ext)

        zeros = jnp.zeros((rows, width), jnp.float32)
        init = (jnp.ones((rows, width), jnp.float32), zeros, zeros, zeros, zeros)
        _, acc0, acc1, acc2, total = lax.fori_loop(0, depth_len, step, init, unroll=2)
        color_ref[0, sl, :] = acc0
        color_ref[1, sl, :] = acc1
        color_ref[2, sl, :] = acc2
        depth_ref[sl, :] = total


def composite_block(table, lookup, shading, segments):
    depth_len, rows_all, width_all = lookup.shape
    width = 256
    rows = 8
    kernel = lambda *refs: composite_kernel(*refs, segments=segments, rows=rows)
    grid_spec = pltpu.PrefetchScalarGridSpec(
        num_scalar_prefetch=1,
        grid=(width_all // width,),
        in_specs=[
            pl.BlockSpec((depth_len, rows_all, width), lambda j, t: (0, 0, j)),
            pl.BlockSpec((depth_len, rows_all, width), lambda j, t: (0, 0, j)),
        ],
        out_specs=[
            pl.BlockSpec((3, rows_all, width), lambda j, t: (0, 0, j)),
            pl.BlockSpec((rows_all, width), lambda j, t: (0, j)),
        ],
    )
    return pl.pallas_call(
        kernel,
        grid_spec=grid_spec,
        out_shape=[
            jax.ShapeDtypeStruct((3, rows_all, width_all), jnp.float32),
            jax.ShapeDtypeStruct((rows_all, width_all), jnp.float32),
        ],
    )(table, lookup, shading)


def body(volume, knot_pos, knot_color):
    depth_count = lax.axis_size("depth")
    brick_depth, brick_rows, row_width = volume.shape
    sigma_scale = 4.0 / (brick_depth * depth_count)
    extended = padded(volume, (("depth", 0), ("tile", 1)), 1)
    smoothed = smooth_block(extended).astype(jnp.bfloat16)
    smooth_ext = padded(smoothed, (("depth", 0), ("tile", 1)), 1)
    shading, lookup = shade_lookup(smooth_ext, knot_pos)
    table = ramp_table(knot_pos, knot_color, sigma_scale)
    brick_color, optical_depth = composite_block(table, lookup, shading, knot_pos.shape[0] - 1)
    piece = row_width // depth_count
    weighted = jnp.concatenate([brick_color, optical_depth[None]], axis=0)
    weighted = weighted.reshape(4, brick_rows, depth_count, piece).transpose(2, 0, 1, 3)
    blocks = lax.all_to_all(weighted, "depth", 0, 0, tiled=True)
    ahead = jnp.zeros((brick_rows, piece), jnp.float32)
    image = jnp.zeros((3, brick_rows, piece), jnp.float32)
    for b in range(depth_count):
        image = image + blocks[b, :3] * jnp.exp(-ahead)[None]
        ahead = ahead + blocks[b, 3]
    return jnp.concatenate([image, (1.0 - jnp.exp(-ahead))[None]], axis=0)


def solution(mesh):
    in_specs = (P("depth", "tile", None), P(), P())
    out_specs = P(None, "tile", "depth")
    return jax.shard_map(body, mesh=mesh, in_specs=in_specs, out_specs=out_specs, check_vma=False)
```

time: 317 us -> 123 us (0.39)
  other arithmetic: 183 us -> 22.2 us
  between operations: 32.6 us -> 0.23 us
  Pallas kernels: 0 us -> 30.8 us
  waiting for transfers between devices: 39.2 us -> 13.1 us
  blocking collectives: 17.4 us -> 13.5 us
    reduce_sum x4 -> x0, other arithmetic: 168 us -> none  [the longest x3 130 us: composite(): jnp.sum(weight * colors[c], axis=0)]
    pallas_call x0 -> x1, Pallas kernels: none -> 30.8 us  [composite_block(): pl.pallas_call(kernel, grid_spec=grid_spec, out_shape=[jax.ShapeDtypeStru...]
    reduce_scatter x1 -> x0, waiting for transfers between devices: 30 us -> none  [body(): lax.psum_scatter(weighted, 'depth', scatter_dimension=2, tiled=True)]
    all_gather x1 -> x0, blocking collectives: 17.4 us -> none  [carried_in(): pieces = lax.all_gather(value, axis)]
    all_to_all x0 -> x1, blocking collectives: none -> 13.5 us  [body(): blocks = lax.all_to_all(weighted, 'depth', 0, 0, tiled=True)]
    add x0 -> x2, other arithmetic: none -> 10.1 us  [the longest x1 10.1 us: shade_lookup(): 0.3 + 0.7 * facing / jnp.sqrt(slope_z * slope_z + slope_x * slope_x + slo...]
    ppermute x4, waiting for transfers between devices: 2.31 us -> 7.67 us  [padded(): lax.ppermute(lax.slice_in_dim(block, 0, width, axis=dim), axis, backward)]
    slice x6 -> x2, local copies, waits for them, and re-layouts: 4.34 us -> 0.7 us  [the longest x1 0.59 us: shade_lookup(): lookup = jnp.clip(127.5 + 70.0 * center, knot_float[0], knot_float[-1])]
  transfers between devices with their start and end apart: 9 -> 8, of which waited for: 5 -> 5; matrix products, arithmetic and copies ran while one was open for 2% -> 4% of each run, Pallas kernels for 0% -> 0%
where the time goes in v1:
time: 123 us; the launch traced here: 122 us
  Pallas kernels  30.8 us (25%)
  starting transfers between devices  26.3 us (21%)
  other arithmetic  22.2 us (18%)
  local copies, waits for them, and re-layouts  16 us (13%)
  blocking collectives  13.5 us (11%)
  waiting for transfers between devices  13.1 us (11%)
    pallas_call x1, Pallas kernels, composite_block(): pl.pallas_call(kernel, grid_spec=grid_spec, out_shape=[jax.ShapeDtypeStru...  30.8 us
    ppermute x4, starting transfers between devices, padded(): lax.ppermute(lax.slice_in_dim(block, 0, width, axis=dim), axis, backward)  15.1 us
    all_to_all x1, blocking collectives, body(): blocks = lax.all_to_all(weighted, 'depth', 0, 0, tiled=True)  13.5 us
    ppermute x4, starting transfers between devices, padded(): lax.ppermute(lax.slice_in_dim(block, block.shape[dim] - width, None, axis...  11.1 us
    add x1, other arithmetic, shade_lookup(): 0.3 + 0.7 * facing / jnp.sqrt(slope_z * slope_z + slope_x * slope_x + slo...  10.1 us
    slice x2, local copies, waits for them, and re-layouts, next_along(): return jnp.pad(center[:, :, 1:], ((0, 0), (0, 0), (0, 1)))  9.69 us
    ppermute x4, waiting for transfers between devices, padded(): lax.ppermute(lax.slice_in_dim(block, 0, width, axis=dim), axis, backward)  7.67 us
    convert_element_type x1, other arithmetic, body(): smoothed = smooth_block(extended).astype(jnp.bfloat16)  5.95 us
  transfers between devices with their start and end apart: 8, of which 5 were waited for; matrix products, arithmetic and copies ran while one was open for 4% of the time, Pallas kernels for 0%

profile of v1, /device:TPU:24, one launch (start us, length us, event | category | flops | bytes accessed | tf_op | source)
XLA Modules:
  0.0 122.0 jit_solution(3484192721661304126)
XLA Ops:
  0.0 0.8 fusion.30
  0.8 1.7 %collective-permute-start = (bf16[1,16,1024]{2,1,0:T(8,128)(2,1)S(1)}, bf16[1,16,1024]{2,1,0:T(8,128)(2,1)S(1)}, u32[]{:S(2)}, u32[]{:S(2)}) collective-permute-start(bf16[1,16,1024]{2,1,0:T(8,128)(2,1)S(1)} %get-tuple-element.86), channel_id=1, source_target_pairs={{0,32},{32,64},{64,96},{96,128},{128,160},{160,192},{192,224},{1,3... | collective-permute-start | bytes 98312 | tf_op jit(solution)/shard_map/ppermute | solution.py:14
  2.5 1.3 %collective-permute-start.1 = (bf16[1,16,1024]{2,1,0:T(8,128)(2,1)S(1)}, bf16[1,16,1024]{2,1,0:T(8,128)(2,1)S(1)}, u32[]{:S(2)}, u32[]{:S(2)}) collective-permute-start(bf16[1,16,1024]{2,1,0:T(8,128)(2,1)S(1)} %get-tuple-element.85), channel_id=1, source_target_pairs={{32,0},{64,32},{96,64},{128,96},{160,128},{192,160},{224,192},{33,... | collective-permute-start | bytes 98312 | tf_op jit(solution)/shard_map/ppermute | solution.py:17
  3.8 0.7 convert_multiply_fusion
  4.5 0.7 convert_element_type.22
  5.2 0.0 collective-permute-done
  5.2 1.8 %constant_dynamic-update-slice_fusion.1 = bf16[66,16,1024]{2,1,0:T(8,128)(2,1)S(1)} fusion(bf16[66,16,1024]{2,1,0:T(8,128)(2,1)S(1)} %constant_dynamic-update-slice_fusion.2, bf16[64,16,1024]{2,1,0:T(8,128)(2,1)} %param.13), kind=kLoop, calls=%fused_computation.58 | loop fusion | bytes 4194304
  7.1 0.0 collective-permute-done.1
  7.1 0.5 fusion.28
  7.6 3.8 %collective-permute-start.2 = (bf16[66,1,1024]{2,1,0:T(2,128)(2,1)S(1)}, bf16[66,1,1024]{2,1,0:T(2,128)(2,1)S(1)}, u32[]{:S(2)}, u32[]{:S(2)}) collective-permute-start(bf16[66,1,1024]{2,1,0:T(2,128)(2,1)S(1)} %get-tuple-element.81), channel_id=1, source_target_pairs={{0,1},{1,2},{2,3},{3,4},{4,5},{5,6},{6,7},{7,8},{8,9},{9,10},{10,1... | collective-permute-start | bytes 405512 | tf_op jit(solution)/shard_map/ppermute | solution.py:14
  11.4 6.0 %collective-permute-start.3 = (bf16[66,1,1024]{2,1,0:T(2,128)(2,1)S(1)}, bf16[66,1,1024]{2,1,0:T(2,128)(2,1)S(1)}, u32[]{:S(2)}, u32[]{:S(2)}) collective-permute-start(bf16[66,1,1024]{2,1,0:T(2,128)(2,1)S(1)} %get-tuple-element.82), channel_id=1, source_target_pairs={{1,0},{2,1},{3,2},{4,3},{5,4},{6,5},{7,6},{8,7},{9,8},{10,9},{11,1... | collective-permute-start | bytes 405512 | tf_op jit(solution)/shard_map/ppermute | solution.py:17
  17.4 0.1 slice_subtract_fusion.2
  17.5 3.6 %collective-permute-done.2 = bf16[66,1,1024]{2,1,0:T(2,128)(2,1)S(1)} collective-permute-done((bf16[66,1,1024]{2,1,0:T(2,128)(2,1)S(1)}, bf16[66,1,1024]{2,1,0:T(2,128)(2,1)S(1)}, u32[]{:S(2)}, u32[]{:S(2)}) %collective-permute-start.2) | collective-permute-done | bytes 135200 | tf_op jit(solution)/shard_map/ppermute | solution.py:14
  21.1 1.7 %collective-permute-done.3 = bf16[66,1,1024]{2,1,0:T(2,128)(2,1)S(1)} collective-permute-done((bf16[66,1,1024]{2,1,0:T(2,128)(2,1)S(1)}, bf16[66,1,1024]{2,1,0:T(2,128)(2,1)S(1)}, u32[]{:S(2)}, u32[]{:S(2)}) %collective-permute-start.3) | collective-permute-done | bytes 135200 | tf_op jit(solution)/shard_map/ppermute | solution.py:17
  22.8 1.7 %maximum_convert_fusion = f32[66,18,1024]{2,1,0:T(8,128)S(1)} fusion(bf16[66,1,1024]{2,1,0:T(2,128)(2,1)S(1)} %collective-permute-done.3, bf16[66,16,1024]{2,1,0:T(8,128)(2,1)S(1)} %constant_dynamic-update-slice_fusion, bf16[66,1,1024]{2,1,0:T(2,128)(2,1)S(1)} %collective-permute-done.2), kind=kLoop, calls=%fused_computation.16 | loop fusion | flops 7299072 | bytes 7299072 | tf_op jit(solution)/shard_map/convert_element_type | solution.py:31
  24.5 4.3 %fusion.27 = (f32[64,16,1023]{2,1,0:T(8,128)S(1)}, f32[64,16,1023]{2,1,0:T(8,128)}) fusion(f32[66,18,1024]{2,1,0:T(8,128)S(1)} %maximum_convert_fusion), kind=kLoop, calls=%fused_computation.74 | loop fusion | bytes 16760832 | tf_op jit(solution)/shard_map/slice | solution.py:23
  28.8 6.0 %fusion.7 = bf16[64,16,1024]{2,1,0:T(8,128)(2,1)S(1)} fusion(f32[66,18,1024]{2,1,0:T(8,128)S(1)} %maximum_convert_fusion, f32[64,16,1023]{2,1,0:T(8,128)} %get-tuple-element.78, f32[64,16,1023]{2,1,0:T(8,128)S(1)} %get-tuple-element.77), kind=kLoop, calls=%fused_computation.11 | loop fusion | flops 9437184 | bytes 31449088 | tf_op jit(solution)/shard_map/convert_element_type | solution.py:135
  34.8 3.5 %collective-permute-start.4 = (bf16[1,16,1024]{2,1,0:T(8,128)(2,1)S(1)}, bf16[1,16,1024]{2,1,0:T(8,128)(2,1)S(1)}, u32[]{:S(2)}, u32[]{:S(2)}) collective-permute-start(bf16[1,16,1024]{2,1,0:T(8,128)(2,1)S(1)} %get-tuple-element.83), channel_id=1, source_target_pairs={{0,32},{32,64},{64,96},{96,128},{128,160},{160,192},{192,224},{1,3... | collective-permute-start | bytes 98312 | tf_op jit(solution)/shard_map/ppermute | solution.py:14
  38.3 1.3 %collective-permute-start.5 = (bf16[1,16,1024]{2,1,0:T(8,128)(2,1)S(1)}, bf16[1,16,1024]{2,1,0:T(8,128)(2,1)S(1)}, u32[]{:S(2)}, u32[]{:S(2)}) collective-permute-start(bf16[1,16,1024]{2,1,0:T(8,128)(2,1)S(1)} %get-tuple-element.84), channel_id=1, source_target_pairs={{32,0},{64,32},{96,64},{128,96},{160,128},{192,160},{224,192},{33,... | collective-permute-start | bytes 98312 | tf_op jit(solution)/shard_map/ppermute | solution.py:17
  39.6 0.1 subtract_divide_fusion
  39.6 0.0 collective-permute-done.4
  39.6 4.2 %collective-permute-done.5 = bf16[1,16,1024]{2,1,0:T(8,128)(2,1)S(1)} collective-permute-done((bf16[1,16,1024]{2,1,0:T(8,128)(2,1)S(1)}, bf16[1,16,1024]{2,1,0:T(8,128)(2,1)S(1)}, u32[]{:S(2)}, u32[]{:S(2)}) %collective-permute-start.5) | collective-permute-done | bytes 32800 | tf_op jit(solution)/shard_map/ppermute | solution.py:17
  43.8 0.5 pad_maximum_fusion.2
  44.3 2.1 %collective-permute-start.6 = (bf16[66,1,1024]{2,1,0:T(2,128)(2,1)S(1)}, bf16[66,1,1024]{2,1,0:T(2,128)(2,1)S(1)}, u32[]{:S(2)}, u32[]{:S(2)}) collective-permute-start(bf16[66,1,1024]{2,1,0:T(2,128)(2,1)S(1)} %get-tuple-element.79), channel_id=1, source_target_pairs={{0,1},{1,2},{2,3},{3,4},{4,5},{5,6},{6,7},{7,8},{8,9},{9,10},{10,1... | collective-permute-start | bytes 405512 | tf_op jit(solution)/shard_map/ppermute | solution.py:14
  46.4 6.5 %collective-permute-start.7 = (bf16[66,1,1024]{2,1,0:T(2,128)(2,1)S(1)}, bf16[66,1,1024]{2,1,0:T(2,128)(2,1)S(1)}, u32[]{:S(2)}, u32[]{:S(2)}) collective-permute-start(bf16[66,1,1024]{2,1,0:T(2,128)(2,1)S(1)} %get-tuple-element.80), channel_id=1, source_target_pairs={{1,0},{2,1},{3,2},{4,3},{5,4},{6,5},{7,6},{8,7},{9,8},{10,9},{11,1... | collective-permute-start | bytes 405512 | tf_op jit(solution)/shard_map/ppermute | solution.py:17
  52.9 0.1 slice_reduce_fusion
  53.0 0.2 scatter.15
  53.2 0.3 scatter.16
  53.5 0.2 scatter.19.refs_0_
  53.7 0.0 copy-start
  53.8 0.6 fusion.31
  54.3 1.8 %collective-permute-done.6 = bf16[66,1,1024]{2,1,0:T(2,128)(2,1)S(1)} collective-permute-done((bf16[66,1,1024]{2,1,0:T(2,128)(2,1)S(1)}, bf16[66,1,1024]{2,1,0:T(2,128)(2,1)S(1)}, u32[]{:S(2)}, u32[]{:S(2)}) %collective-permute-start.6) | collective-permute-done | bytes 135200 | tf_op jit(solution)/shard_map/ppermute | solution.py:14
  56.2 1.7 %collective-permute-done.7 = bf16[66,1,1024]{2,1,0:T(2,128)(2,1)S(1)} collective-permute-done((bf16[66,1,1024]{2,1,0:T(2,128)(2,1)S(1)}, bf16[66,1,1024]{2,1,0:T(2,128)(2,1)S(1)}, u32[]{:S(2)}, u32[]{:S(2)}) %collective-permute-start.7) | collective-permute-done | bytes 135200 | tf_op jit(solution)/shard_map/ppermute | solution.py:17
  57.9 1.8 %maximum_convert_fusion.1 = f32[66,18,1024]{2,1,0:T(8,128)S(1)} fusion(bf16[66,1,1024]{2,1,0:T(2,128)(2,1)S(1)} %collective-permute-done.7, bf16[1,16,1024]{2,1,0:T(8,128)(2,1)S(1)} %collective-permute-done.5, bf16[64,16,1024]{2,1,0:T(8,128)(2,1)S(1)} %fusion.7, bf16[1,16,1024]{2,1,0:T(8,128)(2,1)S(1)} %collective-permute-done.4, ...), kind=kLoop, calls=%fused_computation.17 | loop fusion | flops 12165120 | bytes 7299072 | tf_op jit(solution)/shard_map/convert_element_type | solution.py:39
  59.8 0.0 copy-done
  59.8 5.4 %fusion.26 = (f32[64,16,1023]{2,1,0:T(8,128)}, f32[64,16,1023]{2,1,0:T(8,128)}) fusion(f32[66,18,1024]{2,1,0:T(8,128)S(1)} %maximum_convert_fusion.1), kind=kLoop, calls=%fused_computation.73 | loop fusion | bytes 16760832 | tf_op jit(solution)/shard_map/slice | solution.py:23
  65.2 10.1 %multiply_add_fusion = (f32[64,16,1024]{2,1,0:T(8,128)}, f32[64,16,1024]{2,1,0:T(8,128)}) fusion(f32[64,16,1023]{2,1,0:T(8,128)} %get-tuple-element.76, f32[64,16,1023]{2,1,0:T(8,128)} %get-tuple-element.75, f32[66,18,1024]{2,1,0:T(8,128)S(1)} %maximum_convert_fusion.1, f32[]{:T(128)} %bitcast.3, f32[]{:T(128)} %bitcast.2), kind=kLoop, calls=%fused_computation.15 | loop fusion | flops 24117248 | bytes 37740552 | tf_op jit(solution)/shard_map/add | solution.py:45
  75.2 30.8 %shard_map.37 = (f32[3,16,1024]{2,1,0:T(8,128)}, f32[16,1024]{1,0:T(8,128)}) custom-call(f32[8,128]{1,0:T(8,128)} %copy-done, f32[64,16,1024]{2,1,0:T(8,128)} %get-tuple-element.74.refs_1_, f32[64,16,1024]{2,1,0:T(8,128)} %get-tuple-element.73.refs_2_), custom_call_target="tpu_custom_call" | custom-call | tf_op jit(solution)/shard_map/pallas_call | solution.py:120
  106.0 0.9 copy_bitcast_fusion
  106.9 0.9 copy.9
  107.8 13.5 %all_to_all.5 = f32[8,4,16,128]{3,2,1,0:T(8,128)S(1)} all-to-all(f32[8,4,16,128]{3,2,1,0:T(8,128)S(1)} %maximum_bitcast_fusion), channel_id=1, replica_groups=mesh['depth'=8,'tile'=32] {'depth'}, dimensions={0} | all-to-all | bytes 524288 | tf_op jit(solution)/shard_map/all_to_all | solution.py:143
  121.4 0.6 pad_maximum_fusion.3
  (12 shorter events, 0.2 us)
Async XLA Ops:
  0.8 4.4 %collective-permute-start = (bf16[1,16,1024]{2,1,0:T(8,128)(2,1)S(1)}, bf16[1,16,1024]{2,1,0:T(8,128)(2,1)S(1)}, u32[]{:S(2)}, u32[]{:S(2)}) collective-permute-start(bf16[1,16,1024]{2,1,0:T(8,128)(2,1)S(1)} %get-tuple-element.86), channel_id=1, source_target_pairs={{0,32},{32,64},{64,96},{96,128},{128,160},{160,192},{192,224},{1,3... | collective-permute-start | bytes 98312 | tf_op jit(solution)/shard_map/ppermute | solution.py:14
  2.5 4.5 %collective-permute-start.1 = (bf16[1,16,1024]{2,1,0:T(8,128)(2,1)S(1)}, bf16[1,16,1024]{2,1,0:T(8,128)(2,1)S(1)}, u32[]{:S(2)}, u32[]{:S(2)}) collective-permute-start(bf16[1,16,1024]{2,1,0:T(8,128)(2,1)S(1)} %get-tuple-element.85), channel_id=1, source_target_pairs={{32,0},{64,32},{96,64},{128,96},{160,128},{192,160},{224,192},{33,... | collective-permute-start | bytes 98312 | tf_op jit(solution)/shard_map/ppermute | solution.py:17
  7.6 13.5 %collective-permute-start.2 = (bf16[66,1,1024]{2,1,0:T(2,128)(2,1)S(1)}, bf16[66,1,1024]{2,1,0:T(2,128)(2,1)S(1)}, u32[]{:S(2)}, u32[]{:S(2)}) collective-permute-start(bf16[66,1,1024]{2,1,0:T(2,128)(2,1)S(1)} %get-tuple-element.81), channel_id=1, source_target_pairs={{0,1},{1,2},{2,3},{3,4},{4,5},{5,6},{6,7},{7,8},{8,9},{9,10},{10,1... | collective-permute-start | bytes 405512 | tf_op jit(solution)/shard_map/ppermute | solution.py:14
  11.4 11.4 %collective-permute-start.3 = (bf16[66,1,1024]{2,1,0:T(2,128)(2,1)S(1)}, bf16[66,1,1024]{2,1,0:T(2,128)(2,1)S(1)}, u32[]{:S(2)}, u32[]{:S(2)}) collective-permute-start(bf16[66,1,1024]{2,1,0:T(2,128)(2,1)S(1)} %get-tuple-element.82), channel_id=1, source_target_pairs={{1,0},{2,1},{3,2},{4,3},{5,4},{6,5},{7,6},{8,7},{9,8},{10,9},{11,1... | collective-permute-start | bytes 405512 | tf_op jit(solution)/shard_map/ppermute | solution.py:17
  34.8 4.9 %collective-permute-start.4 = (bf16[1,16,1024]{2,1,0:T(8,128)(2,1)S(1)}, bf16[1,16,1024]{2,1,0:T(8,128)(2,1)S(1)}, u32[]{:S(2)}, u32[]{:S(2)}) collective-permute-start(bf16[1,16,1024]{2,1,0:T(8,128)(2,1)S(1)} %get-tuple-element.83), channel_id=1, source_target_pairs={{0,32},{32,64},{64,96},{96,128},{128,160},{160,192},{192,224},{1,3... | collective-permute-start | bytes 98312 | tf_op jit(solution)/shard_map/ppermute | solution.py:14
  38.3 5.6 %collective-permute-start.5 = (bf16[1,16,1024]{2,1,0:T(8,128)(2,1)S(1)}, bf16[1,16,1024]{2,1,0:T(8,128)(2,1)S(1)}, u32[]{:S(2)}, u32[]{:S(2)}) collective-permute-start(bf16[1,16,1024]{2,1,0:T(8,128)(2,1)S(1)} %get-tuple-element.84), channel_id=1, source_target_pairs={{32,0},{64,32},{96,64},{128,96},{160,128},{192,160},{224,192},{33,... | collective-permute-start | bytes 98312 | tf_op jit(solution)/shard_map/ppermute | solution.py:17
  44.3 11.9 %collective-permute-start.6 = (bf16[66,1,1024]{2,1,0:T(2,128)(2,1)S(1)}, bf16[66,1,1024]{2,1,0:T(2,128)(2,1)S(1)}, u32[]{:S(2)}, u32[]{:S(2)}) collective-permute-start(bf16[66,1,1024]{2,1,0:T(2,128)(2,1)S(1)} %get-tuple-element.79), channel_id=1, source_target_pairs={{0,1},{1,2},{2,3},{3,4},{4,5},{5,6},{6,7},{7,8},{8,9},{9,10},{10,1... | collective-permute-start | bytes 405512 | tf_op jit(solution)/shard_map/ppermute | solution.py:14
  46.4 11.5 %collective-permute-start.7 = (bf16[66,1,1024]{2,1,0:T(2,128)(2,1)S(1)}, bf16[66,1,1024]{2,1,0:T(2,128)(2,1)S(1)}, u32[]{:S(2)}, u32[]{:S(2)}) collective-permute-start(bf16[66,1,1024]{2,1,0:T(2,128)(2,1)S(1)} %get-tuple-element.80), channel_id=1, source_target_pairs={{1,0},{2,1},{3,2},{4,3},{5,4},{6,5},{7,6},{8,7},{9,8},{10,9},{11,1... | collective-permute-start | bytes 405512 | tf_op jit(solution)/shard_map/ppermute | solution.py:17
  53.7 6.0 %copy-start = (f32[8,128]{1,0:T(8,128)}, f32[8,128]{1,0:T(8,128)S(1)}, u32[]{:S(2)}) copy-start(f32[8,128]{1,0:T(8,128)S(1)} %scatter.19.refs_0_) | copy-start | bytes 12292

commit v2 on v1

--- a/solution.py
+++ b/solution.py
@@ -17,6 +17,56 @@
         high = lax.ppermute(lax.slice_in_dim(block, 0, width, axis=dim), axis, backward)
         block = jnp.concatenate([low, block, high], axis=dim)
     return block
+
+
+def shifted(block, axes, moves):
+    sizes = [lax.axis_size(a) for a in axes]
+    pairs = []
+    for index in range(sizes[0] * (sizes[1] if len(sizes) > 1 else 1)):
+        coords = [index] if len(sizes) == 1 else [index // sizes[1], index % sizes[1]]
+        target = [c + m for c, m in zip(coords, moves)]
+        if all(0 <= c < s for c, s in zip(target, sizes)):
+            flat = target[0] if len(sizes) == 1 else target[0] * sizes[1] + target[1]
+            pairs.append((index, flat))
+    return lax.ppermute(block, axes if len(axes) > 1 else axes[0], pairs)
+
+
+def extended_volume(volume):
+    depth, rows, width = volume.shape
+    dz = ("depth",)
+    tx = ("tile",)
+    both = ("depth", "tile")
+    z_low = shifted(volume[depth - 2:], dz, (1,))
+    z_high = shifted(volume[:2], dz, (-1,))
+    x_low = shifted(volume[:, rows - 2:], tx, (1,))
+    x_high = shifted(volume[:, :2], tx, (-1,))
+    c_ll = shifted(volume[depth - 1:, rows - 1:], both, (1, 1))
+    c_lh = shifted(volume[depth - 1:, :1], both, (1, -1))
+    c_hl = shifted(volume[:1, rows - 1:], both, (-1, 1))
+    c_hh = shifted(volume[:1, :1], both, (-1, -1))
+    zero1 = jnp.zeros((1, 1, width), volume.dtype)
+    zero2 = jnp.zeros((2, 2, width), volume.dtype)
+    left = jnp.concatenate(
+        [zero2[:1], jnp.concatenate([zero1, c_ll], 1), x_low,
+         jnp.concatenate([zero1, c_hl], 1), zero2[:1]], axis=0)
+    right = jnp.concatenate(
+        [zero2[:1], jnp.concatenate([c_lh, zero1], 1), x_high,
+         jnp.concatenate([c_hh, zero1], 1), zero2[:1]], axis=0)
+    middle = jnp.concatenate([z_low, volume, z_high], axis=0)
+    return jnp.concatenate([left, middle, right], axis=1)
+
+
+def inside_mask(depth_len, rows):
+    d = lax.axis_index("depth")
+    t = lax.axis_index("tile")
+    z = lax.broadcasted_iota(jnp.int32, (depth_len, rows, 1), 0)
+    x = lax.broadcasted_iota(jnp.int32, (depth_len, rows, 1), 1)
+    keep = jnp.ones((depth_len, rows, 1), jnp.bool_)
+    keep = keep & ~((z == 0) & (d == 0))
+    keep = keep & ~((z == depth_len - 1) & (d == lax.axis_size("depth") - 1))
+    keep = keep & ~((x == 0) & (t == 0))
+    keep = keep & ~((x == rows - 1) & (t == lax.axis_size("tile") - 1))
+    return keep
 
 
 def next_along(center):
@@ -131,9 +181,10 @@
     depth_count = lax.axis_size("depth")
     brick_depth, brick_rows, row_width = volume.shape
     sigma_scale = 4.0 / (brick_depth * depth_count)
-    extended = padded(volume, (("depth", 0), ("tile", 1)), 1)
-    smoothed = smooth_block(extended).astype(jnp.bfloat16)
-    smooth_ext = padded(smoothed, (("depth", 0), ("tile", 1)), 1)
+    extended = extended_volume(volume)
+    smoothed = smooth_block(extended)
+    keep = inside_mask(smoothed.shape[0], smoothed.shape[1])
+    smooth_ext = jnp.where(keep, smoothed, 0.0).astype(jnp.bfloat16)
     shading, lookup = shade_lookup(smooth_ext, knot_pos)
     table = ramp_table(knot_pos, knot_color, sigma_scale)
     brick_color, optical_depth = composite_block(table, lookup, shading, knot_pos.shape[0] - 1)

time: 123 us -> 137 us (1.11)
  other arithmetic: 22.2 us -> 38.4 us
  waiting for transfers between devices: 13.1 us -> 2.94 us
  local copies, waits for them, and re-layouts: 16 us -> 25.1 us
    convert_element_type x1, other arithmetic: 1.84 us -> 20.9 us  [shade_lookup(): field = smooth_ext.astype(jnp.float32)]
    ppermute x8, waiting for transfers between devices: 13.1 us -> 2.94 us  [shifted(): return lax.ppermute(block, axes if len(axes) > 1 else axes[0], pairs)]
    slice x2, local copies, waits for them, and re-layouts: 9.69 us -> 17.6 us  [next_along(): return jnp.pad(center[:, :, 1:], ((0, 0), (0, 0), (0, 1)))]
    convert_element_type x1 -> x0, other arithmetic: 5.95 us -> none  [body(): smoothed = smooth_block(extended).astype(jnp.bfloat16)]
    convert_element_type x1, other arithmetic: 1.66 us -> 4.93 us  [smooth_block(): field = extended.astype(jnp.float32)]
    slice x3, local copies, waits for them, and re-layouts: 1.25 us -> 3.66 us  [the longest x1 1.99 us: extended_volume(): x_low = shifted(volume[:, rows - 2:], tx, (1,))]
    unnamed x5 -> x11, local copies, waits for them, and re-layouts: 2.71 us -> 1.34 us
  transfers between devices with their start and end apart: 8 -> 8, of which waited for: 5 -> 1; matrix products, arithmetic and copies ran while one was open for 4% -> 5% of each run, Pallas kernels for 0% -> 0%
where the time goes in v2:
time: 137 us
  other arithmetic  38.4 us (28%)
  Pallas kernels  30.8 us (22%)
  starting transfers between devices  25.2 us (18%)
  local copies, waits for them, and re-layouts  25.1 us (18%)
  blocking collectives  13.8 us (10%)
  waiting for transfers between devices  2.94 us (2%)
    pallas_call x1, Pallas kernels, composite_block(): pl.pallas_call(kernel, grid_spec=grid_spec, out_shape=[jax.ShapeDtypeStru...  30.8 us
    ppermute x8, starting transfers between devices, shifted(): return lax.ppermute(block, axes if len(axes) > 1 else axes[0], pairs)  25.2 us
    convert_element_type x1, other arithmetic, shade_lookup(): field = smooth_ext.astype(jnp.float32)  20.9 us
    slice x2, local copies, waits for them, and re-layouts, next_along(): return jnp.pad(center[:, :, 1:], ((0, 0), (0, 0), (0, 1)))  17.6 us
    all_to_all x1, blocking collectives, body(): blocks = lax.all_to_all(weighted, 'depth', 0, 0, tiled=True)  13.8 us
    add x1, other arithmetic, shade_lookup(): 0.3 + 0.7 * facing / jnp.sqrt(slope_z * slope_z + slope_x * slope_x + slo...  10.2 us
    convert_element_type x1, other arithmetic, smooth_block(): field = extended.astype(jnp.float32)  4.93 us
    ppermute x8, waiting for transfers between devices, shifted(): return lax.ppermute(block, axes if len(axes) > 1 else axes[0], pairs)  2.94 us
  transfers between devices with their start and end apart: 8, of which 1 were waited for; matrix products, arithmetic and copies ran while one was open for 5% of the time, Pallas kernels for 0%

profile of v2, /device:TPU:24, one launch (start us, length us, event | category | flops | bytes accessed | tf_op | source)
XLA Modules:
  0.0 136.5 jit_solution(9560733355083444143)
XLA Ops:
  0.0 0.8 fusion.30
  0.8 3.3 %collective-permute-start = (bf16[1,1,1024]{2,1,0:T(2,128)(2,1)S(1)}, bf16[1,1,1024]{2,1,0:T(2,128)(2,1)S(1)}, u32[]{:S(2)}, u32[]{:S(2)}) collective-permute-start(bf16[1,1,1024]{2,1,0:T(2,128)(2,1)S(1)} %get-tuple-element.81), channel_id=1, source_target_pairs={{0,33},{1,34},{2,35},{3,36},{4,37},{5,38},{6,39},{7,40},{8,41},{9,... | collective-permute-start | bytes 6152 | tf_op jit(solution)/shard_map/ppermute | solution.py:31
  4.1 2.0 %fusion.31 = (bf16[64,2,1024]{2,1,0:T(2,128)(2,1)S(1)}, bf16[64,2,1024]{2,1,0:T(2,128)(2,1)S(1)}) fusion(bf16[64,16,1024]{2,1,0:T(8,128)(2,1)} %param.13), kind=kLoop, calls=%fused_computation.85 | loop fusion | bytes 1048576 | tf_op jit(solution)/shard_map/slice | solution.py:41
  6.1 3.8 %collective-permute-start.1 = (bf16[64,2,1024]{2,1,0:T(2,128)(2,1)S(1)}, bf16[64,2,1024]{2,1,0:T(2,128)(2,1)S(1)}, u32[]{:S(2)}, u32[]{:S(2)}) collective-permute-start(bf16[64,2,1024]{2,1,0:T(2,128)(2,1)S(1)} %get-tuple-element.83), channel_id=1, source_target_pairs={{0,1},{1,2},{2,3},{3,4},{4,5},{5,6},{6,7},{7,8},{8,9},{9,10},{10,1... | collective-permute-start | bytes 786440 | tf_op jit(solution)/shard_map/ppermute | solution.py:31
  9.9 1.3 collective-permute-start.2
  11.2 6.4 %collective-permute-start.5 = (bf16[1,1,1024]{2,1,0:T(2,128)(2,1)S(1)}, bf16[1,1,1024]{2,1,0:T(2,128)(2,1)S(1)}, u32[]{:S(2)}, u32[]{:S(2)}) collective-permute-start(bf16[1,1,1024]{2,1,0:T(2,128)(2,1)S(1)} %get-tuple-element.80), channel_id=1, source_target_pairs={{1,32},{2,33},{3,34},{4,35},{5,36},{6,37},{7,38},{8,39},{9,40},{10... | collective-permute-start | bytes 6152 | tf_op jit(solution)/shard_map/ppermute | solution.py:31
  17.6 3.5 %collective-permute-start.6 = (bf16[64,2,1024]{2,1,0:T(2,128)(2,1)S(1)}, bf16[64,2,1024]{2,1,0:T(2,128)(2,1)S(1)}, u32[]{:S(2)}, u32[]{:S(2)}) collective-permute-start(bf16[64,2,1024]{2,1,0:T(2,128)(2,1)S(1)} %get-tuple-element.84), channel_id=1, source_target_pairs={{1,0},{2,1},{3,2},{4,3},{5,4},{6,5},{7,6},{8,7},{9,8},{10,9},{11,1... | collective-permute-start | bytes 786440 | tf_op jit(solution)/shard_map/ppermute | solution.py:31
  21.1 0.9 fusion.32
  22.0 0.7 convert_element_type.24
  22.7 0.6 fusion.33
  23.3 0.1 slice_subtract_fusion.2
  23.4 0.7 convert_multiply_fusion
  24.1 0.1 subtract_divide_fusion
  24.2 0.1 and_and_fusion
  24.3 0.1 slice_reduce_fusion
  24.4 0.2 scatter.15
  24.6 0.3 scatter.16
  24.9 0.2 scatter.19.refs_0_
  25.1 0.0 copy-start
  25.2 0.0 collective-permute-done
  25.2 1.3 collective-permute-start.7
  26.5 0.0 collective-permute-done.5
  26.5 4.4 %collective-permute-start.3 = (bf16[2,16,1024]{2,1,0:T(8,128)(2,1)S(1)}, bf16[2,16,1024]{2,1,0:T(8,128)(2,1)S(1)}, u32[]{:S(2)}, u32[]{:S(2)}) collective-permute-start(bf16[2,16,1024]{2,1,0:T(8,128)(2,1)S(1)} %get-tuple-element.85), channel_id=1, source_target_pairs={{0,32},{32,64},{64,96},{96,128},{128,160},{160,192},{192,224},{1,3... | collective-permute-start | bytes 196616 | tf_op jit(solution)/shard_map/ppermute | solution.py:31
  30.9 0.0 collective-permute-done.1
  30.9 1.3 collective-permute-start.4
  32.2 0.2 constant_dynamic-update-slice_fusion.2
  32.4 0.0 collective-permute-done.2
  32.4 0.0 collective-permute-done.6
  32.5 0.2 constant_dynamic-update-slice_fusion.7
  32.7 0.0 collective-permute-done.7
  32.7 0.0 collective-permute-done.3
  32.7 2.9 %collective-permute-done.4 = bf16[2,16,1024]{2,1,0:T(8,128)(2,1)S(1)} collective-permute-done((bf16[2,16,1024]{2,1,0:T(8,128)(2,1)S(1)}, bf16[2,16,1024]{2,1,0:T(8,128)(2,1)S(1)}, u32[]{:S(2)}, u32[]{:S(2)}) %collective-permute-start.4) | collective-permute-done | bytes 65568 | tf_op jit(solution)/shard_map/ppermute | solution.py:31
  35.6 4.9 %maximum_convert_fusion = f32[68,20,1024]{2,1,0:T(8,128)} fusion(bf16[68,2,1024]{2,1,0:T(2,128)(2,1)S(1)} %constant_dynamic-update-slice_fusion.5, bf16[2,16,1024]{2,1,0:T(8,128)(2,1)S(1)} %collective-permute-done.4, bf16[64,16,1024]{2,1,0:T(8,128)(2,1)} %param.13, bf16[2,16,1024]{2,1,0:T(8,128)(2,1)S(1)} %collective-permute-done.3, ...), kind=kLoop, calls=%fused_computation.17 | loop fusion | flops 13926400 | bytes 8355840 | tf_op jit(solution)/shard_map/convert_element_type | solution.py:81
  40.6 0.0 copy-done
  40.6 12.2 %fusion.28 = (f32[66,18,1023]{2,1,0:T(8,128)}, f32[66,18,1023]{2,1,0:T(8,128)}) fusion(f32[68,20,1024]{2,1,0:T(8,128)} %maximum_convert_fusion), kind=kLoop, calls=%fused_computation.82 | loop fusion | bytes 19445184 | tf_op jit(solution)/shard_map/slice | solution.py:73
  52.8 20.9 %fusion.9 = f32[66,18,1024]{2,1,0:T(8,128)S(1)} fusion(f32[66,18,1023]{2,1,0:T(8,128)} %get-tuple-element.74, f32[66,18,1023]{2,1,0:T(8,128)} %get-tuple-element.73, f32[68,20,1024]{2,1,0:T(8,128)} %maximum_convert_fusion, pred[66,18]{1,0:T(8,128)(4,1)S(1)} %and_and_fusion), kind=kLoop, calls=%fused_computation.18 | loop fusion | flops 13381632 | bytes 38920068 | tf_op jit(solution)/shard_map/convert_element_type | solution.py:89
  73.8 5.4 %fusion.29 = (f32[64,16,1023]{2,1,0:T(8,128)}, f32[64,16,1023]{2,1,0:T(8,128)}) fusion(f32[66,18,1024]{2,1,0:T(8,128)S(1)} %fusion.9), kind=kLoop, calls=%fused_computation.83 | loop fusion | bytes 16760832 | tf_op jit(solution)/shard_map/slice | solution.py:73
  79.1 10.2 %multiply_add_fusion = (f32[64,16,1024]{2,1,0:T(8,128)}, f32[64,16,1024]{2,1,0:T(8,128)}) fusion(f32[64,16,1023]{2,1,0:T(8,128)} %get-tuple-element.78, f32[64,16,1023]{2,1,0:T(8,128)} %get-tuple-element.77, f32[66,18,1024]{2,1,0:T(8,128)S(1)} %fusion.9, f32[]{:T(128)} %bitcast.3, f32[]{:T(128)} %bitcast.2), kind=kLoop, calls=%fused_computation.16 | loop fusion | flops 24117248 | bytes 37740552 | tf_op jit(solution)/shard_map/add | solution.py:95
  89.4 30.8 %shard_map.37 = (f32[3,16,1024]{2,1,0:T(8,128)}, f32[16,1024]{1,0:T(8,128)}) custom-call(f32[8,128]{1,0:T(8,128)} %copy-done, f32[64,16,1024]{2,1,0:T(8,128)} %get-tuple-element.76.refs_1_, f32[64,16,1024]{2,1,0:T(8,128)} %get-tuple-element.75.refs_2_), custom_call_target="tpu_custom_call" | custom-call | tf_op jit(solution)/shard_map/pallas_call | solution.py:170
  120.1 0.9 copy_bitcast_fusion
  121.1 0.9 copy.9
  122.0 13.8 %all_to_all.5 = f32[8,4,16,128]{3,2,1,0:T(8,128)S(1)} all-to-all(f32[8,4,16,128]{3,2,1,0:T(8,128)S(1)} %maximum_bitcast_fusion), channel_id=1, replica_groups=mesh['depth'=8,'tile'=32] {'depth'}, dimensions={0} | all-to-all | bytes 524288 | tf_op jit(solution)/shard_map/all_to_all | solution.py:194
  135.9 0.6 pad_maximum_fusion
  (19 shorter events, 0.3 us)
Async XLA Ops:
  0.8 24.4 %collective-permute-start = (bf16[1,1,1024]{2,1,0:T(2,128)(2,1)S(1)}, bf16[1,1,1024]{2,1,0:T(2,128)(2,1)S(1)}, u32[]{:S(2)}, u32[]{:S(2)}) collective-permute-start(bf16[1,1,1024]{2,1,0:T(2,128)(2,1)S(1)} %get-tuple-element.81), channel_id=1, source_target_pairs={{0,33},{1,34},{2,35},{3,36},{4,37},{5,38},{6,39},{7,40},{8,41},{9,... | collective-permute-start | bytes 6152 | tf_op jit(solution)/shard_map/ppermute | solution.py:31
  6.1 24.8 %collective-permute-start.1 = (bf16[64,2,1024]{2,1,0:T(2,128)(2,1)S(1)}, bf16[64,2,1024]{2,1,0:T(2,128)(2,1)S(1)}, u32[]{:S(2)}, u32[]{:S(2)}) collective-permute-start(bf16[64,2,1024]{2,1,0:T(2,128)(2,1)S(1)} %get-tuple-element.83), channel_id=1, source_target_pairs={{0,1},{1,2},{2,3},{3,4},{4,5},{5,6},{6,7},{7,8},{8,9},{9,10},{10,1... | collective-permute-start | bytes 786440 | tf_op jit(solution)/shard_map/ppermute | solution.py:31
  9.9 22.5 %collective-permute-start.2 = (bf16[1,1,1024]{2,1,0:T(2,128)(2,1)S(1)}, bf16[1,1,1024]{2,1,0:T(2,128)(2,1)S(1)}, u32[]{:S(2)}, u32[]{:S(2)}) collective-permute-start(bf16[1,1,1024]{2,1,0:T(2,128)(2,1)S(1)} %get-tuple-element.79), channel_id=1, source_target_pairs={{32,1},{33,2},{34,3},{35,4},{36,5},{37,6},{38,7},{39,8},{40,9},{41... | collective-permute-start | bytes 6152 | tf_op jit(solution)/shard_map/ppermute | solution.py:31
  11.2 15.3 %collective-permute-start.5 = (bf16[1,1,1024]{2,1,0:T(2,128)(2,1)S(1)}, bf16[1,1,1024]{2,1,0:T(2,128)(2,1)S(1)}, u32[]{:S(2)}, u32[]{:S(2)}) collective-permute-start(bf16[1,1,1024]{2,1,0:T(2,128)(2,1)S(1)} %get-tuple-element.80), channel_id=1, source_target_pairs={{1,32},{2,33},{3,34},{4,35},{5,36},{6,37},{7,38},{8,39},{9,40},{10... | collective-permute-start | bytes 6152 | tf_op jit(solution)/shard_map/ppermute | solution.py:31
  17.6 14.9 %collective-permute-start.6 = (bf16[64,2,1024]{2,1,0:T(2,128)(2,1)S(1)}, bf16[64,2,1024]{2,1,0:T(2,128)(2,1)S(1)}, u32[]{:S(2)}, u32[]{:S(2)}) collective-permute-start(bf16[64,2,1024]{2,1,0:T(2,128)(2,1)S(1)} %get-tuple-element.84), channel_id=1, source_target_pairs={{1,0},{2,1},{3,2},{4,3},{5,4},{6,5},{7,6},{8,7},{9,8},{10,9},{11,1... | collective-permute-start | bytes 786440 | tf_op jit(solution)/shard_map/ppermute | solution.py:31
  25.1 15.4 %copy-start = (f32[8,128]{1,0:T(8,128)}, f32[8,128]{1,0:T(8,128)S(1)}, u32[]{:S(2)}) copy-start(f32[8,128]{1,0:T(8,128)S(1)} %scatter.19.refs_0_) | copy-start | bytes 12292
  25.2 7.5 %collective-permute-start.7 = (bf16[1,1,1024]{2,1,0:T(2,128)(2,1)S(1)}, bf16[1,1,1024]{2,1,0:T(2,128)(2,1)S(1)}, u32[]{:S(2)}, u32[]{:S(2)}) collective-permute-start(bf16[1,1,1024]{2,1,0:T(2,128)(2,1)S(1)} %get-tuple-element.82), channel_id=1, source_target_pairs={{33,0},{34,1},{35,2},{36,3},{37,4},{38,5},{39,6},{40,7},{41,8},{42... | collective-permute-start | bytes 6152 | tf_op jit(solution)/shard_map/ppermute | solution.py:31
  26.5 6.2 %collective-permute-start.3 = (bf16[2,16,1024]{2,1,0:T(8,128)(2,1)S(1)}, bf16[2,16,1024]{2,1,0:T(8,128)(2,1)S(1)}, u32[]{:S(2)}, u32[]{:S(2)}) collective-permute-start(bf16[2,16,1024]{2,1,0:T(8,128)(2,1)S(1)} %get-tuple-element.85), channel_id=1, source_target_pairs={{0,32},{32,64},{64,96},{96,128},{128,160},{160,192},{192,224},{1,3... | collective-permute-start | bytes 196616 | tf_op jit(solution)/shard_map/ppermute | solution.py:31
  30.9 4.7 %collective-permute-start.4 = (bf16[2,16,1024]{2,1,0:T(8,128)(2,1)S(1)}, bf16[2,16,1024]{2,1,0:T(8,128)(2,1)S(1)}, u32[]{:S(2)}, u32[]{:S(2)}) collective-permute-start(bf16[2,16,1024]{2,1,0:T(8,128)(2,1)S(1)} %get-tuple-element.86), channel_id=1, source_target_pairs={{32,0},{64,32},{96,64},{128,96},{160,128},{192,160},{224,192},{33,... | collective-permute-start | bytes 196616 | tf_op jit(solution)/shard_map/ppermute | solution.py:31

commit v3 on v2

--- a/solution.py
+++ b/solution.py
@@ -53,7 +53,8 @@
         [zero2[:1], jnp.concatenate([c_lh, zero1], 1), x_high,
          jnp.concatenate([c_hh, zero1], 1), zero2[:1]], axis=0)
     middle = jnp.concatenate([z_low, volume, z_high], axis=0)
-    return jnp.concatenate([left, middle, right], axis=1)
+    gap = jnp.zeros((depth + 4, 4, width), volume.dtype)
+    return jnp.concatenate([middle, right, gap, left], axis=1).astype(jnp.float32)
 
 
 def inside_mask(depth_len, rows):
@@ -112,82 +113,125 @@
     table = table.at[1, :count].set(gaps)
     table = table.at[2:6, :count].set(slopes)
     table = table.at[6, :4].set(palette[:, 0])
+    table = table.at[7, 0].set(knot_float[0])
+    table = table.at[7, 1].set(knot_float[-1])
     return table
 
 
-def composite_kernel(table, lookup_ref, shade_ref, color_ref, depth_ref, *, segments, rows):
-    depth_len = lookup_ref.shape[0]
-    width = lookup_ref.shape[2]
+def render_kernel(table, flags, planes_ref, color_ref, depth_ref, smooth_ref, square_ref, facing_ref,
+                  *, segments, rows, width):
+    stack, tall, lanes = planes_ref.shape
+    count = stack - 2
+    row = lax.broadcasted_iota(jnp.int32, (tall, lanes), 0)
+    keep_rows = ((row != tall - 1) | (flags[2] == 0)) & ((row != rows) | (flags[3] == 0))
+
+    def y_prev(a):
+        lane = lax.broadcasted_iota(jnp.int32, a.shape, 1)
+        return jnp.where(lane == 0, 0.0, pltpu.roll(a, 1, 1))
+
+    def y_next(a):
+        lane = lax.broadcasted_iota(jnp.int32, a.shape, 1)
+        return jnp.where(lane == lanes - 1, 0.0, pltpu.roll(a, lanes - 1, 1))
+
+    def smooth_plane(i, carry):
+        low = planes_ref[i]
+        mid = planes_ref[i + 1]
+        high = planes_ref[i + 2]
+        x_prev = pltpu.roll(mid, 1, 0)
+        x_next = pltpu.roll(mid, tall - 1, 0)
+        near = low + high + x_next + x_prev
+        near = near + y_prev(mid) + y_next(mid)
+        smooth = 0.4 * mid + 0.1 * near
+        inside = (i > 0) | (flags[0] == 0)
+        inside = inside & ((i < count - 1) | (flags[1] == 0))
+        smooth = jnp.where(keep_rows & inside, smooth, 0.0)
+        smooth = smooth.astype(jnp.bfloat16).astype(jnp.float32)
+        center = smooth[:rows]
+        slope_x = 0.5 * (pltpu.roll(smooth, tall - 1, 0)[:rows] - pltpu.roll(smooth, 1, 0)[:rows])
+        slope_y = 0.5 * (y_next(center) - y_prev(center))
+        smooth_ref[i] = center
+        square_ref[i] = slope_x * slope_x + slope_y * slope_y
+        facing_ref[i] = 0.8 * slope_x
+        return carry
+
+    lax.fori_loop(0, count, smooth_plane, 0)
+
     knots = [table[0, k] for k in range(segments)]
     gaps = [table[1, k] for k in range(segments)]
     slopes = [[table[2 + c, k] for k in range(segments)] for c in range(4)]
     base = [table[6, c] for c in range(4)]
-    for half in range(lookup_ref.shape[1] // rows):
-        sl = pl.ds(half * rows, rows)
-
-        def step(z, carry):
-            trans, acc0, acc1, acc2, total = carry
-            lookup = lookup_ref[z, sl, :]
-            shade = shade_ref[z, sl, :]
-            chan = [jnp.full_like(lookup, base[c]) for c in range(4)]
-            for k in range(segments):
-                t = jnp.minimum(jnp.maximum(lookup - knots[k], 0.0), gaps[k])
-                chan = [chan[c] + t * slopes[c][k] for c in range(4)]
-            ext = chan[3]
-            fade = jnp.exp(-ext)
-            weight = shade * (1.0 - fade) * trans
-            acc0 = acc0 + weight * chan[0]
-            acc1 = acc1 + weight * chan[1]
-            acc2 = acc2 + weight * chan[2]
-            return (trans * fade, acc0, acc1, acc2, total + ext)
-
-        zeros = jnp.zeros((rows, width), jnp.float32)
-        init = (jnp.ones((rows, width), jnp.float32), zeros, zeros, zeros, zeros)
-        _, acc0, acc1, acc2, total = lax.fori_loop(0, depth_len, step, init, unroll=2)
-        color_ref[0, sl, :] = acc0
-        color_ref[1, sl, :] = acc1
-        color_ref[2, sl, :] = acc2
-        depth_ref[sl, :] = total
-
-
-def composite_block(table, lookup, shading, segments):
-    depth_len, rows_all, width_all = lookup.shape
-    width = 256
-    rows = 8
-    kernel = lambda *refs: composite_kernel(*refs, segments=segments, rows=rows)
-    grid_spec = pltpu.PrefetchScalarGridSpec(
-        num_scalar_prefetch=1,
-        grid=(width_all // width,),
+    lo = table[7, 0]
+    hi = table[7, 1]
+    sub = 8
+    for r0 in range(0, rows, sub):
+        for c0 in range(0, lanes, width):
+            rs = pl.ds(r0, sub)
+            cs = pl.ds(c0, width)
+
+            def step(z, carry):
+                trans, acc0, acc1, acc2, total = carry
+                center = smooth_ref[z + 1, rs, cs]
+                slope_z = 0.5 * (smooth_ref[z + 2, rs, cs] - smooth_ref[z, rs, cs])
+                facing = jnp.abs(0.6 * slope_z + facing_ref[z + 1, rs, cs])
+                norm = slope_z * slope_z + square_ref[z + 1, rs, cs] + 0.1
+                shade = 0.3 + 0.7 * facing * lax.rsqrt(norm)
+                lookup = jnp.clip(127.5 + 70.0 * center, lo, hi)
+                chan = [jnp.full_like(lookup, base[c]) for c in range(4)]
+                for k in range(segments):
+                    t = jnp.minimum(jnp.maximum(lookup - knots[k], 0.0), gaps[k])
+                    chan = [chan[c] + t * slopes[c][k] for c in range(4)]
+                ext = chan[3]
+                fade = jnp.exp(-ext)
+                weight = shade * (1.0 - fade) * trans
+                acc0 = acc0 + weight * chan[0]
+                acc1 = acc1 + weight * chan[1]
+                acc2 = acc2 + weight * chan[2]
+                return (trans * fade, acc0, acc1, acc2, total + ext)
+
+            zeros = jnp.zeros((sub, width), jnp.float32)
+            init = (jnp.ones((sub, width), jnp.float32), zeros, zeros, zeros, zeros)
+            _, acc0, acc1, acc2, total = lax.fori_loop(0, count - 2, step, init, unroll=2)
+            color_ref[0, rs, cs] = acc0
+            color_ref[1, rs, cs] = acc1
+            color_ref[2, rs, cs] = acc2
+            depth_ref[rs, cs] = total
+
+
+def render_block(table, flags, planes, rows, segments):
+    stack, tall, lanes = planes.shape
+    count = stack - 2
+    kernel = lambda *refs: render_kernel(*refs, segments=segments, rows=rows, width=256)
+    return pl.pallas_call(
+        kernel,
         in_specs=[
-            pl.BlockSpec((depth_len, rows_all, width), lambda j, t: (0, 0, j)),
-            pl.BlockSpec((depth_len, rows_all, width), lambda j, t: (0, 0, j)),
+            pl.BlockSpec(memory_space=pltpu.SMEM),
+            pl.BlockSpec(memory_space=pltpu.SMEM),
+            pl.BlockSpec(memory_space=pltpu.VMEM),
         ],
         out_specs=[
-            pl.BlockSpec((3, rows_all, width), lambda j, t: (0, 0, j)),
-            pl.BlockSpec((rows_all, width), lambda j, t: (0, j)),
+            pl.BlockSpec(memory_space=pltpu.VMEM),
+            pl.BlockSpec(memory_space=pltpu.VMEM),
         ],
-    )
-    return pl.pallas_call(
-        kernel,
-        grid_spec=grid_spec,
         out_shape=[
-            jax.ShapeDtypeStruct((3, rows_all, width_all), jnp.float32),
-            jax.ShapeDtypeStruct((rows_all, width_all), jnp.float32),
+            jax.ShapeDtypeStruct((3, rows, lanes), jnp.float32),
+            jax.ShapeDtypeStruct((rows, lanes), jnp.float32),
         ],
-    )(table, lookup, shading)
+        scratch_shapes=[pltpu.VMEM((count, rows, lanes), jnp.float32) for _ in range(3)],
+        compiler_params=pltpu.CompilerParams(vmem_limit_bytes=48 * 1024 * 1024),
+    )(table, flags, planes)
 
 
 def body(volume, knot_pos, knot_color):
     depth_count = lax.axis_size("depth")
     brick_depth, brick_rows, row_width = volume.shape
     sigma_scale = 4.0 / (brick_depth * depth_count)
-    extended = extended_volume(volume)
-    smoothed = smooth_block(extended)
-    keep = inside_mask(smoothed.shape[0], smoothed.shape[1])
-    smooth_ext = jnp.where(keep, smoothed, 0.0).astype(jnp.bfloat16)
-    shading, lookup = shade_lookup(smooth_ext, knot_pos)
+    planes = extended_volume(volume)
+    d = lax.axis_index("depth")
+    t = lax.axis_index("tile")
+    flags = jnp.stack([d == 0, d == depth_count - 1, t == 0, t == lax.axis_size("tile") - 1])
     table = ramp_table(knot_pos, knot_color, sigma_scale)
-    brick_color, optical_depth = composite_block(table, lookup, shading, knot_pos.shape[0] - 1)
+    brick_color, optical_depth = render_block(
+        table, flags.astype(jnp.int32), planes, brick_rows, knot_pos.shape[0] - 1)
     piece = row_width // depth_count
     weighted = jnp.concatenate([brick_color, optical_depth[None]], axis=0)
     weighted = weighted.reshape(4, brick_rows, depth_count, piece).transpose(2, 0, 1, 3)

time: 137 us -> 101 us (0.74)
  other arithmetic: 38.4 us -> 7.05 us
  local copies, waits for them, and re-layouts: 25.1 us -> 7.17 us
  Pallas kernels: 30.8 us -> 44.4 us
    convert_element_type x2, other arithmetic: 25.9 us -> 4.85 us  [the longest x1 4.77 us: extended_volume(): jnp.concatenate([middle, right, gap, left], axis=1).astype(jnp.float32)]
    slice x5 -> x3, local copies, waits for them, and re-layouts: 21 us -> 3.36 us  [the longest x1 1.99 us: extended_volume(): x_high = shifted(volume[:, :2], tx, (-1,))]
    pallas_call x1, Pallas kernels: 30.8 us -> 44.4 us  [render_block(): pl.pallas_call(kernel, in_specs=[pl.BlockSpec(memory_space=pltpu.SMEM), p...]
    add x1 -> x0, other arithmetic: 10.2 us -> none  [shade_lookup(): 0.3 + 0.7 * facing / jnp.sqrt(slope_z * slope_z + slope_x * slope_x + slo...]
    scatter x0 -> x2, local copies, waits for them, and re-layouts: none -> 1.48 us  [the longest x1 0.78 us: ramp_table(): table = table.at[7, 1].set(knot_float[-1])]
  transfers between devices with their start and end apart: 8 -> 8, of which waited for: 1 -> 2; matrix products, arithmetic and copies ran while one was open for 5% -> 8% of each run, Pallas kernels for 0% -> 0%
where the time goes in v3:
time: 101 us
  Pallas kernels  44.4 us (44%)
  starting transfers between devices  25.8 us (26%)
  blocking collectives  13.8 us (14%)
  local copies, waits for them, and re-layouts  7.17 us (7%)
  other arithmetic  7.05 us (7%)
  waiting for transfers between devices  2.33 us (2%)
    pallas_call x1, Pallas kernels, render_block(): pl.pallas_call(kernel, in_specs=[pl.BlockSpec(memory_space=pltpu.SMEM), p...  44.4 us
    ppermute x8, starting transfers between devices, shifted(): return lax.ppermute(block, axes if len(axes) > 1 else axes[0], pairs)  25.8 us
    all_to_all x1, blocking collectives, body(): blocks = lax.all_to_all(weighted, 'depth', 0, 0, tiled=True)  13.8 us
    convert_element_type x1, other arithmetic, extended_volume(): jnp.concatenate([middle, right, gap, left], axis=1).astype(jnp.float32)  4.77 us
    ppermute x8, waiting for transfers between devices, shifted(): return lax.ppermute(block, axes if len(axes) > 1 else axes[0], pairs)  2.33 us
  transfers between devices with their start and end apart: 8, of which 2 were waited for; matrix products, arithmetic and copies ran while one was open for 8% of the time, Pallas kernels for 0%

profile of v3, /device:TPU:24, one launch (start us, length us, event | category | flops | bytes accessed | tf_op | source)
XLA Modules:
  0.0 100.8 jit_solution(8345108190374992369)
XLA Ops:
  0.0 0.8 fusion.19
  0.8 7.4 %collective-permute-start.2 = (bf16[1,1,1024]{2,1,0:T(2,128)(2,1)S(1)}, bf16[1,1,1024]{2,1,0:T(2,128)(2,1)S(1)}, u32[]{:S(2)}, u32[]{:S(2)}) collective-permute-start(bf16[1,1,1024]{2,1,0:T(2,128)(2,1)S(1)} %get-tuple-element.101), channel_id=1, source_target_pairs={{1,32},{2,33},{3,34},{4,35},{5,36},{6,37},{7,38},{8,39},{9,40},{10... | collective-permute-start | bytes 6152 | tf_op jit(solution)/shard_map/ppermute | solution.py:31
  8.2 2.0 %fusion.20 = (bf16[64,2,1024]{2,1,0:T(2,128)(2,1)S(1)}, bf16[64,2,1024]{2,1,0:T(2,128)(2,1)S(1)}) fusion(bf16[64,16,1024]{2,1,0:T(8,128)(2,1)} %param.17), kind=kLoop, calls=%fused_computation.63 | loop fusion | bytes 1048576 | tf_op jit(solution)/shard_map/slice | solution.py:42
  10.2 2.9 %collective-permute-start.3 = (bf16[64,2,1024]{2,1,0:T(2,128)(2,1)S(1)}, bf16[64,2,1024]{2,1,0:T(2,128)(2,1)S(1)}, u32[]{:S(2)}, u32[]{:S(2)}) collective-permute-start(bf16[64,2,1024]{2,1,0:T(2,128)(2,1)S(1)} %get-tuple-element.103), channel_id=1, source_target_pairs={{1,0},{2,1},{3,2},{4,3},{5,4},{6,5},{7,6},{8,7},{9,8},{10,9},{11,1... | collective-permute-start | bytes 786440 | tf_op jit(solution)/shard_map/ppermute | solution.py:31
  13.1 1.3 %collective-permute-start.4 = (bf16[1,1,1024]{2,1,0:T(2,128)(2,1)S(1)}, bf16[1,1,1024]{2,1,0:T(2,128)(2,1)S(1)}, u32[]{:S(2)}, u32[]{:S(2)}) collective-permute-start(bf16[1,1,1024]{2,1,0:T(2,128)(2,1)S(1)} %get-tuple-element.99), channel_id=1, source_target_pairs={{33,0},{34,1},{35,2},{36,3},{37,4},{38,5},{39,6},{40,7},{41,8},{42... | collective-permute-start | bytes 6152 | tf_op jit(solution)/shard_map/ppermute | solution.py:31
  14.4 4.5 %collective-permute-start.5 = (bf16[1,1,1024]{2,1,0:T(2,128)(2,1)S(1)}, bf16[1,1,1024]{2,1,0:T(2,128)(2,1)S(1)}, u32[]{:S(2)}, u32[]{:S(2)}) collective-permute-start(bf16[1,1,1024]{2,1,0:T(2,128)(2,1)S(1)} %get-tuple-element.100), channel_id=1, source_target_pairs={{0,33},{1,34},{2,35},{3,36},{4,37},{5,38},{6,39},{7,40},{8,41},{9,... | collective-permute-start | bytes 6152 | tf_op jit(solution)/shard_map/ppermute | solution.py:31
  18.9 2.7 %collective-permute-start.6 = (bf16[64,2,1024]{2,1,0:T(2,128)(2,1)S(1)}, bf16[64,2,1024]{2,1,0:T(2,128)(2,1)S(1)}, u32[]{:S(2)}, u32[]{:S(2)}) collective-permute-start(bf16[64,2,1024]{2,1,0:T(2,128)(2,1)S(1)} %get-tuple-element.104), channel_id=1, source_target_pairs={{0,1},{1,2},{2,3},{3,4},{4,5},{5,6},{6,7},{7,8},{8,9},{9,10},{10,1... | collective-permute-start | bytes 786440 | tf_op jit(solution)/shard_map/ppermute | solution.py:31
  21.6 0.7 convert_element_type.12
  22.3 0.1 slice_subtract_fusion
  22.3 0.6 fusion.21
  22.9 0.9 fusion.18
  23.8 0.7 convert_multiply_fusion
  24.6 0.1 slice_reduce_fusion
  24.7 0.1 subtract_divide_fusion
  24.7 0.1 add_convert_fusion.refs_1_
  24.8 0.2 scatter.21
  25.0 0.3 scatter.24
  25.3 0.2 scatter.25
  25.5 0.7 scatter.26
  26.2 0.8 scatter.29.refs_0_
  27.0 0.1 pad.37.clone
  27.1 0.0 collective-permute-done.2
  27.1 1.3 %collective-permute-start.7 = (bf16[1,1,1024]{2,1,0:T(2,128)(2,1)S(1)}, bf16[1,1,1024]{2,1,0:T(2,128)(2,1)S(1)}, u32[]{:S(2)}, u32[]{:S(2)}) collective-permute-start(bf16[1,1,1024]{2,1,0:T(2,128)(2,1)S(1)} %get-tuple-element.102), channel_id=1, source_target_pairs={{32,1},{33,2},{34,3},{35,4},{36,5},{37,6},{38,7},{39,8},{40,9},{41... | collective-permute-start | bytes 6152 | tf_op jit(solution)/shard_map/ppermute | solution.py:31
  28.4 0.0 collective-permute-done.5
  28.4 4.5 %collective-permute-start = (bf16[2,16,1024]{2,1,0:T(8,128)(2,1)S(1)}, bf16[2,16,1024]{2,1,0:T(8,128)(2,1)S(1)}, u32[]{:S(2)}, u32[]{:S(2)}) collective-permute-start(bf16[2,16,1024]{2,1,0:T(8,128)(2,1)S(1)} %get-tuple-element.97), channel_id=1, source_target_pairs={{0,32},{32,64},{64,96},{96,128},{128,160},{160,192},{192,224},{1,3... | collective-permute-start | bytes 196616 | tf_op jit(solution)/shard_map/ppermute | solution.py:31
  32.9 0.0 collective-permute-done.3
  32.9 1.3 %collective-permute-start.1 = (bf16[2,16,1024]{2,1,0:T(8,128)(2,1)S(1)}, bf16[2,16,1024]{2,1,0:T(8,128)(2,1)S(1)}, u32[]{:S(2)}, u32[]{:S(2)}) collective-permute-start(bf16[2,16,1024]{2,1,0:T(8,128)(2,1)S(1)} %get-tuple-element.98), channel_id=1, source_target_pairs={{32,0},{64,32},{96,64},{128,96},{160,128},{192,160},{224,192},{33,... | collective-permute-start | bytes 196616 | tf_op jit(solution)/shard_map/ppermute | solution.py:31
  34.2 0.2 constant_dynamic-update-slice_fusion.2
  34.5 0.0 collective-permute-done.4
  34.5 0.0 collective-permute-done.6
  34.5 0.2 constant_dynamic-update-slice_fusion.7
  34.7 0.2 collective-permute-done.7
  35.0 0.0 collective-permute-done
  35.0 2.1 %collective-permute-done.1 = bf16[2,16,1024]{2,1,0:T(8,128)(2,1)S(1)} collective-permute-done((bf16[2,16,1024]{2,1,0:T(8,128)(2,1)S(1)}, bf16[2,16,1024]{2,1,0:T(8,128)(2,1)S(1)}, u32[]{:S(2)}, u32[]{:S(2)}) %collective-permute-start.1) | collective-permute-done | bytes 65568 | tf_op jit(solution)/shard_map/ppermute | solution.py:31
  37.1 4.8 %maximum_convert_fusion.refs_2_ = f32[68,24,1024]{2,1,0:T(8,128)} fusion(bf16[68,2,1024]{2,1,0:T(2,128)(2,1)S(1)} %constant_dynamic-update-slice_fusion.5, bf16[68,2,1024]{2,1,0:T(2,128)(2,1)S(1)} %constant_dynamic-update-slice_fusion, bf16[2,16,1024]{2,1,0:T(8,128)(2,1)S(1)} %collective-permute-done.1, bf16[64,16,1024]{2,1,0:T(8,128)(2,1)} %param.17, ...), kind=kLoop, calls=%fused_computation | loop fusion | flops 20054016 | bytes 9470000 | tf_op jit(solution)/shard_map/convert_element_type | solution.py:57
  41.8 44.4 %shard_map.37 = (f32[3,16,1024]{2,1,0:T(8,128)S(1)}, f32[16,1024]{1,0:T(8,128)S(1)}) custom-call(f32[8,128]{1,0:T(8,128)S(1)} %scatter.29.refs_0_, s32[4]{0:T(128)S(1)} %add_convert_fusion.refs_1_, f32[68,24,1024]{2,1,0:T(8,128)} %maximum_convert_fusion.refs_2_), custom_call_target="tpu_custom_call" | custom-call | tf_op jit(solution)/shard_map/pallas_call | solution.py:204
  86.3 13.8 %all_to_all.5 = f32[8,4,16,128]{3,2,1,0:T(8,128)S(1)} all-to-all(f32[8,4,16,128]{3,2,1,0:T(8,128)S(1)} %maximum_bitcast_fusion), channel_id=1, replica_groups=mesh['depth'=8,'tile'=32] {'depth'}, dimensions={0} | all-to-all | bytes 524288 | tf_op jit(solution)/shard_map/all_to_all | solution.py:238
  100.2 0.6 pad_maximum_fusion
  (20 shorter events, 0.3 us)
Async XLA Ops:
  0.8 26.3 %collective-permute-start.2 = (bf16[1,1,1024]{2,1,0:T(2,128)(2,1)S(1)}, bf16[1,1,1024]{2,1,0:T(2,128)(2,1)S(1)}, u32[]{:S(2)}, u32[]{:S(2)}) collective-permute-start(bf16[1,1,1024]{2,1,0:T(2,128)(2,1)S(1)} %get-tuple-element.101), channel_id=1, source_target_pairs={{1,32},{2,33},{3,34},{4,35},{5,36},{6,37},{7,38},{8,39},{9,40},{10... | collective-permute-start | bytes 6152 | tf_op jit(solution)/shard_map/ppermute | solution.py:31
  10.2 22.8 %collective-permute-start.3 = (bf16[64,2,1024]{2,1,0:T(2,128)(2,1)S(1)}, bf16[64,2,1024]{2,1,0:T(2,128)(2,1)S(1)}, u32[]{:S(2)}, u32[]{:S(2)}) collective-permute-start(bf16[64,2,1024]{2,1,0:T(2,128)(2,1)S(1)} %get-tuple-element.103), channel_id=1, source_target_pairs={{1,0},{2,1},{3,2},{4,3},{5,4},{6,5},{7,6},{8,7},{9,8},{10,9},{11,1... | collective-permute-start | bytes 786440 | tf_op jit(solution)/shard_map/ppermute | solution.py:31
  13.1 21.4 %collective-permute-start.4 = (bf16[1,1,1024]{2,1,0:T(2,128)(2,1)S(1)}, bf16[1,1,1024]{2,1,0:T(2,128)(2,1)S(1)}, u32[]{:S(2)}, u32[]{:S(2)}) collective-permute-start(bf16[1,1,1024]{2,1,0:T(2,128)(2,1)S(1)} %get-tuple-element.99), channel_id=1, source_target_pairs={{33,0},{34,1},{35,2},{36,3},{37,4},{38,5},{39,6},{40,7},{41,8},{42... | collective-permute-start | bytes 6152 | tf_op jit(solution)/shard_map/ppermute | solution.py:31
  14.4 14.0 %collective-permute-start.5 = (bf16[1,1,1024]{2,1,0:T(2,128)(2,1)S(1)}, bf16[1,1,1024]{2,1,0:T(2,128)(2,1)S(1)}, u32[]{:S(2)}, u32[]{:S(2)}) collective-permute-start(bf16[1,1,1024]{2,1,0:T(2,128)(2,1)S(1)} %get-tuple-element.100), channel_id=1, source_target_pairs={{0,33},{1,34},{2,35},{3,36},{4,37},{5,38},{6,39},{7,40},{8,41},{9,... | collective-permute-start | bytes 6152 | tf_op jit(solution)/shard_map/ppermute | solution.py:31
  18.9 15.6 %collective-permute-start.6 = (bf16[64,2,1024]{2,1,0:T(2,128)(2,1)S(1)}, bf16[64,2,1024]{2,1,0:T(2,128)(2,1)S(1)}, u32[]{:S(2)}, u32[]{:S(2)}) collective-permute-start(bf16[64,2,1024]{2,1,0:T(2,128)(2,1)S(1)} %get-tuple-element.104), channel_id=1, source_target_pairs={{0,1},{1,2},{2,3},{3,4},{4,5},{5,6},{6,7},{7,8},{8,9},{9,10},{10,1... | collective-permute-start | bytes 786440 | tf_op jit(solution)/shard_map/ppermute | solution.py:31
  27.1 7.9 %collective-permute-start.7 = (bf16[1,1,1024]{2,1,0:T(2,128)(2,1)S(1)}, bf16[1,1,1024]{2,1,0:T(2,128)(2,1)S(1)}, u32[]{:S(2)}, u32[]{:S(2)}) collective-permute-start(bf16[1,1,1024]{2,1,0:T(2,128)(2,1)S(1)} %get-tuple-element.102), channel_id=1, source_target_pairs={{32,1},{33,2},{34,3},{35,4},{36,5},{37,6},{38,7},{39,8},{40,9},{41... | collective-permute-start | bytes 6152 | tf_op jit(solution)/shard_map/ppermute | solution.py:31
  28.4 6.6 %collective-permute-start = (bf16[2,16,1024]{2,1,0:T(8,128)(2,1)S(1)}, bf16[2,16,1024]{2,1,0:T(8,128)(2,1)S(1)}, u32[]{:S(2)}, u32[]{:S(2)}) collective-permute-start(bf16[2,16,1024]{2,1,0:T(8,128)(2,1)S(1)} %get-tuple-element.97), channel_id=1, source_target_pairs={{0,32},{32,64},{64,96},{96,128},{128,160},{160,192},{192,224},{1,3... | collective-permute-start | bytes 196616 | tf_op jit(solution)/shard_map/ppermute | solution.py:31
  32.9 4.1 %collective-permute-start.1 = (bf16[2,16,1024]{2,1,0:T(8,128)(2,1)S(1)}, bf16[2,16,1024]{2,1,0:T(8,128)(2,1)S(1)}, u32[]{:S(2)}, u32[]{:S(2)}) collective-permute-start(bf16[2,16,1024]{2,1,0:T(8,128)(2,1)S(1)} %get-tuple-element.98), channel_id=1, source_target_pairs={{32,0},{64,32},{96,64},{128,96},{160,128},{192,160},{224,192},{33,... | collective-permute-start | bytes 196616 | tf_op jit(solution)/shard_map/ppermute | solution.py:31

commit v4 on v3

--- a/solution.py
+++ b/solution.py
@@ -101,24 +101,31 @@
     return shading, lookup
 
 
-def ramp_table(knot_pos, knot_color, sigma_scale):
+def segment_tables(knot_pos, knot_color, sigma_scale):
     knot_float = knot_pos.astype(jnp.float32)
     palette = knot_color.astype(jnp.float32) / 255.0
     palette = palette.at[3].multiply(sigma_scale)
+    count = knot_pos.shape[0]
+    inner = knot_float[1:count - 1]
+    bins = 32
+    start = 8.0 * jnp.arange(bins, dtype=jnp.float32)
+    in_bin = (inner[None, :] >= start[:, None]) & (inner[None, :] < start[:, None] + 8.0)
+    threshold = jnp.where(in_bin.any(axis=1), jnp.sum(jnp.where(in_bin, inner[None, :], 0.0), axis=1), 1e30)
+    below = jnp.sum((inner[None, :] < start[:, None]).astype(jnp.int32), axis=1)
+    segment = jnp.minimum(jnp.stack([below, below + 1], axis=1).reshape(-1), count - 2)
     gaps = knot_float[1:] - knot_float[:-1]
     slopes = (palette[:, 1:] - palette[:, :-1]) / gaps[None]
-    count = knot_pos.shape[0] - 1
-    table = jnp.zeros((8, 128), jnp.float32)
-    table = table.at[0, :count].set(knot_float[:-1])
-    table = table.at[1, :count].set(gaps)
-    table = table.at[2:6, :count].set(slopes)
-    table = table.at[6, :4].set(palette[:, 0])
-    table = table.at[7, 0].set(knot_float[0])
-    table = table.at[7, 1].set(knot_float[-1])
-    return table
-
-
-def render_kernel(table, flags, planes_ref, color_ref, depth_ref, smooth_ref, square_ref, facing_ref,
+    rows = [threshold, knot_float[segment]]
+    rows += [palette[c, segment] for c in range(4)]
+    rows += [slopes[c, segment] for c in range(4)]
+    table = jnp.zeros((len(rows), 128), jnp.float32)
+    for r, values in enumerate(rows):
+        table = table.at[r, :values.shape[0]].set(values)
+    bounds = jnp.zeros((8, 128), jnp.float32).at[0, 0].set(knot_float[0]).at[0, 1].set(knot_float[-1])
+    return jnp.broadcast_to(table[:, None, :], (len(rows), 8, 128)), bounds
+
+
+def render_kernel(table, flags, lanes_ref, planes_ref, color_ref, depth_ref, smooth_ref, square_ref, facing_ref,
                   *, segments, rows, width):
     stack, tall, lanes = planes_ref.shape
     count = stack - 2
@@ -156,17 +163,22 @@
 
     lax.fori_loop(0, count, smooth_plane, 0)
 
-    knots = [table[0, k] for k in range(segments)]
-    gaps = [table[1, k] for k in range(segments)]
-    slopes = [[table[2 + c, k] for k in range(segments)] for c in range(4)]
-    base = [table[6, c] for c in range(4)]
-    lo = table[7, 0]
-    hi = table[7, 1]
+    lo = table[0, 0]
+    hi = table[0, 1]
     sub = 8
     for r0 in range(0, rows, sub):
         for c0 in range(0, lanes, width):
             rs = pl.ds(r0, sub)
             cs = pl.ds(c0, width)
+            tabs = [lanes_ref[r] for r in range(lanes_ref.shape[0])]
+
+            def classify(lookup):
+                scaled = (lookup * 0.125).astype(jnp.int32)
+                above = lookup >= jnp.take_along_axis(tabs[0], scaled, axis=1, mode="promise_in_bounds")
+                index = scaled + scaled + above.astype(jnp.int32)
+                pick = lambda r: jnp.take_along_axis(tabs[r], index, axis=1, mode="promise_in_bounds")
+                offset = lookup - pick(1)
+                return [pick(2 + c) + pick(6 + c) * offset for c in range(4)]
 
             def step(z, carry):
                 trans, acc0, acc1, acc2, total = carry
@@ -176,10 +188,8 @@
                 norm = slope_z * slope_z + square_ref[z + 1, rs, cs] + 0.1
                 shade = 0.3 + 0.7 * facing * lax.rsqrt(norm)
                 lookup = jnp.clip(127.5 + 70.0 * center, lo, hi)
-                chan = [jnp.full_like(lookup, base[c]) for c in range(4)]
-                for k in range(segments):
-                    t = jnp.minimum(jnp.maximum(lookup - knots[k], 0.0), gaps[k])
-                    chan = [chan[c] + t * slopes[c][k] for c in range(4)]
+                parts = [classify(lookup[:, g:g + 128]) for g in range(0, width, 128)]
+                chan = [jnp.concatenate([p[c] for p in parts], axis=1) for c in range(4)]
                 ext = chan[3]
                 fade = jnp.exp(-ext)
                 weight = shade * (1.0 - fade) * trans
@@ -197,7 +207,7 @@
             depth_ref[rs, cs] = total
 
 
-def render_block(table, flags, planes, rows, segments):
+def render_block(table, flags, lane_tables, planes, rows, segments):
     stack, tall, lanes = planes.shape
     count = stack - 2
     kernel = lambda *refs: render_kernel(*refs, segments=segments, rows=rows, width=256)
@@ -207,6 +217,7 @@
             pl.BlockSpec(memory_space=pltpu.SMEM),
             pl.BlockSpec(memory_space=pltpu.SMEM),
             pl.BlockSpec(memory_space=pltpu.VMEM),
+            pl.BlockSpec(memory_space=pltpu.VMEM),
         ],
         out_specs=[
             pl.BlockSpec(memory_space=pltpu.VMEM),
@@ -218,7 +229,7 @@
         ],
         scratch_shapes=[pltpu.VMEM((count, rows, lanes), jnp.float32) for _ in range(3)],
         compiler_params=pltpu.CompilerParams(vmem_limit_bytes=48 * 1024 * 1024),
-    )(table, flags, planes)
+    )(table, flags, lane_tables, planes)
 
 
 def body(volume, knot_pos, knot_color):
@@ -229,9 +240,9 @@
     d = lax.axis_index("depth")
     t = lax.axis_index("tile")
     flags = jnp.stack([d == 0, d == depth_count - 1, t == 0, t == lax.axis_size("tile") - 1])
-    table = ramp_table(knot_pos, knot_color, sigma_scale)
+    lane_tables, bounds = segment_tables(knot_pos, knot_color, sigma_scale)
     brick_color, optical_depth = render_block(
-        table, flags.astype(jnp.int32), planes, brick_rows, knot_pos.shape[0] - 1)
+        bounds, flags.astype(jnp.int32), lane_tables, planes, brick_rows, knot_pos.shape[0] - 1)
     piece = row_width // depth_count
     weighted = jnp.concatenate([brick_color, optical_depth[None]], axis=0)
     weighted = weighted.reshape(4, brick_rows, depth_count, piece).transpose(2, 0, 1, 3)

time: 101 us -> 153 us (1.51)
  Pallas kernels: 44.4 us -> 72.5 us
  local copies, waits for them, and re-layouts: 7.17 us -> 27.9 us
  other arithmetic: 7.05 us -> 10.1 us
    pallas_call x1, Pallas kernels: 44.4 us -> 72.5 us  [render_block(): pl.pallas_call(kernel, in_specs=[pl.BlockSpec(memory_space=pltpu.SMEM), p...]
    gather x0 -> x9, local copies, waits for them, and re-layouts: none -> 10.1 us  [the longest x4 5.16 us: segment_tables(): rows += [palette[c, segment] for c in range(4)]]
    scatter x6 -> x12, local copies, waits for them, and re-layouts: 2.15 us -> 7.2 us  [the longest x10 4.61 us: segment_tables(): table = table.at[r, :values.shape[0]].set(values)]
    unnamed x9 -> x11, local copies, waits for them, and re-layouts: 0.49 us -> 2.5 us
  transfers between devices with their start and end apart: 8 -> 8, of which waited for: 2 -> 1; matrix products, arithmetic and copies ran while one was open for 8% -> 21% of each run, Pallas kernels for 0% -> 0%
where the time goes in v4:
time: 153 us; the launch traced here: 152 us
  Pallas kernels  72.5 us (47%)
  local copies, waits for them, and re-layouts  27.9 us (18%)
  starting transfers between devices  25.8 us (17%)
  blocking collectives  13.8 us (9%)
  other arithmetic  10.1 us (7%)
  waiting for transfers between devices  1.66 us (1%)
    pallas_call x1, Pallas kernels, render_block(): pl.pallas_call(kernel, in_specs=[pl.BlockSpec(memory_space=pltpu.SMEM), p...  72.5 us
    ppermute x8, starting transfers between devices, shifted(): return lax.ppermute(block, axes if len(axes) > 1 else axes[0], pairs)  25.8 us
    all_to_all x1, blocking collectives, body(): blocks = lax.all_to_all(weighted, 'depth', 0, 0, tiled=True)  13.8 us
    gather x4, local copies, waits for them, and re-layouts, segment_tables(): rows += [palette[c, segment] for c in range(4)]  5.16 us
    scatter x10, local copies, waits for them, and re-layouts, segment_tables(): table = table.at[r, :values.shape[0]].set(values)  4.61 us
    convert_element_type x1, other arithmetic, extended_volume(): jnp.concatenate([middle, right, gap, left], axis=1).astype(jnp.float32)  3.53 us
    gather x4, local copies, waits for them, and re-layouts, segment_tables(): rows += [slopes[c, segment] for c in range(4)]  3.53 us
  transfers between devices with their start and end apart: 8, of which 1 were waited for; matrix products, arithmetic and copies ran while one was open for 21% of the time, Pallas kernels for 0%

profile of v4, /device:TPU:24, one launch (start us, length us, event | category | flops | bytes accessed | tf_op | source)
XLA Modules:
  0.0 152.0 jit_solution(6712580188335517113)
XLA Ops:
  0.0 1.5 %fusion.24 = (bf16[1,1,1024]{2,1,0:T(2,128)(2,1)}, bf16[1,1,1024]{2,1,0:T(2,128)(2,1)}, bf16[1,1,1024]{2,1,0:T(2,128)(2,1)}, bf16[1,1,1024]{2,1,0:T(2,128)(2,1)}) fusion(bf16[64,16,1024]{2,1,0:T(8,128)(2,1)} %param.29), kind=kLoop, calls=%fused_computation.91 | loop fusion | bytes 16384 | tf_op jit(solution)/shard_map/slice | solution.py:46
  1.5 8.0 %collective-permute-start.2 = (bf16[1,1,1024]{2,1,0:T(2,128)(2,1)}, bf16[1,1,1024]{2,1,0:T(2,128)(2,1)}, u32[]{:S(2)}, u32[]{:S(2)}) collective-permute-start(bf16[1,1,1024]{2,1,0:T(2,128)(2,1)} %get-tuple-element.177), channel_id=1, source_target_pairs={{1,32},{2,33},{3,34},{4,35},{5,36},{6,37},{7,38},{8,39},{9,40},{10... | collective-permute-start | bytes 6152 | tf_op jit(solution)/shard_map/ppermute | solution.py:31
  9.5 2.7 %fusion.25 = (bf16[64,2,1024]{2,1,0:T(2,128)(2,1)}, bf16[64,2,1024]{2,1,0:T(2,128)(2,1)S(1)}) fusion(bf16[64,16,1024]{2,1,0:T(8,128)(2,1)} %param.29), kind=kLoop, calls=%fused_computation.92 | loop fusion | bytes 1048576 | tf_op jit(solution)/shard_map/slice | solution.py:42
  12.2 2.9 %collective-permute-start.3 = (bf16[64,2,1024]{2,1,0:T(2,128)(2,1)}, bf16[64,2,1024]{2,1,0:T(2,128)(2,1)S(1)}, u32[]{:S(2)}, u32[]{:S(2)}) collective-permute-start(bf16[64,2,1024]{2,1,0:T(2,128)(2,1)} %get-tuple-element.179), channel_id=1, source_target_pairs={{1,0},{2,1},{3,2},{4,3},{5,4},{6,5},{7,6},{8,7},{9,8},{10,9},{11,1... | collective-permute-start | bytes 786440 | tf_op jit(solution)/shard_map/ppermute | solution.py:31
  15.1 1.3 collective-permute-start.4
  16.4 4.8 %collective-permute-start.5 = (bf16[1,1,1024]{2,1,0:T(2,128)(2,1)}, bf16[1,1,1024]{2,1,0:T(2,128)(2,1)}, u32[]{:S(2)}, u32[]{:S(2)}) collective-permute-start(bf16[1,1,1024]{2,1,0:T(2,128)(2,1)} %get-tuple-element.176), channel_id=1, source_target_pairs={{0,33},{1,34},{2,35},{3,36},{4,37},{5,38},{6,39},{7,40},{8,41},{9,... | collective-permute-start | bytes 6152 | tf_op jit(solution)/shard_map/ppermute | solution.py:31
  21.2 2.9 %collective-permute-start.6 = (bf16[64,2,1024]{2,1,0:T(2,128)(2,1)S(1)}, bf16[64,2,1024]{2,1,0:T(2,128)(2,1)S(1)}, u32[]{:S(2)}, u32[]{:S(2)}) collective-permute-start(bf16[64,2,1024]{2,1,0:T(2,128)(2,1)S(1)} %get-tuple-element.180), channel_id=1, source_target_pairs={{0,1},{1,2},{2,3},{3,4},{4,5},{5,6},{6,7},{7,8},{8,9},{9,10},{10,1... | collective-permute-start | bytes 786440 | tf_op jit(solution)/shard_map/ppermute | solution.py:31
  24.2 0.7 convert_element_type.15
  24.8 0.1 slice.338
  24.9 0.1 convert_reduce_fusion
  25.0 0.1 fusion.18
  25.1 0.7 select_reduce_fusion
  25.7 0.6 slice_subtract_fusion
  26.3 1.5 fusion.23
  27.8 0.6 fusion.27
  28.5 0.1 copy.10
  28.6 0.1 min.22
  28.7 0.6 pad_clamp_fusion
  29.3 0.7 convert_multiply_fusion
  30.0 0.6 slice_multiply_fusion
  30.6 0.6 fusion.26
  31.2 1.1 select_bitcast_fusion
  32.3 0.7 scatter-mul.4
  33.0 0.7 subtract_divide_fusion
  33.7 0.1 add_convert_fusion.refs_1_
  33.8 1.4 gather_fusion
  35.2 1.4 gather_fusion.1
  36.6 1.4 gather_fusion.2
  38.0 1.4 gather_fusion.3
  39.5 0.9 gather_fusion.4
  40.4 0.9 gather_fusion.5
  41.2 0.9 gather_fusion.6
  42.1 0.9 gather_fusion.7
  43.0 0.9 gather_fusion.8
  43.9 0.6 scatter.44
  44.5 0.6 scatter.40
  45.1 0.7 scatter.45
  45.8 0.8 scatter.46
  46.6 0.8 scatter.49
  47.4 0.8 scatter.50
  48.2 0.2 scatter.51
  48.4 0.2 scatter.54
  48.6 0.2 scatter.55
  48.8 0.1 pad.63.clone
  48.9 0.1 scatter.56
  49.1 0.2 scatter.59
  49.3 2.0 %scatter.41.refs_0_ = f32[8,128]{1,0:T(8,128)S(1)} dynamic-update-slice(f32[8,128]{1,0:T(8,128)S(1)} %scatter.40, f32[1,1]{1,0:T(1,128)} %bitcast.1, s32[]{:T(128)} %bitcast.2, s32[]{:T(128)} %bitcast.3) | dynamic-update-slice | bytes 12 | tf_op jit(solution)/shard_map/scatter | solution.py:124
  51.2 0.0 collective-permute-done.2
  51.2 1.3 collective-permute-start.7
  52.5 0.7 constant_dynamic-update-slice_fusion.3
  53.2 0.0 collective-permute-done.5
  53.2 3.4 %collective-permute-start = (bf16[2,16,1024]{2,1,0:T(8,128)(2,1)}, bf16[2,16,1024]{2,1,0:T(8,128)(2,1)S(1)}, u32[]{:S(2)}, u32[]{:S(2)}) collective-permute-start(bf16[2,16,1024]{2,1,0:T(8,128)(2,1)} %get-tuple-element.173), channel_id=1, source_target_pairs={{0,32},{32,64},{64,96},{96,128},{128,160},{160,192},{192,224},{1,3... | collective-permute-start | bytes 196616 | tf_op jit(solution)/shard_map/ppermute | solution.py:31
  56.6 0.7 constant_dynamic-update-slice_fusion.8
  57.3 1.3 collective-permute-start.1
  58.6 0.2 constant_dynamic-update-slice_fusion.2
  58.8 0.0 collective-permute-done.4
  58.8 0.7 constant_dynamic-update-slice_fusion.1
  59.5 0.2 constant_dynamic-update-slice_fusion.7
  59.7 0.0 collective-permute-done.7
  59.8 1.6 %collective-permute-done.1 = bf16[2,16,1024]{2,1,0:T(8,128)(2,1)S(1)} collective-permute-done((bf16[2,16,1024]{2,1,0:T(8,128)(2,1)S(1)}, bf16[2,16,1024]{2,1,0:T(8,128)(2,1)S(1)}, u32[]{:S(2)}, u32[]{:S(2)}) %collective-permute-start.1) | collective-permute-done | bytes 65568 | tf_op jit(solution)/shard_map/ppermute | solution.py:31
  61.4 3.5 %maximum_convert_fusion.refs_3_ = f32[68,24,1024]{2,1,0:T(8,128)} fusion(bf16[68,2,1024]{2,1,0:T(2,128)(2,1)S(1)} %constant_dynamic-update-slice_fusion.5, bf16[68,2,1024]{2,1,0:T(2,128)(2,1)S(1)} %constant_dynamic-update-slice_fusion, bf16[2,16,1024]{2,1,0:T(8,128)(2,1)S(1)} %collective-permute-done.1, bf16[64,16,1024]{2,1,0:T(8,128)(2,1)S(1)} %copy-done, ...), kind=kLoop, calls=%fused_computation.9 | loop fusion | flops 20054016 | bytes 9470000 | tf_op jit(solution)/shard_map/convert_element_type | solution.py:57
  64.9 72.5 %shard_map.37 = (f32[3,16,1024]{2,1,0:T(8,128)S(1)}, f32[16,1024]{1,0:T(8,128)S(1)}) custom-call(f32[8,128]{1,0:T(8,128)S(1)} %scatter.41.refs_0_, s32[4]{0:T(128)S(1)} %add_convert_fusion.refs_1_, f32[10,8,128]{2,1,0:T(8,128)S(1)} %broadcast_in_dim.23.refs_2_, f32[68,24,1024]{2,1,0:T(8,128)} %maximum_convert_fusion.refs_3_), custom_call_target="tpu_custom_call" | custom-call | tf_op jit(solution)/shard_map/pallas_call | solution.py:214
  137.5 13.8 %all_to_all.5 = f32[8,4,16,128]{3,2,1,0:T(8,128)S(1)} all-to-all(f32[8,4,16,128]{3,2,1,0:T(8,128)S(1)} %maximum_bitcast_fusion), channel_id=1, replica_groups=mesh['depth'=8,'tile'=32] {'depth'}, dimensions={0} | all-to-all | bytes 524288 | tf_op jit(solution)/shard_map/all_to_all | solution.py:249
  151.4 0.6 pad_maximum_fusion
  (27 shorter events, 0.2 us)
Async XLA Ops:
  0.0 61.4 %copy-start = (bf16[64,16,1024]{2,1,0:T(8,128)(2,1)S(1)}, bf16[64,16,1024]{2,1,0:T(8,128)(2,1)}, u32[]{:S(2)}) copy-start(bf16[64,16,1024]{2,1,0:T(8,128)(2,1)} %param.29) | copy-start | bytes 6291460
  1.5 49.7 %collective-permute-start.2 = (bf16[1,1,1024]{2,1,0:T(2,128)(2,1)}, bf16[1,1,1024]{2,1,0:T(2,128)(2,1)}, u32[]{:S(2)}, u32[]{:S(2)}) collective-permute-start(bf16[1,1,1024]{2,1,0:T(2,128)(2,1)} %get-tuple-element.177), channel_id=1, source_target_pairs={{1,32},{2,33},{3,34},{4,35},{5,36},{6,37},{7,38},{8,39},{9,40},{10... | collective-permute-start | bytes 6152 | tf_op jit(solution)/shard_map/ppermute | solution.py:31
  12.2 45.1 %collective-permute-start.3 = (bf16[64,2,1024]{2,1,0:T(2,128)(2,1)}, bf16[64,2,1024]{2,1,0:T(2,128)(2,1)S(1)}, u32[]{:S(2)}, u32[]{:S(2)}) collective-permute-start(bf16[64,2,1024]{2,1,0:T(2,128)(2,1)} %get-tuple-element.179), channel_id=1, source_target_pairs={{1,0},{2,1},{3,2},{4,3},{5,4},{6,5},{7,6},{8,7},{9,8},{10,9},{11,1... | collective-permute-start | bytes 786440 | tf_op jit(solution)/shard_map/ppermute | solution.py:31
  15.1 43.7 %collective-permute-start.4 = (bf16[1,1,1024]{2,1,0:T(2,128)(2,1)}, bf16[1,1,1024]{2,1,0:T(2,128)(2,1)}, u32[]{:S(2)}, u32[]{:S(2)}) collective-permute-start(bf16[1,1,1024]{2,1,0:T(2,128)(2,1)} %get-tuple-element.175), channel_id=1, source_target_pairs={{33,0},{34,1},{35,2},{36,3},{37,4},{38,5},{39,6},{40,7},{41,8},{42... | collective-permute-start | bytes 6152 | tf_op jit(solution)/shard_map/ppermute | solution.py:31
  16.4 36.8 %collective-permute-start.5 = (bf16[1,1,1024]{2,1,0:T(2,128)(2,1)}, bf16[1,1,1024]{2,1,0:T(2,128)(2,1)}, u32[]{:S(2)}, u32[]{:S(2)}) collective-permute-start(bf16[1,1,1024]{2,1,0:T(2,128)(2,1)} %get-tuple-element.176), channel_id=1, source_target_pairs={{0,33},{1,34},{2,35},{3,36},{4,37},{5,38},{6,39},{7,40},{8,41},{9,... | collective-permute-start | bytes 6152 | tf_op jit(solution)/shard_map/ppermute | solution.py:31
  21.2 38.3 %collective-permute-start.6 = (bf16[64,2,1024]{2,1,0:T(2,128)(2,1)S(1)}, bf16[64,2,1024]{2,1,0:T(2,128)(2,1)S(1)}, u32[]{:S(2)}, u32[]{:S(2)}) collective-permute-start(bf16[64,2,1024]{2,1,0:T(2,128)(2,1)S(1)} %get-tuple-element.180), channel_id=1, source_target_pairs={{0,1},{1,2},{2,3},{3,4},{4,5},{5,6},{6,7},{7,8},{8,9},{9,10},{10,1... | collective-permute-start | bytes 786440 | tf_op jit(solution)/shard_map/ppermute | solution.py:31
  51.2 8.5 %collective-permute-start.7 = (bf16[1,1,1024]{2,1,0:T(2,128)(2,1)}, bf16[1,1,1024]{2,1,0:T(2,128)(2,1)S(1)}, u32[]{:S(2)}, u32[]{:S(2)}) collective-permute-start(bf16[1,1,1024]{2,1,0:T(2,128)(2,1)} %get-tuple-element.178), channel_id=1, source_target_pairs={{32,1},{33,2},{34,3},{35,4},{36,5},{37,6},{38,7},{39,8},{40,9},{41... | collective-permute-start | bytes 6152 | tf_op jit(solution)/shard_map/ppermute | solution.py:31
  53.2 6.5 %collective-permute-start = (bf16[2,16,1024]{2,1,0:T(8,128)(2,1)}, bf16[2,16,1024]{2,1,0:T(8,128)(2,1)S(1)}, u32[]{:S(2)}, u32[]{:S(2)}) collective-permute-start(bf16[2,16,1024]{2,1,0:T(8,128)(2,1)} %get-tuple-element.173), channel_id=1, source_target_pairs={{0,32},{32,64},{64,96},{96,128},{128,160},{160,192},{192,224},{1,3... | collective-permute-start | bytes 196616 | tf_op jit(solution)/shard_map/ppermute | solution.py:31
  57.3 4.1 %collective-permute-start.1 = (bf16[2,16,1024]{2,1,0:T(8,128)(2,1)S(1)}, bf16[2,16,1024]{2,1,0:T(8,128)(2,1)S(1)}, u32[]{:S(2)}, u32[]{:S(2)}) collective-permute-start(bf16[2,16,1024]{2,1,0:T(8,128)(2,1)S(1)} %get-tuple-element.174), channel_id=1, source_target_pairs={{32,0},{64,32},{96,64},{128,96},{160,128},{192,160},{224,192},{33,... | collective-permute-start | bytes 196616 | tf_op jit(solution)/shard_map/ppermute | solution.py:31

commit v5 on v3

--- a/solution.py
+++ b/solution.py
@@ -33,28 +33,13 @@
 
 def extended_volume(volume):
     depth, rows, width = volume.shape
-    dz = ("depth",)
-    tx = ("tile",)
-    both = ("depth", "tile")
-    z_low = shifted(volume[depth - 2:], dz, (1,))
-    z_high = shifted(volume[:2], dz, (-1,))
-    x_low = shifted(volume[:, rows - 2:], tx, (1,))
-    x_high = shifted(volume[:, :2], tx, (-1,))
-    c_ll = shifted(volume[depth - 1:, rows - 1:], both, (1, 1))
-    c_lh = shifted(volume[depth - 1:, :1], both, (1, -1))
-    c_hl = shifted(volume[:1, rows - 1:], both, (-1, 1))
-    c_hh = shifted(volume[:1, :1], both, (-1, -1))
-    zero1 = jnp.zeros((1, 1, width), volume.dtype)
-    zero2 = jnp.zeros((2, 2, width), volume.dtype)
-    left = jnp.concatenate(
-        [zero2[:1], jnp.concatenate([zero1, c_ll], 1), x_low,
-         jnp.concatenate([zero1, c_hl], 1), zero2[:1]], axis=0)
-    right = jnp.concatenate(
-        [zero2[:1], jnp.concatenate([c_lh, zero1], 1), x_high,
-         jnp.concatenate([c_hh, zero1], 1), zero2[:1]], axis=0)
+    z_low = shifted(volume[depth - 2:], ("depth",), (1,))
+    z_high = shifted(volume[:2], ("depth",), (-1,))
     middle = jnp.concatenate([z_low, volume, z_high], axis=0)
+    x_low = shifted(middle[:, rows - 2:], ("tile",), (1,))
+    x_high = shifted(middle[:, :2], ("tile",), (-1,))
     gap = jnp.zeros((depth + 4, 4, width), volume.dtype)
-    return jnp.concatenate([middle, right, gap, left], axis=1).astype(jnp.float32)
+    return jnp.concatenate([middle, x_high, gap, x_low], axis=1).astype(jnp.float32)
 
 
 def inside_mask(depth_len, rows):
@@ -104,18 +89,15 @@
 def ramp_table(knot_pos, knot_color, sigma_scale):
     knot_float = knot_pos.astype(jnp.float32)
     palette = knot_color.astype(jnp.float32) / 255.0
-    palette = palette.at[3].multiply(sigma_scale)
+    palette = palette * jnp.array([1.0, 1.0, 1.0, sigma_scale], jnp.float32)[:, None]
     gaps = knot_float[1:] - knot_float[:-1]
     slopes = (palette[:, 1:] - palette[:, :-1]) / gaps[None]
-    count = knot_pos.shape[0] - 1
-    table = jnp.zeros((8, 128), jnp.float32)
-    table = table.at[0, :count].set(knot_float[:-1])
-    table = table.at[1, :count].set(gaps)
-    table = table.at[2:6, :count].set(slopes)
-    table = table.at[6, :4].set(palette[:, 0])
-    table = table.at[7, 0].set(knot_float[0])
-    table = table.at[7, 1].set(knot_float[-1])
-    return table
+    count = knot_pos.shape[0]
+    pad = lambda v: jnp.pad(v, (0, count - v.shape[0]))
+    bounds = jnp.stack([knot_float[0], knot_float[-1]])
+    rows = [knot_float, pad(gaps)] + [pad(slopes[c]) for c in range(4)]
+    rows += [pad(palette[:, 0]), pad(bounds)]
+    return jnp.stack(rows)
 
 
 def render_kernel(table, flags, planes_ref, color_ref, depth_ref, smooth_ref, square_ref, facing_ref,

time: 101 us -> 91.6 us (0.907)
  starting transfers between devices: 25.8 us -> 12.9 us
  waiting for transfers between devices: 2.33 us -> 8.99 us
  local copies, waits for them, and re-layouts: 7.17 us -> 4.09 us
    ppermute x8 -> x4, starting transfers between devices: 25.8 us -> 12.9 us  [shifted(): return lax.ppermute(block, axes if len(axes) > 1 else axes[0], pairs)]
    ppermute x8 -> x4, waiting for transfers between devices: 2.33 us -> 8.99 us  [shifted(): return lax.ppermute(block, axes if len(axes) > 1 else axes[0], pairs)]
    slice x5 -> x4, local copies, waits for them, and re-layouts: 4.36 us -> 2.07 us  [the longest x1 0.88 us: extended_volume(): z_high = shifted(volume[:2], ('depth',), (-1,))]
    scatter x6 -> x0, local copies, waits for them, and re-layouts: 2.15 us -> none  [the longest x1 0.78 us: ramp_table(): table = table.at[7, 1].set(knot_float[-1])]
    unnamed x9 -> x3, local copies, waits for them, and re-layouts: 0.49 us -> 1.87 us
    convert_element_type x1, other arithmetic: 4.77 us -> 3.47 us  [extended_volume(): jnp.concatenate([middle, x_high, gap, x_low], axis=1).astype(jnp.float32)]
    another operation x0 -> x1, other arithmetic: none -> 1.28 us  [ramp_table(): return jnp.stack(rows)]
  transfers between devices with their start and end apart: 8 -> 4, of which waited for: 2 -> 2; matrix products, arithmetic and copies ran while one was open for 8% -> 6% of each run, Pallas kernels for 0% -> 0%
where the time goes in v5:
time: 91.6 us; the launch traced here: 91.2 us
  Pallas kernels  44.4 us (48%)
  blocking collectives  13.6 us (15%)
  starting transfers between devices  12.9 us (14%)
  waiting for transfers between devices  8.99 us (10%)
  other arithmetic  7.09 us (8%)
  local copies, waits for them, and re-layouts  4.09 us (4%)
    pallas_call x1, Pallas kernels, render_block(): pl.pallas_call(kernel, in_specs=[pl.BlockSpec(memory_space=pltpu.SMEM), p...  44.4 us
    all_to_all x1, blocking collectives, body(): blocks = lax.all_to_all(weighted, 'depth', 0, 0, tiled=True)  13.6 us
    ppermute x4, starting transfers between devices, shifted(): return lax.ppermute(block, axes if len(axes) > 1 else axes[0], pairs)  12.9 us
    ppermute x4, waiting for transfers between devices, shifted(): return lax.ppermute(block, axes if len(axes) > 1 else axes[0], pairs)  8.99 us
    convert_element_type x1, other arithmetic, extended_volume(): jnp.concatenate([middle, x_high, gap, x_low], axis=1).astype(jnp.float32)  3.47 us
    unnamed x3, local copies, waits for them, and re-layouts  1.87 us
  transfers between devices with their start and end apart: 4, of which 2 were waited for; matrix products, arithmetic and copies ran while one was open for 6% of the time, Pallas kernels for 0%

profile of v5, /device:TPU:24, one launch (start us, length us, event | category | flops | bytes accessed | tf_op | source)
XLA Modules:
  0.0 91.2 jit_solution(5733286769629613550)
XLA Ops:
  0.0 0.9 fusion.21
  0.9 1.7 %collective-permute-start = (bf16[2,16,1024]{2,1,0:T(8,128)(2,1)S(1)}, bf16[2,16,1024]{2,1,0:T(8,128)(2,1)S(1)}, u32[]{:S(2)}, u32[]{:S(2)}) collective-permute-start(bf16[2,16,1024]{2,1,0:T(8,128)(2,1)S(1)} %get-tuple-element.16), channel_id=1, source_target_pairs={{0,32},{32,64},{64,96},{96,128},{128,160},{160,192},{192,224},{1,3... | collective-permute-start | bytes 196616 | tf_op jit(solution)/shard_map/ppermute | solution.py:31
  2.6 1.3 %collective-permute-start.1 = (bf16[2,16,1024]{2,1,0:T(8,128)(2,1)S(1)}, bf16[2,16,1024]{2,1,0:T(8,128)(2,1)S(1)}, u32[]{:S(2)}, u32[]{:S(2)}) collective-permute-start(bf16[2,16,1024]{2,1,0:T(8,128)(2,1)S(1)} %get-tuple-element.15), channel_id=1, source_target_pairs={{32,0},{64,32},{96,64},{128,96},{160,128},{192,160},{224,192},{33,... | collective-permute-start | bytes 196616 | tf_op jit(solution)/shard_map/ppermute | solution.py:31
  3.9 0.7 fusion.23
  4.6 0.1 slice_subtract_fusion
  4.7 0.6 fusion.22
  5.3 0.8 convert_multiply_fusion
  6.0 0.1 slice_reduce_fusion
  6.1 0.1 subtract_divide_fusion
  6.2 0.0 collective-permute-done
  6.2 1.8 %constant_dynamic-update-slice_fusion.1 = bf16[68,16,1024]{2,1,0:T(8,128)(2,1)S(1)} fusion(bf16[68,16,1024]{2,1,0:T(8,128)(2,1)S(1)} %constant_dynamic-update-slice_fusion.2, bf16[64,16,1024]{2,1,0:T(8,128)(2,1)} %param.4), kind=kLoop, calls=%fused_computation.38 | loop fusion | bytes 4194304
  8.1 0.0 collective-permute-done.1
  8.1 0.5 fusion.20
  8.6 7.9 %collective-permute-start.2 = (bf16[68,2,1024]{2,1,0:T(2,128)(2,1)S(1)}, bf16[68,2,1024]{2,1,0:T(2,128)(2,1)S(1)}, u32[]{:S(2)}, u32[]{:S(2)}) collective-permute-start(bf16[68,2,1024]{2,1,0:T(2,128)(2,1)S(1)} %get-tuple-element.13), channel_id=1, source_target_pairs={{1,0},{2,1},{3,2},{4,3},{5,4},{6,5},{7,6},{8,7},{9,8},{10,9},{11,1... | collective-permute-start | bytes 835592 | tf_op jit(solution)/shard_map/ppermute | solution.py:31
  16.6 1.9 %collective-permute-start.3 = (bf16[68,2,1024]{2,1,0:T(2,128)(2,1)S(1)}, bf16[68,2,1024]{2,1,0:T(2,128)(2,1)S(1)}, u32[]{:S(2)}, u32[]{:S(2)}) collective-permute-start(bf16[68,2,1024]{2,1,0:T(2,128)(2,1)S(1)} %get-tuple-element.14), channel_id=1, source_target_pairs={{0,1},{1,2},{2,3},{3,4},{4,5},{5,6},{6,7},{7,8},{8,9},{9,10},{10,1... | collective-permute-start | bytes 835592 | tf_op jit(solution)/shard_map/ppermute | solution.py:31
  18.5 1.3 %fusion.19 = f32[1,16]{1,0:T(1,128)S(1)} fusion(f32[1]{0:T(128)} %get-tuple-element.28, f32[1]{0:T(128)} %get-tuple-element.27), kind=kLoop, calls=%fused_computation.65 | loop fusion | flops 64 | bytes 72 | tf_op jit(solution)/shard_map/stack | solution.py:100
  19.8 0.1 pad.37.clone
  19.9 0.1 add_convert_fusion.refs_1_
  20.0 2.2 %collective-permute-done.2 = bf16[68,2,1024]{2,1,0:T(2,128)(2,1)S(1)} collective-permute-done((bf16[68,2,1024]{2,1,0:T(2,128)(2,1)S(1)}, bf16[68,2,1024]{2,1,0:T(2,128)(2,1)S(1)}, u32[]{:S(2)}, u32[]{:S(2)}) %collective-permute-start.2) | collective-permute-done | bytes 278560 | tf_op jit(solution)/shard_map/ppermute | solution.py:31
  22.2 6.8 %collective-permute-done.3 = bf16[68,2,1024]{2,1,0:T(2,128)(2,1)S(1)} collective-permute-done((bf16[68,2,1024]{2,1,0:T(2,128)(2,1)S(1)}, bf16[68,2,1024]{2,1,0:T(2,128)(2,1)S(1)}, u32[]{:S(2)}, u32[]{:S(2)}) %collective-permute-start.3) | collective-permute-done | bytes 278560 | tf_op jit(solution)/shard_map/ppermute | solution.py:31
  29.0 3.5 %maximum_convert_fusion.refs_2_ = f32[68,24,1024]{2,1,0:T(8,128)} fusion(bf16[68,2,1024]{2,1,0:T(2,128)(2,1)S(1)} %collective-permute-done.3, bf16[68,2,1024]{2,1,0:T(2,128)(2,1)S(1)} %collective-permute-done.2, bf16[68,16,1024]{2,1,0:T(8,128)(2,1)S(1)} %constant_dynamic-update-slice_fusion, bf16[24]{0:T(256)(128)(2,1)S(1)} %pad.37.clone), kind=kLoop, calls=%fused_computation | loop fusion | flops 13369344 | bytes 9470000 | tf_op jit(solution)/shard_map/convert_element_type | solution.py:42
  32.4 44.4 %shard_map.46 = (f32[3,16,1024]{2,1,0:T(8,128)S(1)}, f32[16,1024]{1,0:T(8,128)S(1)}) custom-call(f32[8,16]{1,0:T(8,128)S(1)} %stack.54.refs_0_, s32[4]{0:T(128)S(1)} %add_convert_fusion.refs_1_, f32[68,24,1024]{2,1,0:T(8,128)} %maximum_convert_fusion.refs_2_), custom_call_target="tpu_custom_call" | custom-call | tf_op jit(solution)/shard_map/pallas_call | solution.py:186
  76.9 13.6 %all_to_all.5 = f32[8,4,16,128]{3,2,1,0:T(8,128)S(1)} all-to-all(f32[8,4,16,128]{3,2,1,0:T(8,128)S(1)} %maximum_bitcast_fusion), channel_id=1, replica_groups=mesh['depth'=8,'tile'=32] {'depth'}, dimensions={0} | all-to-all | bytes 524288 | tf_op jit(solution)/shard_map/all_to_all | solution.py:220
  90.6 0.6 pad_maximum_fusion
  (16 shorter events, 0.2 us)
Async XLA Ops:
  0.9 5.3 %collective-permute-start = (bf16[2,16,1024]{2,1,0:T(8,128)(2,1)S(1)}, bf16[2,16,1024]{2,1,0:T(8,128)(2,1)S(1)}, u32[]{:S(2)}, u32[]{:S(2)}) collective-permute-start(bf16[2,16,1024]{2,1,0:T(8,128)(2,1)S(1)} %get-tuple-element.16), channel_id=1, source_target_pairs={{0,32},{32,64},{64,96},{96,128},{128,160},{160,192},{192,224},{1,3... | collective-permute-start | bytes 196616 | tf_op jit(solution)/shard_map/ppermute | solution.py:31
  2.6 5.5 %collective-permute-start.1 = (bf16[2,16,1024]{2,1,0:T(8,128)(2,1)S(1)}, bf16[2,16,1024]{2,1,0:T(8,128)(2,1)S(1)}, u32[]{:S(2)}, u32[]{:S(2)}) collective-permute-start(bf16[2,16,1024]{2,1,0:T(8,128)(2,1)S(1)} %get-tuple-element.15), channel_id=1, source_target_pairs={{32,0},{64,32},{96,64},{128,96},{160,128},{192,160},{224,192},{33,... | collective-permute-start | bytes 196616 | tf_op jit(solution)/shard_map/ppermute | solution.py:31
  8.6 13.5 %collective-permute-start.2 = (bf16[68,2,1024]{2,1,0:T(2,128)(2,1)S(1)}, bf16[68,2,1024]{2,1,0:T(2,128)(2,1)S(1)}, u32[]{:S(2)}, u32[]{:S(2)}) collective-permute-start(bf16[68,2,1024]{2,1,0:T(2,128)(2,1)S(1)} %get-tuple-element.13), channel_id=1, source_target_pairs={{1,0},{2,1},{3,2},{4,3},{5,4},{6,5},{7,6},{8,7},{9,8},{10,9},{11,1... | collective-permute-start | bytes 835592 | tf_op jit(solution)/shard_map/ppermute | solution.py:31
  16.6 12.4 %collective-permute-start.3 = (bf16[68,2,1024]{2,1,0:T(2,128)(2,1)S(1)}, bf16[68,2,1024]{2,1,0:T(2,128)(2,1)S(1)}, u32[]{:S(2)}, u32[]{:S(2)}) collective-permute-start(bf16[68,2,1024]{2,1,0:T(2,128)(2,1)S(1)} %get-tuple-element.14), channel_id=1, source_target_pairs={{0,1},{1,2},{2,3},{3,4},{4,5},{5,6},{6,7},{7,8},{8,9},{9,10},{10,1... | collective-permute-start | bytes 835592 | tf_op jit(solution)/shard_map/ppermute | solution.py:31

commit v6 on v5

--- a/solution.py
+++ b/solution.py
@@ -35,9 +35,10 @@
     depth, rows, width = volume.shape
     z_low = shifted(volume[depth - 2:], ("depth",), (1,))
     z_high = shifted(volume[:2], ("depth",), (-1,))
+    edge = lambda a, b: jnp.concatenate([z_low[:, a:b], volume[:, a:b], z_high[:, a:b]], axis=0)
+    x_low = shifted(edge(rows - 2, rows), ("tile",), (1,))
+    x_high = shifted(edge(0, 2), ("tile",), (-1,))
     middle = jnp.concatenate([z_low, volume, z_high], axis=0)
-    x_low = shifted(middle[:, rows - 2:], ("tile",), (1,))
-    x_high = shifted(middle[:, :2], ("tile",), (-1,))
     gap = jnp.zeros((depth + 4, 4, width), volume.dtype)
     return jnp.concatenate([middle, x_high, gap, x_low], axis=1).astype(jnp.float32)
 
@@ -92,11 +93,12 @@
     palette = palette * jnp.array([1.0, 1.0, 1.0, sigma_scale], jnp.float32)[:, None]
     gaps = knot_float[1:] - knot_float[:-1]
     slopes = (palette[:, 1:] - palette[:, :-1]) / gaps[None]
+    offsets = palette[:, :-1] - slopes * knot_float[None, :-1]
     count = knot_pos.shape[0]
     pad = lambda v: jnp.pad(v, (0, count - v.shape[0]))
     bounds = jnp.stack([knot_float[0], knot_float[-1]])
-    rows = [knot_float, pad(gaps)] + [pad(slopes[c]) for c in range(4)]
-    rows += [pad(palette[:, 0]), pad(bounds)]
+    rows = [knot_float] + [pad(offsets[c]) for c in range(4)] + [pad(slopes[c]) for c in range(4)]
+    rows += [pad(bounds)]
     return jnp.stack(rows)
 
 
@@ -139,11 +141,10 @@
     lax.fori_loop(0, count, smooth_plane, 0)
 
     knots = [table[0, k] for k in range(segments)]
-    gaps = [table[1, k] for k in range(segments)]
-    slopes = [[table[2 + c, k] for k in range(segments)] for c in range(4)]
-    base = [table[6, c] for c in range(4)]
-    lo = table[7, 0]
-    hi = table[7, 1]
+    offsets = [[table[1 + c, k] for k in range(segments)] for c in range(4)]
+    slopes = [[table[5 + c, k] for k in range(segments)] for c in range(4)]
+    lo = table[9, 0]
+    hi = table[9, 1]
     sub = 8
     for r0 in range(0, rows, sub):
         for c0 in range(0, lanes, width):
@@ -158,10 +159,13 @@
                 norm = slope_z * slope_z + square_ref[z + 1, rs, cs] + 0.1
                 shade = 0.3 + 0.7 * facing * lax.rsqrt(norm)
                 lookup = jnp.clip(127.5 + 70.0 * center, lo, hi)
-                chan = [jnp.full_like(lookup, base[c]) for c in range(4)]
-                for k in range(segments):
-                    t = jnp.minimum(jnp.maximum(lookup - knots[k], 0.0), gaps[k])
-                    chan = [chan[c] + t * slopes[c][k] for c in range(4)]
+                offset = [jnp.full_like(lookup, offsets[c][0]) for c in range(4)]
+                slope = [jnp.full_like(lookup, slopes[c][0]) for c in range(4)]
+                for k in range(1, segments):
+                    above = lookup >= knots[k]
+                    offset = [jnp.where(above, offsets[c][k], offset[c]) for c in range(4)]
+                    slope = [jnp.where(above, slopes[c][k], slope[c]) for c in range(4)]
+                chan = [offset[c] + slope[c] * lookup for c in range(4)]
                 ext = chan[3]
                 fade = jnp.exp(-ext)
                 weight = shade * (1.0 - fade) * trans

time: 91.6 us -> 89.7 us (0.979)
  Pallas kernels: 44.4 us -> 40.6 us
  other arithmetic: 7.09 us -> 9.28 us
    pallas_call x1, Pallas kernels: 44.4 us -> 40.6 us  [render_block(): pl.pallas_call(kernel, in_specs=[pl.BlockSpec(memory_space=pltpu.SMEM), p...]
    unnamed x3 -> x1, local copies, waits for them, and re-layouts: 1.87 us -> 0.01 us
    slice x3 -> x4, local copies, waits for them, and re-layouts: 1.48 us -> 2.91 us  [the longest x1 1.99 us: extended_volume(): volume[:, a:b]]
    convert_element_type x1, other arithmetic: 3.47 us -> 4.78 us  [extended_volume(): jnp.concatenate([middle, x_high, gap, x_low], axis=1).astype(jnp.float32)]
  transfers between devices with their start and end apart: 4 -> 4, of which waited for: 2 -> 2; matrix products, arithmetic and copies ran while one was open for 6% -> 7% of each run, Pallas kernels for 0% -> 0%
where the time goes in v6:
time: 89.7 us; the launch traced here: 89.3 us
  Pallas kernels  40.6 us (45%)
  blocking collectives  13.6 us (15%)
  starting transfers between devices  12.9 us (14%)
  other arithmetic  9.28 us (10%)
  waiting for transfers between devices  8.87 us (10%)
  local copies, waits for them, and re-layouts  3.72 us (4%)
    pallas_call x1, Pallas kernels, render_block(): pl.pallas_call(kernel, in_specs=[pl.BlockSpec(memory_space=pltpu.SMEM), p...  40.6 us
    all_to_all x1, blocking collectives, body(): blocks = lax.all_to_all(weighted, 'depth', 0, 0, tiled=True)  13.6 us
    ppermute x4, starting transfers between devices, shifted(): return lax.ppermute(block, axes if len(axes) > 1 else axes[0], pairs)  12.9 us
    ppermute x4, waiting for transfers between devices, shifted(): return lax.ppermute(block, axes if len(axes) > 1 else axes[0], pairs)  8.87 us
    convert_element_type x1, other arithmetic, extended_volume(): jnp.concatenate([middle, x_high, gap, x_low], axis=1).astype(jnp.float32)  4.78 us
    slice x1, local copies, waits for them, and re-layouts, extended_volume(): volume[:, a:b]  1.99 us
  transfers between devices with their start and end apart: 4, of which 2 were waited for; matrix products, arithmetic and copies ran while one was open for 7% of the time, Pallas kernels for 0%

profile of v6, /device:TPU:24, one launch (start us, length us, event | category | flops | bytes accessed | tf_op | source)
XLA Modules:
  0.0 89.3 jit_solution(15198610348100868026)
XLA Ops:
  0.0 0.9 fusion.21
  0.9 1.7 %collective-permute-start = (bf16[2,16,1024]{2,1,0:T(8,128)(2,1)S(1)}, bf16[2,16,1024]{2,1,0:T(8,128)(2,1)S(1)}, u32[]{:S(2)}, u32[]{:S(2)}) collective-permute-start(bf16[2,16,1024]{2,1,0:T(8,128)(2,1)S(1)} %get-tuple-element.17), channel_id=1, source_target_pairs={{0,32},{32,64},{64,96},{96,128},{128,160},{160,192},{192,224},{1,3... | collective-permute-start | bytes 196616 | tf_op jit(solution)/shard_map/ppermute | solution.py:31
  2.6 1.3 %collective-permute-start.1 = (bf16[2,16,1024]{2,1,0:T(8,128)(2,1)S(1)}, bf16[2,16,1024]{2,1,0:T(8,128)(2,1)S(1)}, u32[]{:S(2)}, u32[]{:S(2)}) collective-permute-start(bf16[2,16,1024]{2,1,0:T(8,128)(2,1)S(1)} %get-tuple-element.18), channel_id=1, source_target_pairs={{32,0},{64,32},{96,64},{128,96},{160,128},{192,160},{224,192},{33,... | collective-permute-start | bytes 196616 | tf_op jit(solution)/shard_map/ppermute | solution.py:31
  3.9 0.7 fusion.25
  4.6 0.1 slice_subtract_fusion
  4.7 0.6 fusion.24
  5.3 2.0 %fusion.20 = (bf16[64,2,1024]{2,1,0:T(2,128)(2,1)S(1)}, bf16[64,2,1024]{2,1,0:T(2,128)(2,1)S(1)}) fusion(bf16[64,16,1024]{2,1,0:T(8,128)(2,1)} %param.4), kind=kLoop, calls=%fused_computation.72 | loop fusion | bytes 1048576 | tf_op jit(solution)/shard_map/slice | solution.py:38
  7.3 0.8 convert_multiply_fusion
  8.0 0.1 multiply_subtract_fusion
  8.2 0.0 collective-permute-done
  8.2 0.0 collective-permute-done.1
  8.3 0.4 pad_maximum_fusion
  8.7 7.9 %collective-permute-start.2 = (bf16[68,2,1024]{2,1,0:T(2,128)(2,1)S(1)}, bf16[68,2,1024]{2,1,0:T(2,128)(2,1)S(1)}, u32[]{:S(2)}, u32[]{:S(2)}) collective-permute-start(bf16[68,2,1024]{2,1,0:T(2,128)(2,1)S(1)} %pad_maximum_fusion), channel_id=1, source_target_pairs={{1,0},{2,1},{3,2},{4,3},{5,4},{6,5},{7,6},{8,7},{9,8},{10,9},{11,1... | collective-permute-start | bytes 835592 | tf_op jit(solution)/shard_map/ppermute | solution.py:31
  16.6 0.4 pad_maximum_fusion.1
  17.0 1.9 %collective-permute-start.3 = (bf16[68,2,1024]{2,1,0:T(2,128)(2,1)S(1)}, bf16[68,2,1024]{2,1,0:T(2,128)(2,1)S(1)}, u32[]{:S(2)}, u32[]{:S(2)}) collective-permute-start(bf16[68,2,1024]{2,1,0:T(2,128)(2,1)S(1)} %pad_maximum_fusion.1), channel_id=1, source_target_pairs={{0,1},{1,2},{2,3},{3,4},{4,5},{5,6},{6,7},{7,8},{8,9},{9,10},{10,1... | collective-permute-start | bytes 835592 | tf_op jit(solution)/shard_map/ppermute | solution.py:31
  19.0 0.1 pad.46.clone
  19.1 1.4 %fusion.19 = f32[1,16]{1,0:T(1,128)S(1)} fusion(f32[1]{0:T(128)} %get-tuple-element.38, f32[1]{0:T(128)} %get-tuple-element.37), kind=kLoop, calls=%fused_computation.70 | loop fusion | flops 64 | bytes 72 | tf_op jit(solution)/shard_map/stack | solution.py:102
  20.5 0.1 add_convert_fusion.refs_1_
  20.5 1.7 %collective-permute-done.2 = bf16[68,2,1024]{2,1,0:T(2,128)(2,1)S(1)} collective-permute-done((bf16[68,2,1024]{2,1,0:T(2,128)(2,1)S(1)}, bf16[68,2,1024]{2,1,0:T(2,128)(2,1)S(1)}, u32[]{:S(2)}, u32[]{:S(2)}) %collective-permute-start.2) | collective-permute-done | bytes 278560 | tf_op jit(solution)/shard_map/ppermute | solution.py:31
  22.2 7.2 %collective-permute-done.3 = bf16[68,2,1024]{2,1,0:T(2,128)(2,1)S(1)} collective-permute-done((bf16[68,2,1024]{2,1,0:T(2,128)(2,1)S(1)}, bf16[68,2,1024]{2,1,0:T(2,128)(2,1)S(1)}, u32[]{:S(2)}, u32[]{:S(2)}) %collective-permute-start.3) | collective-permute-done | bytes 278560 | tf_op jit(solution)/shard_map/ppermute | solution.py:31
  29.4 4.8 %maximum_convert_fusion.refs_2_ = f32[68,24,1024]{2,1,0:T(8,128)} fusion(bf16[68,2,1024]{2,1,0:T(2,128)(2,1)S(1)} %collective-permute-done.3, bf16[68,2,1024]{2,1,0:T(2,128)(2,1)S(1)} %collective-permute-done.2, bf16[2,16,1024]{2,1,0:T(8,128)(2,1)S(1)} %collective-permute-done.1, bf16[64,16,1024]{2,1,0:T(8,128)(2,1)} %param.4, ...), kind=kLoop, calls=%fused_computation | loop fusion | flops 20054016 | bytes 9470000 | tf_op jit(solution)/shard_map/convert_element_type | solution.py:43
  34.2 40.6 %shard_map.46 = (f32[3,16,1024]{2,1,0:T(8,128)S(1)}, f32[16,1024]{1,0:T(8,128)S(1)}) custom-call(f32[10,16]{1,0:T(8,128)S(1)} %stack.62.refs_0_, s32[4]{0:T(128)S(1)} %add_convert_fusion.refs_1_, f32[68,24,1024]{2,1,0:T(8,128)} %maximum_convert_fusion.refs_2_), custom_call_target="tpu_custom_call" | custom-call | tf_op jit(solution)/shard_map/pallas_call | solution.py:190
  74.9 13.6 %all_to_all.5 = f32[8,4,16,128]{3,2,1,0:T(8,128)S(1)} all-to-all(f32[8,4,16,128]{3,2,1,0:T(8,128)S(1)} %maximum_bitcast_fusion), channel_id=1, replica_groups=mesh['depth'=8,'tile'=32] {'depth'}, dimensions={0} | all-to-all | bytes 524288 | tf_op jit(solution)/shard_map/all_to_all | solution.py:224
  88.6 0.6 pad_maximum_fusion.2
  (21 shorter events, 0.2 us)
Async XLA Ops:
  0.9 7.3 %collective-permute-start = (bf16[2,16,1024]{2,1,0:T(8,128)(2,1)S(1)}, bf16[2,16,1024]{2,1,0:T(8,128)(2,1)S(1)}, u32[]{:S(2)}, u32[]{:S(2)}) collective-permute-start(bf16[2,16,1024]{2,1,0:T(8,128)(2,1)S(1)} %get-tuple-element.17), channel_id=1, source_target_pairs={{0,32},{32,64},{64,96},{96,128},{128,160},{160,192},{192,224},{1,3... | collective-permute-start | bytes 196616 | tf_op jit(solution)/shard_map/ppermute | solution.py:31
  2.6 5.6 %collective-permute-start.1 = (bf16[2,16,1024]{2,1,0:T(8,128)(2,1)S(1)}, bf16[2,16,1024]{2,1,0:T(8,128)(2,1)S(1)}, u32[]{:S(2)}, u32[]{:S(2)}) collective-permute-start(bf16[2,16,1024]{2,1,0:T(8,128)(2,1)S(1)} %get-tuple-element.18), channel_id=1, source_target_pairs={{32,0},{64,32},{96,64},{128,96},{160,128},{192,160},{224,192},{33,... | collective-permute-start | bytes 196616 | tf_op jit(solution)/shard_map/ppermute | solution.py:31
  8.7 13.5 %collective-permute-start.2 = (bf16[68,2,1024]{2,1,0:T(2,128)(2,1)S(1)}, bf16[68,2,1024]{2,1,0:T(2,128)(2,1)S(1)}, u32[]{:S(2)}, u32[]{:S(2)}) collective-permute-start(bf16[68,2,1024]{2,1,0:T(2,128)(2,1)S(1)} %pad_maximum_fusion), channel_id=1, source_target_pairs={{1,0},{2,1},{3,2},{4,3},{5,4},{6,5},{7,6},{8,7},{9,8},{10,9},{11,1... | collective-permute-start | bytes 835592 | tf_op jit(solution)/shard_map/ppermute | solution.py:31
  17.0 12.4 %collective-permute-start.3 = (bf16[68,2,1024]{2,1,0:T(2,128)(2,1)S(1)}, bf16[68,2,1024]{2,1,0:T(2,128)(2,1)S(1)}, u32[]{:S(2)}, u32[]{:S(2)}) collective-permute-start(bf16[68,2,1024]{2,1,0:T(2,128)(2,1)S(1)} %pad_maximum_fusion.1), channel_id=1, source_target_pairs={{0,1},{1,2},{2,3},{3,4},{4,5},{5,6},{6,7},{7,8},{8,9},{9,10},{10,1... | collective-permute-start | bytes 835592 | tf_op jit(solution)/shard_map/ppermute | solution.py:31

commit v7 on v0

v7 whole, which is shorter than its diff:
```python
import jax
import jax.numpy as jnp
from jax import lax
from jax.experimental import pallas as pl
from jax.experimental.pallas import tpu as pltpu
from jax.sharding import PartitionSpec as P

TALL = 24
EDGE = 2


def shifted(block, axis, move):
    size = lax.axis_size(axis)
    pairs = [(i, i + move) for i in range(size) if 0 <= i + move < size]
    return lax.ppermute(block, axis, pairs)


def ramp_table(knot_pos, knot_color, sigma_scale):
    knot_float = knot_pos.astype(jnp.float32)
    palette = knot_color.astype(jnp.float32) / 255.0
    palette = palette * jnp.array([1.0, 1.0, 1.0, sigma_scale], jnp.float32)[:, None]
    gaps = knot_float[1:] - knot_float[:-1]
    slopes = (palette[:, 1:] - palette[:, :-1]) / gaps[None]
    offsets = palette[:, :-1] - slopes * knot_float[None, :-1]
    count = knot_pos.shape[0]
    pad = lambda v: jnp.pad(v, (0, count - v.shape[0]))
    bounds = jnp.stack([knot_float[0], knot_float[-1]])
    rows = [knot_float] + [pad(offsets[c]) for c in range(4)] + [pad(slopes[c]) for c in range(4)]
    rows += [pad(bounds)]
    return jnp.stack(rows)


def y_prev(a):
    lane = lax.broadcasted_iota(jnp.int32, a.shape, 1)
    return jnp.where(lane == 0, 0.0, pltpu.roll(a, 1, 1))


def y_next(a):
    lane = lax.broadcasted_iota(jnp.int32, a.shape, 1)
    return jnp.where(lane == a.shape[1] - 1, 0.0, pltpu.roll(a, a.shape[1] - 1, 1))


def smooth_plane(low, mid, high, keep, rows):
    tall = mid.shape[0]
    near = low + high + pltpu.roll(mid, tall - 1, 0) + pltpu.roll(mid, 1, 0)
    near = near + y_prev(mid) + y_next(mid)
    smooth = jnp.where(keep, 0.4 * mid + 0.1 * near, 0.0)
    smooth = smooth.astype(jnp.bfloat16).astype(jnp.float32)
    center = smooth[:rows]
    slope_x = 0.5 * (pltpu.roll(smooth, tall - 1, 0)[:rows] - pltpu.roll(smooth, 1, 0)[:rows])
    slope_y = 0.5 * (y_next(center) - y_prev(center))
    return center, slope_x * slope_x + slope_y * slope_y, 0.8 * slope_x


class Palette:
    def __init__(self, table, segments):
        self.knots = [table[0, k] for k in range(segments)]
        self.offsets = [[table[1 + c, k] for k in range(segments)] for c in range(4)]
        self.slopes = [[table[5 + c, k] for k in range(segments)] for c in range(4)]
        self.lo = table[9, 0]
        self.hi = table[9, 1]
        self.segments = segments

    def cell(self, before, center, after, square, facing):
        slope_z = 0.5 * (after - before)
        facing = jnp.abs(0.6 * slope_z + facing)
        norm = slope_z * slope_z + square + 0.1
        shade = 0.3 + 0.7 * facing * lax.rsqrt(norm)
        lookup = jnp.clip(127.5 + 70.0 * center, self.lo, self.hi)
        offset = [jnp.full_like(lookup, self.offsets[c][0]) for c in range(4)]
        slope = [jnp.full_like(lookup, self.slopes[c][0]) for c in range(4)]
        for k in range(1, self.segments):
            above = lookup >= self.knots[k]
            offset = [jnp.where(above, self.offsets[c][k], offset[c]) for c in range(4)]
            slope = [jnp.where(above, self.slopes[c][k], slope[c]) for c in range(4)]
        chan = [offset[c] + slope[c] * lookup for c in range(4)]
        return shade, chan


def row_keep(flags, tall, lanes, rows):
    row = lax.broadcasted_iota(jnp.int32, (tall, lanes), 0)
    return ((row != tall - 1) | (flags[2] == 0)) & ((row != rows) | (flags[3] == 0))


def middle_kernel(table, flags, planes_ref, color_ref, depth_ref, trans_ref,
                  smooth_ref, square_ref, facing_ref, *, segments, rows, width):
    depth, tall, lanes = planes_ref.shape
    keep = row_keep(flags, tall, lanes, rows)

    def plane(i, carry):
        center, square, facing = smooth_plane(
            planes_ref[i - 1], planes_ref[i], planes_ref[i + 1], keep, rows)
        smooth_ref[i] = center
        square_ref[i] = square
        facing_ref[i] = facing
        return carry

    lax.fori_loop(1, depth - 1, plane, 0)
    palette = Palette(table, segments)
    sub = 8
    for r0 in range(0, rows, sub):
        for c0 in range(0, lanes, width):
            rs = pl.ds(r0, sub)
            cs = pl.ds(c0, width)

            def step(z, carry):
                trans, acc0, acc1, acc2, total = carry
                shade, chan = palette.cell(
                    smooth_ref[z - 1, rs, cs], smooth_ref[z, rs, cs], smooth_ref[z + 1, rs, cs],
                    square_ref[z, rs, cs], facing_ref[z, rs, cs])
                ext = chan[3]
                fade = jnp.exp(-ext)
                weight = shade * (1.0 - fade) * trans
                acc0 = acc0 + weight * chan[0]
                acc1 = acc1 + weight * chan[1]
                acc2 = acc2 + weight * chan[2]
                return (trans * fade, acc0, acc1, acc2, total + ext)

            zeros = jnp.zeros((sub, width), jnp.float32)
            init = (jnp.ones((sub, width), jnp.float32), zeros, zeros, zeros, zeros)
            trans, acc0, acc1, acc2, total = lax.fori_loop(
                EDGE, depth - EDGE, step, init, unroll=2)
            color_ref[0, rs, cs] = acc0
            color_ref[1, rs, cs] = acc1
            color_ref[2, rs, cs] = acc2
            depth_ref[rs, cs] = total
            trans_ref[rs, cs] = trans


def edge_kernel(table, flags, front_ref, back_ref, color_ref, depth_ref, trans_ref,
                out_color_ref, out_depth_ref, *, segments, rows):
    span, tall, lanes = front_ref.shape
    keep = row_keep(flags, tall, lanes, rows)
    palette = Palette(table, segments)

    def side(ref, outside):
        smoothed = []
        for i in range(1, span - 1):
            inside = keep & ~outside(i)
            smoothed.append(smooth_plane(ref[i - 1], ref[i], ref[i + 1], inside, rows))
        cells = []
        for j in range(1, len(smoothed) - 1):
            cells.append(palette.cell(smoothed[j - 1][0], smoothed[j][0], smoothed[j + 1][0],
                                      smoothed[j][1], smoothed[j][2]))
        return cells

    front = side(front_ref, lambda i: (i == 1) & (flags[0] == 1))
    back = side(back_ref, lambda i: (i == span - 2) & (flags[1] == 1))
    mid_color = [color_ref[c] for c in range(3)]
    mid_depth = depth_ref[...]
    mid_trans = trans_ref[...]
    color = [jnp.zeros((rows, lanes), jnp.float32) for c in range(3)]
    total = jnp.zeros((rows, lanes), jnp.float32)
    trans = jnp.ones((rows, lanes), jnp.float32)

    def add_cells(cells, color, total, trans):
        for shade, chan in cells:
            fade = jnp.exp(-chan[3])
            weight = shade * (1.0 - fade) * trans
            color = [color[c] + weight * chan[c] for c in range(3)]
            total = total + chan[3]
            trans = trans * fade
        return color, total, trans

    color, total, trans = add_cells(front, color, total, trans)
    color = [color[c] + trans * mid_color[c] for c in range(3)]
    total = total + mid_depth
    trans = trans * mid_trans
    color, total, trans = add_cells(back, color, total, trans)
    for c in range(3):
        out_color_ref[c] = color[c]
    out_depth_ref[...] = total


def render_block(table, flags, planes, front, back, rows, segments):
    depth, tall, lanes = planes.shape
    smem = pl.BlockSpec(memory_space=pltpu.SMEM)
    vmem = pl.BlockSpec(memory_space=pltpu.VMEM)
    color_shape = jax.ShapeDtypeStruct((3, rows, lanes), jnp.float32)
    plane_shape = jax.ShapeDtypeStruct((rows, lanes), jnp.float32)
    middle = pl.pallas_call(
        lambda *refs: middle_kernel(*refs, segments=segments, rows=rows, width=256),
        in_specs=[smem, smem, vmem],
        out_specs=[vmem, vmem, vmem],
        out_shape=[color_shape, plane_shape, plane_shape],
        scratch_shapes=[pltpu.VMEM((depth, rows, lanes), jnp.float32) for _ in range(3)],
        compiler_params=pltpu.CompilerParams(vmem_limit_bytes=48 * 1024 * 1024),
    )(table, flags, planes)
    return pl.pallas_call(
        lambda *refs: edge_kernel(*refs, segments=segments, rows=rows),
        in_specs=[smem, smem] + [vmem] * 5,
        out_specs=[vmem, vmem],
        out_shape=[color_shape, plane_shape],
        compiler_params=pltpu.CompilerParams(vmem_limit_bytes=48 * 1024 * 1024),
    )(table, flags, front, back, *middle)


def body(volume, knot_pos, knot_color):
    depth_count = lax.axis_size("depth")
    depth, rows, width = volume.shape
    sigma_scale = 4.0 / (depth * depth_count)
    x_low = shifted(volume[:, rows - 2:], "tile", 1)
    x_high = shifted(volume[:, :2], "tile", -1)
    gap = jnp.zeros((depth, TALL - rows - 4, width), volume.dtype)
    planes = jnp.concatenate([volume, x_high, gap, x_low], axis=1).astype(jnp.float32)
    z_low = shifted(planes[depth - 2:], "depth", 1)
    z_high = shifted(planes[:2], "depth", -1)
    front = jnp.concatenate([z_low, planes[:EDGE + 2]], axis=0)
    back = jnp.concatenate([planes[depth - EDGE - 2:], z_high], axis=0)
    d = lax.axis_index("depth")
    t = lax.axis_index("tile")
    flags = jnp.stack([d == 0, d == depth_count - 1, t == 0, t == lax.axis_size("tile") - 1])
    table = ramp_table(knot_pos, knot_color, sigma_scale)
    brick_color, optical_depth = render_block(
        table, flags.astype(jnp.int32), planes, front, back, rows, knot_pos.shape[0] - 1)
    piece = width // depth_count
    weighted = jnp.concatenate([brick_color, optical_depth[None]], axis=0)
    weighted = weighted.reshape(4, rows, depth_count, piece).transpose(2, 0, 1, 3)
    blocks = lax.all_to_all(weighted, "depth", 0, 0, tiled=True)
    ahead = jnp.zeros((rows, piece), jnp.float32)
    image = jnp.zeros((3, rows, piece), jnp.float32)
    for b in range(depth_count):
        image = image + blocks[b, :3] * jnp.exp(-ahead)[None]
        ahead = ahead + blocks[b, 3]
    return jnp.concatenate([image, (1.0 - jnp.exp(-ahead))[None]], axis=0)


def solution(mesh):
    in_specs = (P("depth", "tile", None), P(), P())
    out_specs = P(None, "tile", "depth")
    return jax.shard_map(body, mesh=mesh, in_specs=in_specs, out_specs=out_specs, check_vma=False)
```

time: 317 us -> 83.2 us (0.26)
  other arithmetic: 183 us -> 6.67 us
  Pallas kernels: 0 us -> 40.7 us
  waiting for transfers between devices: 39.2 us -> 6.14 us
  between operations: 32.6 us -> 0.26 us
  local copies, waits for them, and re-layouts: 17.9 us -> 2.85 us
  starting transfers between devices: 23.9 us -> 14.2 us
  blocking collectives: 17.4 us -> 12 us
    reduce_sum x4 -> x0, other arithmetic: 168 us -> none  [the longest x3 130 us: composite(): jnp.sum(weight * colors[c], axis=0)]
    pallas_call x0 -> x2, Pallas kernels: none -> 40.7 us  [the longest x1 37.9 us: render_block(): pl.pallas_call(lambda *refs: middle_kernel(*refs, segments=segments, rows...]
    reduce_scatter x1 -> x0, waiting for transfers between devices: 30 us -> none  [body(): lax.psum_scatter(weighted, 'depth', scatter_dimension=2, tiled=True)]
    all_gather x1 -> x0, blocking collectives: 17.4 us -> none  [carried_in(): pieces = lax.all_gather(value, axis)]
    slice x11 -> x4, local copies, waits for them, and re-layouts: 15.3 us -> 2.64 us  [the longest x1 1.99 us: body(): x_high = shifted(volume[:, :2], 'tile', -1)]
    all_to_all x0 -> x1, blocking collectives: none -> 12 us  [body(): blocks = lax.all_to_all(weighted, 'depth', 0, 0, tiled=True)]
    ppermute x8 -> x4, starting transfers between devices: 23.9 us -> 14.2 us  [shifted(): return lax.ppermute(block, axis, pairs)]
    convert_element_type x4 -> x3, other arithmetic: 9.48 us -> 3.71 us  [the longest x1 2.97 us: body(): jnp.concatenate([volume, x_high, gap, x_low], axis=1).astype(jnp.float32)]
  transfers between devices with their start and end apart: 9 -> 4, of which waited for: 5 -> 1; matrix products, arithmetic and copies ran while one was open for 2% -> 5% of each run, Pallas kernels for 0% -> 46%
where the time goes in v7:
time: 83.2 us; the launch traced here: 82.8 us
  Pallas kernels  40.7 us (49%)
  starting transfers between devices  14.2 us (17%)
  blocking collectives  12 us (14%)
  other arithmetic  6.67 us (8%)
  waiting for transfers between devices  6.14 us (7%)
  local copies, waits for them, and re-layouts  2.85 us (3%)
    pallas_call x1, Pallas kernels, render_block(): pl.pallas_call(lambda *refs: middle_kernel(*refs, segments=segments, rows...  37.9 us
    ppermute x4, starting transfers between devices, shifted(): return lax.ppermute(block, axis, pairs)  14.2 us
    all_to_all x1, blocking collectives, body(): blocks = lax.all_to_all(weighted, 'depth', 0, 0, tiled=True)  12 us
    ppermute x4, waiting for transfers between devices, shifted(): return lax.ppermute(block, axis, pairs)  6.14 us
    convert_element_type x1, other arithmetic, body(): jnp.concatenate([volume, x_high, gap, x_low], axis=1).astype(jnp.float32)  2.97 us
    pallas_call x1, Pallas kernels, render_block(): pl.pallas_call(lambda *refs: edge_kernel(*refs, segments=segments, rows=r...  2.78 us
    slice x1, local copies, waits for them, and re-layouts, body(): x_high = shifted(volume[:, :2], 'tile', -1)  1.99 us
  transfers between devices with their start and end apart: 4, of which 1 were waited for; matrix products, arithmetic and copies ran while one was open for 5% of the time, Pallas kernels for 46%

profile of v7, /device:TPU:24, one launch (start us, length us, event | category | flops | bytes accessed | tf_op | source)
XLA Modules:
  0.0 82.8 jit_solution(16982250786517041985)
XLA Ops:
  0.0 2.0 %fusion.22 = (bf16[64,2,1024]{2,1,0:T(2,128)(2,1)S(1)}, bf16[64,2,1024]{2,1,0:T(2,128)(2,1)S(1)}) fusion(bf16[64,16,1024]{2,1,0:T(8,128)(2,1)} %param.4), kind=kLoop, calls=%fused_computation.74 | loop fusion | bytes 1048576 | tf_op jit(solution)/shard_map/slice | solution.py:203
  2.0 7.9 %collective-permute-start = (bf16[64,2,1024]{2,1,0:T(2,128)(2,1)S(1)}, bf16[64,2,1024]{2,1,0:T(2,128)(2,1)S(1)}, u32[]{:S(2)}, u32[]{:S(2)}) collective-permute-start(bf16[64,2,1024]{2,1,0:T(2,128)(2,1)S(1)} %get-tuple-element.25), channel_id=1, source_target_pairs={{1,0},{2,1},{3,2},{4,3},{5,4},{6,5},{7,6},{8,7},{9,8},{10,9},{11,1... | collective-permute-start | bytes 786440 | tf_op jit(solution)/shard_map/ppermute | solution.py:15
  9.9 1.9 %collective-permute-start.1 = (bf16[64,2,1024]{2,1,0:T(2,128)(2,1)S(1)}, bf16[64,2,1024]{2,1,0:T(2,128)(2,1)S(1)}, u32[]{:S(2)}, u32[]{:S(2)}) collective-permute-start(bf16[64,2,1024]{2,1,0:T(2,128)(2,1)S(1)} %get-tuple-element.26), channel_id=1, source_target_pairs={{0,1},{1,2},{2,3},{3,4},{4,5},{5,6},{6,7},{7,8},{8,9},{9,10},{10,1... | collective-permute-start | bytes 786440 | tf_op jit(solution)/shard_map/ppermute | solution.py:15
  11.9 0.7 fusion.24
  12.5 0.1 slice_subtract_fusion
  12.6 0.6 fusion.23
  13.2 0.8 convert_multiply_fusion
  13.9 0.1 multiply_subtract_fusion
  14.1 0.1 pad.48.clone
  14.2 1.3 %fusion.19 = f32[1,16]{1,0:T(1,128)S(1)} fusion(f32[1]{0:T(128)} %get-tuple-element.42, f32[1]{0:T(128)} %get-tuple-element.41), kind=kLoop, calls=%fused_computation.70 | loop fusion | flops 64 | bytes 72 | tf_op jit(solution)/shard_map/stack | solution.py:30
  15.5 0.1 add_convert_fusion.refs_1_
  15.6 0.0 collective-permute-done
  15.6 6.1 %collective-permute-done.1 = bf16[64,2,1024]{2,1,0:T(2,128)(2,1)S(1)} collective-permute-done((bf16[64,2,1024]{2,1,0:T(2,128)(2,1)S(1)}, bf16[64,2,1024]{2,1,0:T(2,128)(2,1)S(1)}, u32[]{:S(2)}, u32[]{:S(2)}) %collective-permute-start.1) | collective-permute-done | bytes 262176 | tf_op jit(solution)/shard_map/ppermute | solution.py:15
  21.7 3.0 %maximum_convert_fusion.refs_2_ = f32[64,24,1024]{2,1,0:T(8,128)S(1)} fusion(bf16[64,2,1024]{2,1,0:T(2,128)(2,1)S(1)} %collective-permute-done.1, bf16[64,2,1024]{2,1,0:T(2,128)(2,1)S(1)} %collective-permute-done, bf16[64,16,1024]{2,1,0:T(8,128)(2,1)} %param.4, bf16[24]{0:T(256)(128)(2,1)S(1)} %pad.48.clone), kind=kLoop, calls=%fused_computation | loop fusion | flops 12582912 | bytes 8912944 | tf_op jit(solution)/shard_map/convert_element_type | solution.py:205
  24.7 0.0 copy-start
  24.7 1.3 %collective-permute-start.3 = (f32[2,24,1024]{2,1,0:T(8,128)S(1)}, f32[2,24,1024]{2,1,0:T(8,128)S(1)}, u32[]{:S(2)}, u32[]{:S(2)}) collective-permute-start(f32[2,24,1024]{2,1,0:T(8,128)S(1)} %get-tuple-element.23), channel_id=1, source_target_pairs={{32,0},{64,32},{96,64},{128,96},{160,128},{192,160},{224,192},{33,... | collective-permute-start | bytes 589832 | tf_op jit(solution)/shard_map/ppermute | solution.py:15
  26.0 3.0 %collective-permute-start.2 = (f32[2,24,1024]{2,1,0:T(8,128)S(1)}, f32[2,24,1024]{2,1,0:T(8,128)S(1)}, u32[]{:S(2)}, u32[]{:S(2)}) collective-permute-start(f32[2,24,1024]{2,1,0:T(8,128)S(1)} %get-tuple-element.24), channel_id=1, source_target_pairs={{0,32},{32,64},{64,96},{96,128},{128,160},{160,192},{192,224},{1,3... | collective-permute-start | bytes 589832 | tf_op jit(solution)/shard_map/ppermute | solution.py:15
  29.1 0.1 fusion.20
  29.2 0.0 copy-done
  29.2 37.9 %shard_map.46 = (f32[3,16,1024]{2,1,0:T(8,128)S(1)}, f32[16,1024]{1,0:T(8,128)S(1)}, f32[16,1024]{1,0:T(8,128)S(1)}) custom-call(f32[10,16]{1,0:T(8,128)S(1)} %stack.62.refs_0_, s32[4]{0:T(128)S(1)} %add_convert_fusion.refs_1_, f32[64,24,1024]{2,1,0:T(8,128)} %copy-done), custom_call_target="tpu_custom_call" | custom-call | tf_op jit(solution)/shard_map/pallas_call | solution.py:181
  67.1 0.0 collective-permute-done.3
  67.2 0.0 collective-permute-done.2
  67.2 2.8 %shard_map.47 = (f32[3,16,1024]{2,1,0:T(8,128)S(1)}, f32[16,1024]{1,0:T(8,128)S(1)}) custom-call(f32[10,16]{1,0:T(8,128)S(1)} %stack.62.refs_0_, s32[4]{0:T(128)S(1)} %add_convert_fusion.refs_1_, f32[6,24,1024]{2,1,0:T(8,128)S(1)} %pad_maximum_fusion.refs_2_, f32[6,24,1024]{2,1,0:T(8,128)S(1)} %pad_maximum_fusion.1.refs_3_, ...), custom_call_target="tpu_custom_call" | custom-call | tf_op jit(solution)/shard_map/pallas_call | solution.py:189
  70.1 12.0 %all_to_all.5 = f32[8,4,16,128]{3,2,1,0:T(8,128)S(1)} all-to-all(f32[8,4,16,128]{3,2,1,0:T(8,128)S(1)} %maximum_bitcast_fusion), channel_id=1, replica_groups=mesh['depth'=8,'tile'=32] {'depth'}, dimensions={0} | all-to-all | bytes 524288 | tf_op jit(solution)/shard_map/all_to_all | solution.py:219
  82.2 0.6 pad_maximum_fusion.2
  (22 shorter events, 0.3 us)
Async XLA Ops:
  2.0 13.6 %collective-permute-start = (bf16[64,2,1024]{2,1,0:T(2,128)(2,1)S(1)}, bf16[64,2,1024]{2,1,0:T(2,128)(2,1)S(1)}, u32[]{:S(2)}, u32[]{:S(2)}) collective-permute-start(bf16[64,2,1024]{2,1,0:T(2,128)(2,1)S(1)} %get-tuple-element.25), channel_id=1, source_target_pairs={{1,0},{2,1},{3,2},{4,3},{5,4},{6,5},{7,6},{8,7},{9,8},{10,9},{11,1... | collective-permute-start | bytes 786440 | tf_op jit(solution)/shard_map/ppermute | solution.py:15
  9.9 11.8 %collective-permute-start.1 = (bf16[64,2,1024]{2,1,0:T(2,128)(2,1)S(1)}, bf16[64,2,1024]{2,1,0:T(2,128)(2,1)S(1)}, u32[]{:S(2)}, u32[]{:S(2)}) collective-permute-start(bf16[64,2,1024]{2,1,0:T(2,128)(2,1)S(1)} %get-tuple-element.26), channel_id=1, source_target_pairs={{0,1},{1,2},{2,3},{3,4},{4,5},{5,6},{6,7},{7,8},{8,9},{9,10},{10,1... | collective-permute-start | bytes 786440 | tf_op jit(solution)/shard_map/ppermute | solution.py:15
  24.7 4.5 %copy-start = (f32[64,24,1024]{2,1,0:T(8,128)}, f32[64,24,1024]{2,1,0:T(8,128)S(1)}, u32[]{:S(2)}) copy-start(f32[64,24,1024]{2,1,0:T(8,128)S(1)} %maximum_convert_fusion.refs_2_) | copy-start | bytes 18874372
  24.7 42.4 %collective-permute-start.3 = (f32[2,24,1024]{2,1,0:T(8,128)S(1)}, f32[2,24,1024]{2,1,0:T(8,128)S(1)}, u32[]{:S(2)}, u32[]{:S(2)}) collective-permute-start(f32[2,24,1024]{2,1,0:T(8,128)S(1)} %get-tuple-element.23), channel_id=1, source_target_pairs={{32,0},{64,32},{96,64},{128,96},{160,128},{192,160},{224,192},{33,... | collective-permute-start | bytes 589832 | tf_op jit(solution)/shard_map/ppermute | solution.py:15
  26.0 41.1 %collective-permute-start.2 = (f32[2,24,1024]{2,1,0:T(8,128)S(1)}, f32[2,24,1024]{2,1,0:T(8,128)S(1)}, u32[]{:S(2)}, u32[]{:S(2)}) collective-permute-start(f32[2,24,1024]{2,1,0:T(8,128)S(1)} %get-tuple-element.24), channel_id=1, source_target_pairs={{0,32},{32,64},{64,96},{96,128},{128,160},{160,192},{192,224},{1,3... | collective-permute-start | bytes 589832 | tf_op jit(solution)/shard_map/ppermute | solution.py:15

commit v8 on v7

--- a/solution.py
+++ b/solution.py
@@ -82,14 +82,17 @@
     return ((row != tall - 1) | (flags[2] == 0)) & ((row != rows) | (flags[3] == 0))
 
 
-def middle_kernel(table, flags, planes_ref, color_ref, depth_ref, trans_ref,
+def middle_kernel(table, flags, volume_ref, side_ref, color_ref, depth_ref, trans_ref,
                   smooth_ref, square_ref, facing_ref, *, segments, rows, width):
-    depth, tall, lanes = planes_ref.shape
+    depth, _, lanes = volume_ref.shape
+    tall = rows + side_ref.shape[1]
     keep = row_keep(flags, tall, lanes, rows)
 
+    def joined(i):
+        return jnp.concatenate([volume_ref[i].astype(jnp.float32), side_ref[i]], axis=0)
+
     def plane(i, carry):
-        center, square, facing = smooth_plane(
-            planes_ref[i - 1], planes_ref[i], planes_ref[i + 1], keep, rows)
+        center, square, facing = smooth_plane(joined(i - 1), joined(i), joined(i + 1), keep, rows)
         smooth_ref[i] = center
         square_ref[i] = square
         facing_ref[i] = facing
@@ -172,20 +175,20 @@
     out_depth_ref[...] = total
 
 
-def render_block(table, flags, planes, front, back, rows, segments):
-    depth, tall, lanes = planes.shape
+def render_block(table, flags, volume, side, front, back, rows, segments):
+    depth, _, lanes = volume.shape
     smem = pl.BlockSpec(memory_space=pltpu.SMEM)
     vmem = pl.BlockSpec(memory_space=pltpu.VMEM)
     color_shape = jax.ShapeDtypeStruct((3, rows, lanes), jnp.float32)
     plane_shape = jax.ShapeDtypeStruct((rows, lanes), jnp.float32)
     middle = pl.pallas_call(
         lambda *refs: middle_kernel(*refs, segments=segments, rows=rows, width=256),
-        in_specs=[smem, smem, vmem],
+        in_specs=[smem, smem, vmem, vmem],
         out_specs=[vmem, vmem, vmem],
         out_shape=[color_shape, plane_shape, plane_shape],
         scratch_shapes=[pltpu.VMEM((depth, rows, lanes), jnp.float32) for _ in range(3)],
         compiler_params=pltpu.CompilerParams(vmem_limit_bytes=48 * 1024 * 1024),
-    )(table, flags, planes)
+    )(table, flags, volume, side)
     return pl.pallas_call(
         lambda *refs: edge_kernel(*refs, segments=segments, rows=rows),
         in_specs=[smem, smem] + [vmem] * 5,
@@ -202,17 +205,18 @@
     x_low = shifted(volume[:, rows - 2:], "tile", 1)
     x_high = shifted(volume[:, :2], "tile", -1)
     gap = jnp.zeros((depth, TALL - rows - 4, width), volume.dtype)
-    planes = jnp.concatenate([volume, x_high, gap, x_low], axis=1).astype(jnp.float32)
-    z_low = shifted(planes[depth - 2:], "depth", 1)
-    z_high = shifted(planes[:2], "depth", -1)
-    front = jnp.concatenate([z_low, planes[:EDGE + 2]], axis=0)
-    back = jnp.concatenate([planes[depth - EDGE - 2:], z_high], axis=0)
+    side = jnp.concatenate([x_high, gap, x_low], axis=1).astype(jnp.float32)
+    planes = lambda a, b: jnp.concatenate([volume[a:b].astype(jnp.float32), side[a:b]], axis=1)
+    z_low = shifted(planes(depth - 2, depth), "depth", 1)
+    z_high = shifted(planes(0, 2), "depth", -1)
+    front = jnp.concatenate([z_low, planes(0, EDGE + 2)], axis=0)
+    back = jnp.concatenate([planes(depth - EDGE - 2, depth), z_high], axis=0)
     d = lax.axis_index("depth")
     t = lax.axis_index("tile")
     flags = jnp.stack([d == 0, d == depth_count - 1, t == 0, t == lax.axis_size("tile") - 1])
     table = ramp_table(knot_pos, knot_color, sigma_scale)
     brick_color, optical_depth = render_block(
-        table, flags.astype(jnp.int32), planes, front, back, rows, knot_pos.shape[0] - 1)
+        table, flags.astype(jnp.int32), volume, side, front, back, rows, knot_pos.shape[0] - 1)
     piece = width // depth_count
     weighted = jnp.concatenate([brick_color, optical_depth[None]], axis=0)
     weighted = weighted.reshape(4, rows, depth_count, piece).transpose(2, 0, 1, 3)

time: 83.2 us -> 78.3 us (0.941)
  Pallas kernels: 40.7 us -> 38.2 us
  waiting for transfers between devices: 6.14 us -> 3.96 us
    pallas_call x1, Pallas kernels: 37.9 us -> 35.4 us  [render_block(): pl.pallas_call(lambda *refs: middle_kernel(*refs, segments=segments, rows...]
    ppermute x4, waiting for transfers between devices: 6.14 us -> 3.96 us  [shifted(): return lax.ppermute(block, axis, pairs)]
    convert_element_type x1 -> x3, other arithmetic: 2.97 us -> 2.47 us  [the longest x2 1.9 us: body(): volume[a:b].astype(jnp.float32)]
  transfers between devices with their start and end apart: 4 -> 4, of which waited for: 1 -> 1; matrix products, arithmetic and copies ran while one was open for 5% -> 8% of each run, Pallas kernels for 46% -> 45%
where the time goes in v8:
time: 78.3 us; the launch traced here: 77.9 us
  Pallas kernels  38.2 us (49%)
  starting transfers between devices  14.2 us (18%)
  blocking collectives  12 us (15%)
  other arithmetic  6.35 us (8%)
  waiting for transfers between devices  3.96 us (5%)
  local copies, waits for them, and re-layouts  2.9 us (4%)
    pallas_call x1, Pallas kernels, render_block(): pl.pallas_call(lambda *refs: middle_kernel(*refs, segments=segments, rows...  35.4 us
    ppermute x4, starting transfers between devices, shifted(): return lax.ppermute(block, axis, pairs)  14.2 us
    all_to_all x1, blocking collectives, body(): blocks = lax.all_to_all(weighted, 'depth', 0, 0, tiled=True)  12 us
    ppermute x4, waiting for transfers between devices, shifted(): return lax.ppermute(block, axis, pairs)  3.96 us
    pallas_call x1, Pallas kernels, render_block(): pl.pallas_call(lambda *refs: edge_kernel(*refs, segments=segments, rows=r...  2.78 us
    slice x1, local copies, waits for them, and re-layouts, body(): x_high = shifted(volume[:, :2], 'tile', -1)  1.99 us
    convert_element_type x2, other arithmetic, body(): volume[a:b].astype(jnp.float32)  1.9 us
  transfers between devices with their start and end apart: 4, of which 1 were waited for; matrix products, arithmetic and copies ran while one was open for 8% of the time, Pallas kernels for 45%

profile of v8, /device:TPU:24, one launch (start us, length us, event | category | flops | bytes accessed | tf_op | source)
XLA Modules:
  0.0 77.9 jit_solution(9624442088521712263)
XLA Ops:
  0.0 2.0 %fusion.22 = (bf16[64,2,1024]{2,1,0:T(2,128)(2,1)S(1)}, bf16[64,2,1024]{2,1,0:T(2,128)(2,1)S(1)}) fusion(bf16[64,16,1024]{2,1,0:T(8,128)(2,1)} %refs_2_.1), kind=kLoop, calls=%fused_computation.80 | loop fusion | bytes 1048576 | tf_op jit(solution)/shard_map/slice | solution.py:206
  2.0 7.9 %collective-permute-start = (bf16[64,2,1024]{2,1,0:T(2,128)(2,1)S(1)}, bf16[64,2,1024]{2,1,0:T(2,128)(2,1)S(1)}, u32[]{:S(2)}, u32[]{:S(2)}) collective-permute-start(bf16[64,2,1024]{2,1,0:T(2,128)(2,1)S(1)} %get-tuple-element.29), channel_id=1, source_target_pairs={{1,0},{2,1},{3,2},{4,3},{5,4},{6,5},{7,6},{8,7},{9,8},{10,9},{11,1... | collective-permute-start | bytes 786440 | tf_op jit(solution)/shard_map/ppermute | solution.py:15
  9.9 1.9 %collective-permute-start.1 = (bf16[64,2,1024]{2,1,0:T(2,128)(2,1)S(1)}, bf16[64,2,1024]{2,1,0:T(2,128)(2,1)S(1)}, u32[]{:S(2)}, u32[]{:S(2)}) collective-permute-start(bf16[64,2,1024]{2,1,0:T(2,128)(2,1)S(1)} %get-tuple-element.30), channel_id=1, source_target_pairs={{0,1},{1,2},{2,3},{3,4},{4,5},{5,6},{6,7},{7,8},{8,9},{9,10},{10,1... | collective-permute-start | bytes 786440 | tf_op jit(solution)/shard_map/ppermute | solution.py:15
  11.9 0.7 fusion.24
  12.5 0.1 slice_subtract_fusion
  12.6 0.7 fusion.23
  13.3 0.9 %slice_convert_fusion.2 = (f32[2,16,1024]{2,1,0:T(8,128)S(1)}, f32[2,16,1024]{2,1,0:T(8,128)S(1)}) fusion(bf16[64,16,1024]{2,1,0:T(8,128)(2,1)} %refs_2_.1), kind=kLoop, calls=%fused_computation.9 | loop fusion | flops 65536 | bytes 393216 | tf_op jit(solution)/shard_map/convert_element_type | solution.py:209
  14.2 0.8 convert_multiply_fusion
  14.9 0.1 multiply_subtract_fusion
  15.1 1.4 %fusion.19 = f32[1,16]{1,0:T(1,128)S(1)} fusion(f32[1]{0:T(128)} %get-tuple-element.46, f32[1]{0:T(128)} %get-tuple-element.45), kind=kLoop, calls=%fused_computation.76 | loop fusion | flops 64 | bytes 72 | tf_op jit(solution)/shard_map/stack | solution.py:30
  16.5 0.1 add_convert_fusion.refs_1_
  16.6 0.1 pad.53.clone
  16.7 1.0 %slice_convert_fusion = (f32[4,16,1024]{2,1,0:T(8,128)S(1)}, f32[4,16,1024]{2,1,0:T(8,128)S(1)}) fusion(bf16[64,16,1024]{2,1,0:T(8,128)(2,1)} %refs_2_.1), kind=kLoop, calls=%fused_computation.7 | loop fusion | flops 131072 | bytes 786432 | tf_op jit(solution)/shard_map/convert_element_type | solution.py:209
  17.7 0.0 copy-start
  17.8 0.0 collective-permute-done
  17.8 4.0 %collective-permute-done.1 = bf16[64,2,1024]{2,1,0:T(2,128)(2,1)S(1)} collective-permute-done((bf16[64,2,1024]{2,1,0:T(2,128)(2,1)S(1)}, bf16[64,2,1024]{2,1,0:T(2,128)(2,1)S(1)}, u32[]{:S(2)}, u32[]{:S(2)}) %collective-permute-start.1) | collective-permute-done | bytes 262176 | tf_op jit(solution)/shard_map/ppermute | solution.py:15
  21.7 0.6 maximum_convert_fusion.refs_3_
  22.3 1.3 %collective-permute-start.3 = (f32[2,24,1024]{2,1,0:T(8,128)S(1)}, f32[2,24,1024]{2,1,0:T(8,128)S(1)}, u32[]{:S(2)}, u32[]{:S(2)}) collective-permute-start(f32[2,24,1024]{2,1,0:T(8,128)S(1)} %pad_maximum_fusion.2), channel_id=1, source_target_pairs={{32,0},{64,32},{96,64},{128,96},{160,128},{192,160},{224,192},{33,... | collective-permute-start | bytes 589832 | tf_op jit(solution)/shard_map/ppermute | solution.py:15
  23.7 3.0 %collective-permute-start.2 = (f32[2,24,1024]{2,1,0:T(8,128)S(1)}, f32[2,24,1024]{2,1,0:T(8,128)S(1)}, u32[]{:S(2)}, u32[]{:S(2)}) collective-permute-start(f32[2,24,1024]{2,1,0:T(8,128)S(1)} %pad_maximum_fusion.1), channel_id=1, source_target_pairs={{0,32},{32,64},{64,96},{96,128},{128,160},{160,192},{192,224},{1,3... | collective-permute-start | bytes 589832 | tf_op jit(solution)/shard_map/ppermute | solution.py:15
  26.7 0.0 copy-done
  26.7 35.4 %shard_map.46 = (f32[3,16,1024]{2,1,0:T(8,128)S(1)}, f32[16,1024]{1,0:T(8,128)S(1)}, f32[16,1024]{1,0:T(8,128)S(1)}) custom-call(f32[10,16]{1,0:T(8,128)S(1)} %stack.62.refs_0_, s32[4]{0:T(128)S(1)} %add_convert_fusion.refs_1_, bf16[64,16,1024]{2,1,0:T(8,128)(2,1)S(1)} %copy-done, f32[64,8,1024]{2,1,0:T(8,128)S(1)} %maximum_convert_fusion.refs_3_), custom_call_target="tpu_custom_call" | custom-call | tf_op jit(solution)/shard_map/pallas_call | solution.py:184
  62.2 0.0 collective-permute-done.3
  62.2 0.0 collective-permute-done.2
  62.3 2.8 %shard_map.47 = (f32[3,16,1024]{2,1,0:T(8,128)S(1)}, f32[16,1024]{1,0:T(8,128)S(1)}) custom-call(f32[10,16]{1,0:T(8,128)S(1)} %stack.62.refs_0_, s32[4]{0:T(128)S(1)} %add_convert_fusion.refs_1_, f32[6,24,1024]{2,1,0:T(8,128)S(1)} %maximum_maximum_fusion.refs_2_, f32[6,24,1024]{2,1,0:T(8,128)S(1)} %pad_maximum_fusion.refs_3_, ...), custom_call_target="tpu_custom_call" | custom-call | tf_op jit(solution)/shard_map/pallas_call | solution.py:192
  65.2 12.0 %all_to_all.5 = f32[8,4,16,128]{3,2,1,0:T(8,128)S(1)} all-to-all(f32[8,4,16,128]{3,2,1,0:T(8,128)S(1)} %maximum_bitcast_fusion), channel_id=1, replica_groups=mesh['depth'=8,'tile'=32] {'depth'}, dimensions={0} | all-to-all | bytes 524288 | tf_op jit(solution)/shard_map/all_to_all | solution.py:223
  77.3 0.6 pad_maximum_fusion.3
  (25 shorter events, 0.4 us)
Async XLA Ops:
  2.0 15.8 %collective-permute-start = (bf16[64,2,1024]{2,1,0:T(2,128)(2,1)S(1)}, bf16[64,2,1024]{2,1,0:T(2,128)(2,1)S(1)}, u32[]{:S(2)}, u32[]{:S(2)}) collective-permute-start(bf16[64,2,1024]{2,1,0:T(2,128)(2,1)S(1)} %get-tuple-element.29), channel_id=1, source_target_pairs={{1,0},{2,1},{3,2},{4,3},{5,4},{6,5},{7,6},{8,7},{9,8},{10,9},{11,1... | collective-permute-start | bytes 786440 | tf_op jit(solution)/shard_map/ppermute | solution.py:15
  9.9 11.8 %collective-permute-start.1 = (bf16[64,2,1024]{2,1,0:T(2,128)(2,1)S(1)}, bf16[64,2,1024]{2,1,0:T(2,128)(2,1)S(1)}, u32[]{:S(2)}, u32[]{:S(2)}) collective-permute-start(bf16[64,2,1024]{2,1,0:T(2,128)(2,1)S(1)} %get-tuple-element.30), channel_id=1, source_target_pairs={{0,1},{1,2},{2,3},{3,4},{4,5},{5,6},{6,7},{7,8},{8,9},{9,10},{10,1... | collective-permute-start | bytes 786440 | tf_op jit(solution)/shard_map/ppermute | solution.py:15
  17.7 9.0 %copy-start = (bf16[64,16,1024]{2,1,0:T(8,128)(2,1)S(1)}, bf16[64,16,1024]{2,1,0:T(8,128)(2,1)}, u32[]{:S(2)}) copy-start(bf16[64,16,1024]{2,1,0:T(8,128)(2,1)} %refs_2_.1) | copy-start | bytes 6291460
  22.3 39.8 %collective-permute-start.3 = (f32[2,24,1024]{2,1,0:T(8,128)S(1)}, f32[2,24,1024]{2,1,0:T(8,128)S(1)}, u32[]{:S(2)}, u32[]{:S(2)}) collective-permute-start(f32[2,24,1024]{2,1,0:T(8,128)S(1)} %pad_maximum_fusion.2), channel_id=1, source_target_pairs={{32,0},{64,32},{96,64},{128,96},{160,128},{192,160},{224,192},{33,... | collective-permute-start | bytes 589832 | tf_op jit(solution)/shard_map/ppermute | solution.py:15
  23.7 38.6 %collective-permute-start.2 = (f32[2,24,1024]{2,1,0:T(8,128)S(1)}, f32[2,24,1024]{2,1,0:T(8,128)S(1)}, u32[]{:S(2)}, u32[]{:S(2)}) collective-permute-start(f32[2,24,1024]{2,1,0:T(8,128)S(1)} %pad_maximum_fusion.1), channel_id=1, source_target_pairs={{0,32},{32,64},{64,96},{96,128},{128,160},{160,192},{192,224},{1,3... | collective-permute-start | bytes 589832 | tf_op jit(solution)/shard_map/ppermute | solution.py:15

commit v9 on v8

--- a/solution.py
+++ b/solution.py
@@ -31,20 +31,28 @@
 
 
 def y_prev(a):
-    lane = lax.broadcasted_iota(jnp.int32, a.shape, 1)
-    return jnp.where(lane == 0, 0.0, pltpu.roll(a, 1, 1))
+    rolled = pltpu.roll(a, 1, 1)
+    lane = lax.broadcasted_iota(jnp.int32, (a.shape[0], 128), 1)
+    first = jnp.where(lane == 0, 0.0, rolled[:, :128])
+    return jnp.concatenate([first, rolled[:, 128:]], axis=1)
 
 
 def y_next(a):
-    lane = lax.broadcasted_iota(jnp.int32, a.shape, 1)
-    return jnp.where(lane == a.shape[1] - 1, 0.0, pltpu.roll(a, a.shape[1] - 1, 1))
+    rolled = pltpu.roll(a, a.shape[1] - 1, 1)
+    lane = lax.broadcasted_iota(jnp.int32, (a.shape[0], 128), 1)
+    last = jnp.where(lane == 127, 0.0, rolled[:, -128:])
+    return jnp.concatenate([rolled[:, :-128], last], axis=1)
 
 
 def smooth_plane(low, mid, high, keep, rows):
     tall = mid.shape[0]
     near = low + high + pltpu.roll(mid, tall - 1, 0) + pltpu.roll(mid, 1, 0)
     near = near + y_prev(mid) + y_next(mid)
-    smooth = jnp.where(keep, 0.4 * mid + 0.1 * near, 0.0)
+    smooth = 0.4 * mid + 0.1 * near
+    if keep.shape[0] == tall:
+        smooth = jnp.where(keep, smooth, 0.0)
+    else:
+        smooth = jnp.concatenate([smooth[:rows], jnp.where(keep, smooth[rows:], 0.0)], axis=0)
     smooth = smooth.astype(jnp.bfloat16).astype(jnp.float32)
     center = smooth[:rows]
     slope_x = 0.5 * (pltpu.roll(smooth, tall - 1, 0)[:rows] - pltpu.roll(smooth, 1, 0)[:rows])
@@ -86,7 +94,7 @@
                   smooth_ref, square_ref, facing_ref, *, segments, rows, width):
     depth, _, lanes = volume_ref.shape
     tall = rows + side_ref.shape[1]
-    keep = row_keep(flags, tall, lanes, rows)
+    keep = row_keep(flags, tall, lanes, rows)[rows:]
 
     def joined(i):
         return jnp.concatenate([volume_ref[i].astype(jnp.float32), side_ref[i]], axis=0)
@@ -98,7 +106,7 @@
         facing_ref[i] = facing
         return carry
 
-    lax.fori_loop(1, depth - 1, plane, 0)
+    lax.fori_loop(1, depth - 1, plane, 0, unroll=2)
     palette = Palette(table, segments)
     sub = 8
     for r0 in range(0, rows, sub):

time: 78.3 us -> 73.8 us (0.943)
  Pallas kernels: 38.2 us -> 33.7 us
    pallas_call x1, Pallas kernels: 35.4 us -> 30.9 us  [render_block(): pl.pallas_call(lambda *refs: middle_kernel(*refs, segments=segments, rows...]
  transfers between devices with their start and end apart: 4 -> 4, of which waited for: 1 -> 1; matrix products, arithmetic and copies ran while one was open for 8% -> 8% of each run, Pallas kernels for 45% -> 42%
where the time goes in v9:
time: 73.8 us; the launch traced here: 73.4 us
  Pallas kernels  33.7 us (46%)
  starting transfers between devices  14.2 us (19%)
  blocking collectives  12 us (16%)
  other arithmetic  6.35 us (9%)
  waiting for transfers between devices  3.96 us (5%)
  local copies, waits for them, and re-layouts  2.9 us (4%)
    pallas_call x1, Pallas kernels, render_block(): pl.pallas_call(lambda *refs: middle_kernel(*refs, segments=segments, rows...  30.9 us
    ppermute x4, starting transfers between devices, shifted(): return lax.ppermute(block, axis, pairs)  14.2 us
    all_to_all x1, blocking collectives, body(): blocks = lax.all_to_all(weighted, 'depth', 0, 0, tiled=True)  12 us
    ppermute x4, waiting for transfers between devices, shifted(): return lax.ppermute(block, axis, pairs)  3.96 us
    pallas_call x1, Pallas kernels, render_block(): pl.pallas_call(lambda *refs: edge_kernel(*refs, segments=segments, rows=r...  2.8 us
    slice x1, local copies, waits for them, and re-layouts, body(): x_high = shifted(volume[:, :2], 'tile', -1)  1.99 us
    convert_element_type x2, other arithmetic, body(): volume[a:b].astype(jnp.float32)  1.9 us
  transfers between devices with their start and end apart: 4, of which 1 were waited for; matrix products, arithmetic and copies ran while one was open for 8% of the time, Pallas kernels for 42%

profile of v9, /device:TPU:24, one launch (start us, length us, event | category | flops | bytes accessed | tf_op | source)
XLA Modules:
  0.0 73.4 jit_solution(1159389665239534014)
XLA Ops:
  0.0 2.0 %fusion.22 = (bf16[64,2,1024]{2,1,0:T(2,128)(2,1)S(1)}, bf16[64,2,1024]{2,1,0:T(2,128)(2,1)S(1)}) fusion(bf16[64,16,1024]{2,1,0:T(8,128)(2,1)} %refs_2_.1), kind=kLoop, calls=%fused_computation.80 | loop fusion | bytes 1048576 | tf_op jit(solution)/shard_map/slice | solution.py:214
  2.0 7.9 %collective-permute-start = (bf16[64,2,1024]{2,1,0:T(2,128)(2,1)S(1)}, bf16[64,2,1024]{2,1,0:T(2,128)(2,1)S(1)}, u32[]{:S(2)}, u32[]{:S(2)}) collective-permute-start(bf16[64,2,1024]{2,1,0:T(2,128)(2,1)S(1)} %get-tuple-element.29), channel_id=1, source_target_pairs={{1,0},{2,1},{3,2},{4,3},{5,4},{6,5},{7,6},{8,7},{9,8},{10,9},{11,1... | collective-permute-start | bytes 786440 | tf_op jit(solution)/shard_map/ppermute | solution.py:15
  9.9 1.9 %collective-permute-start.1 = (bf16[64,2,1024]{2,1,0:T(2,128)(2,1)S(1)}, bf16[64,2,1024]{2,1,0:T(2,128)(2,1)S(1)}, u32[]{:S(2)}, u32[]{:S(2)}) collective-permute-start(bf16[64,2,1024]{2,1,0:T(2,128)(2,1)S(1)} %get-tuple-element.30), channel_id=1, source_target_pairs={{0,1},{1,2},{2,3},{3,4},{4,5},{5,6},{6,7},{7,8},{8,9},{9,10},{10,1... | collective-permute-start | bytes 786440 | tf_op jit(solution)/shard_map/ppermute | solution.py:15
  11.9 0.7 fusion.24
  12.5 0.1 slice_subtract_fusion
  12.6 0.7 fusion.23
  13.3 0.9 %slice_convert_fusion.2 = (f32[2,16,1024]{2,1,0:T(8,128)S(1)}, f32[2,16,1024]{2,1,0:T(8,128)S(1)}) fusion(bf16[64,16,1024]{2,1,0:T(8,128)(2,1)} %refs_2_.1), kind=kLoop, calls=%fused_computation.9 | loop fusion | flops 65536 | bytes 393216 | tf_op jit(solution)/shard_map/convert_element_type | solution.py:217
  14.2 0.8 %convert_multiply_fusion = f32[4,16]{1,0:T(4,128)S(1)} fusion(s32[4,16]{1,0:T(4,128)} %param.6, f32[4]{0:T(128)} %constant.46), kind=kLoop, calls=%fused_computation.54 | loop fusion | flops 128 | bytes 528 | tf_op jit(solution)/shard_map/mul | solution.py:21
  14.9 0.1 multiply_subtract_fusion
  15.1 1.4 %fusion.19 = f32[1,16]{1,0:T(1,128)S(1)} fusion(f32[1]{0:T(128)} %get-tuple-element.46, f32[1]{0:T(128)} %get-tuple-element.45), kind=kLoop, calls=%fused_computation.76 | loop fusion | flops 64 | bytes 72 | tf_op jit(solution)/shard_map/stack | solution.py:30
  16.5 0.1 add_convert_fusion.refs_1_
  16.6 0.1 pad.53.clone
  16.7 1.0 %slice_convert_fusion = (f32[4,16,1024]{2,1,0:T(8,128)S(1)}, f32[4,16,1024]{2,1,0:T(8,128)S(1)}) fusion(bf16[64,16,1024]{2,1,0:T(8,128)(2,1)} %refs_2_.1), kind=kLoop, calls=%fused_computation.7 | loop fusion | flops 131072 | bytes 786432 | tf_op jit(solution)/shard_map/convert_element_type | solution.py:217
  17.7 0.0 copy-start
  17.8 0.0 collective-permute-done
  17.8 4.0 %collective-permute-done.1 = bf16[64,2,1024]{2,1,0:T(2,128)(2,1)S(1)} collective-permute-done((bf16[64,2,1024]{2,1,0:T(2,128)(2,1)S(1)}, bf16[64,2,1024]{2,1,0:T(2,128)(2,1)S(1)}, u32[]{:S(2)}, u32[]{:S(2)}) %collective-permute-start.1) | collective-permute-done | bytes 262176 | tf_op jit(solution)/shard_map/ppermute | solution.py:15
  21.7 0.6 maximum_convert_fusion.refs_3_
  22.3 1.3 %collective-permute-start.3 = (f32[2,24,1024]{2,1,0:T(8,128)S(1)}, f32[2,24,1024]{2,1,0:T(8,128)S(1)}, u32[]{:S(2)}, u32[]{:S(2)}) collective-permute-start(f32[2,24,1024]{2,1,0:T(8,128)S(1)} %pad_maximum_fusion.2), channel_id=1, source_target_pairs={{32,0},{64,32},{96,64},{128,96},{160,128},{192,160},{224,192},{33,... | collective-permute-start | bytes 589832 | tf_op jit(solution)/shard_map/ppermute | solution.py:15
  23.7 3.0 %collective-permute-start.2 = (f32[2,24,1024]{2,1,0:T(8,128)S(1)}, f32[2,24,1024]{2,1,0:T(8,128)S(1)}, u32[]{:S(2)}, u32[]{:S(2)}) collective-permute-start(f32[2,24,1024]{2,1,0:T(8,128)S(1)} %pad_maximum_fusion.1), channel_id=1, source_target_pairs={{0,32},{32,64},{64,96},{96,128},{128,160},{160,192},{192,224},{1,3... | collective-permute-start | bytes 589832 | tf_op jit(solution)/shard_map/ppermute | solution.py:15
  26.7 0.0 copy-done
  26.7 30.9 %shard_map.46 = (f32[3,16,1024]{2,1,0:T(8,128)S(1)}, f32[16,1024]{1,0:T(8,128)S(1)}, f32[16,1024]{1,0:T(8,128)S(1)}) custom-call(f32[10,16]{1,0:T(8,128)S(1)} %stack.62.refs_0_, s32[4]{0:T(128)S(1)} %add_convert_fusion.refs_1_, bf16[64,16,1024]{2,1,0:T(8,128)(2,1)S(1)} %copy-done, f32[64,8,1024]{2,1,0:T(8,128)S(1)} %maximum_convert_fusion.refs_3_), custom_call_target="tpu_custom_call" | custom-call | tf_op jit(solution)/shard_map/pallas_call | solution.py:192
  57.7 0.0 collective-permute-done.3
  57.8 0.0 collective-permute-done.2
  57.8 2.8 %shard_map.47 = (f32[3,16,1024]{2,1,0:T(8,128)S(1)}, f32[16,1024]{1,0:T(8,128)S(1)}) custom-call(f32[10,16]{1,0:T(8,128)S(1)} %stack.62.refs_0_, s32[4]{0:T(128)S(1)} %add_convert_fusion.refs_1_, f32[6,24,1024]{2,1,0:T(8,128)S(1)} %maximum_maximum_fusion.refs_2_, f32[6,24,1024]{2,1,0:T(8,128)S(1)} %pad_maximum_fusion.refs_3_, ...), custom_call_target="tpu_custom_call" | custom-call | tf_op jit(solution)/shard_map/pallas_call | solution.py:200
  60.7 12.0 %all_to_all.5 = f32[8,4,16,128]{3,2,1,0:T(8,128)S(1)} all-to-all(f32[8,4,16,128]{3,2,1,0:T(8,128)S(1)} %maximum_bitcast_fusion), channel_id=1, replica_groups=mesh['depth'=8,'tile'=32] {'depth'}, dimensions={0} | all-to-all | bytes 524288 | tf_op jit(solution)/shard_map/all_to_all | solution.py:231
  72.8 0.6 pad_maximum_fusion.3
  (25 shorter events, 0.4 us)
Async XLA Ops:
  2.0 15.8 %collective-permute-start = (bf16[64,2,1024]{2,1,0:T(2,128)(2,1)S(1)}, bf16[64,2,1024]{2,1,0:T(2,128)(2,1)S(1)}, u32[]{:S(2)}, u32[]{:S(2)}) collective-permute-start(bf16[64,2,1024]{2,1,0:T(2,128)(2,1)S(1)} %get-tuple-element.29), channel_id=1, source_target_pairs={{1,0},{2,1},{3,2},{4,3},{5,4},{6,5},{7,6},{8,7},{9,8},{10,9},{11,1... | collective-permute-start | bytes 786440 | tf_op jit(solution)/shard_map/ppermute | solution.py:15
  9.9 11.8 %collective-permute-start.1 = (bf16[64,2,1024]{2,1,0:T(2,128)(2,1)S(1)}, bf16[64,2,1024]{2,1,0:T(2,128)(2,1)S(1)}, u32[]{:S(2)}, u32[]{:S(2)}) collective-permute-start(bf16[64,2,1024]{2,1,0:T(2,128)(2,1)S(1)} %get-tuple-element.30), channel_id=1, source_target_pairs={{0,1},{1,2},{2,3},{3,4},{4,5},{5,6},{6,7},{7,8},{8,9},{9,10},{10,1... | collective-permute-start | bytes 786440 | tf_op jit(solution)/shard_map/ppermute | solution.py:15
  17.7 9.0 %copy-start = (bf16[64,16,1024]{2,1,0:T(8,128)(2,1)S(1)}, bf16[64,16,1024]{2,1,0:T(8,128)(2,1)}, u32[]{:S(2)}) copy-start(bf16[64,16,1024]{2,1,0:T(8,128)(2,1)} %refs_2_.1) | copy-start | bytes 6291460
  22.3 35.4 %collective-permute-start.3 = (f32[2,24,1024]{2,1,0:T(8,128)S(1)}, f32[2,24,1024]{2,1,0:T(8,128)S(1)}, u32[]{:S(2)}, u32[]{:S(2)}) collective-permute-start(f32[2,24,1024]{2,1,0:T(8,128)S(1)} %pad_maximum_fusion.2), channel_id=1, source_target_pairs={{32,0},{64,32},{96,64},{128,96},{160,128},{192,160},{224,192},{33,... | collective-permute-start | bytes 589832 | tf_op jit(solution)/shard_map/ppermute | solution.py:15
  23.7 34.1 %collective-permute-start.2 = (f32[2,24,1024]{2,1,0:T(8,128)S(1)}, f32[2,24,1024]{2,1,0:T(8,128)S(1)}, u32[]{:S(2)}, u32[]{:S(2)}) collective-permute-start(f32[2,24,1024]{2,1,0:T(8,128)S(1)} %pad_maximum_fusion.1), channel_id=1, source_target_pairs={{0,32},{32,64},{64,96},{96,128},{128,160},{160,192},{192,224},{1,3... | collective-permute-start | bytes 589832 | tf_op jit(solution)/shard_map/ppermute | solution.py:15

commit v10 on v9

--- a/solution.py
+++ b/solution.py
@@ -215,8 +215,10 @@
     gap = jnp.zeros((depth, TALL - rows - 4, width), volume.dtype)
     side = jnp.concatenate([x_high, gap, x_low], axis=1).astype(jnp.float32)
     planes = lambda a, b: jnp.concatenate([volume[a:b].astype(jnp.float32), side[a:b]], axis=1)
-    z_low = shifted(planes(depth - 2, depth), "depth", 1)
-    z_high = shifted(planes(0, 2), "depth", -1)
+    sides = jnp.concatenate([x_high, gap, x_low], axis=1)
+    narrow = lambda a, b: jnp.concatenate([volume[a:b], sides[a:b]], axis=1)
+    z_low = shifted(narrow(depth - 2, depth), "depth", 1).astype(jnp.float32)
+    z_high = shifted(narrow(0, 2), "depth", -1).astype(jnp.float32)
     front = jnp.concatenate([z_low, planes(0, EDGE + 2)], axis=0)
     back = jnp.concatenate([planes(depth - EDGE - 2, depth), z_high], axis=0)
     d = lax.axis_index("depth")

time: 73.8 us -> 73.9 us (level)
  other arithmetic: 6.35 us -> 5.41 us
  local copies, waits for them, and re-layouts: 2.9 us -> 3.69 us
    convert_element_type x2 -> x1, other arithmetic: 1.9 us -> 1.01 us  [body(): volume[a:b].astype(jnp.float32)]
    slice x0 -> x2, local copies, waits for them, and re-layouts: none -> 0.89 us  [body(): narrow = lambda a, b: jnp.concatenate([volume[a:b], sides[a:b]], axis=1)]
where the time goes in v10:
time: 73.9 us; the launch traced here: 73.5 us
  Pallas kernels  33.7 us (46%)
  starting transfers between devices  14.2 us (19%)
  blocking collectives  12 us (16%)
  other arithmetic  5.41 us (7%)
  waiting for transfers between devices  4.18 us (6%)
  local copies, waits for them, and re-layouts  3.69 us (5%)
    pallas_call x1, Pallas kernels, render_block(): pl.pallas_call(lambda *refs: middle_kernel(*refs, segments=segments, rows...  30.9 us
    ppermute x4, starting transfers between devices, shifted(): return lax.ppermute(block, axis, pairs)  14.2 us
    all_to_all x1, blocking collectives, body(): blocks = lax.all_to_all(weighted, 'depth', 0, 0, tiled=True)  12 us
    ppermute x4, waiting for transfers between devices, shifted(): return lax.ppermute(block, axis, pairs)  4.18 us
    pallas_call x1, Pallas kernels, render_block(): pl.pallas_call(lambda *refs: edge_kernel(*refs, segments=segments, rows=r...  2.8 us
    slice x1, local copies, waits for them, and re-layouts, body(): x_high = shifted(volume[:, :2], 'tile', -1)  1.99 us
  transfers between devices with their start and end apart: 4, of which 1 were waited for; matrix products, arithmetic and copies ran while one was open for 8% of the time, Pallas kernels for 42%

profile of v10, /device:TPU:24, one launch (start us, length us, event | category | flops | bytes accessed | tf_op | source)
XLA Modules:
  0.0 73.5 jit_solution(10171061800263105349)
XLA Ops:
  0.0 2.0 %fusion.23 = (bf16[64,2,1024]{2,1,0:T(2,128)(2,1)S(1)}, bf16[64,2,1024]{2,1,0:T(2,128)(2,1)S(1)}) fusion(bf16[64,16,1024]{2,1,0:T(8,128)(2,1)} %refs_2_.1), kind=kLoop, calls=%fused_computation.79 | loop fusion | bytes 1048576 | tf_op jit(solution)/shard_map/slice | solution.py:214
  2.0 7.9 %collective-permute-start = (bf16[64,2,1024]{2,1,0:T(2,128)(2,1)S(1)}, bf16[64,2,1024]{2,1,0:T(2,128)(2,1)S(1)}, u32[]{:S(2)}, u32[]{:S(2)}) collective-permute-start(bf16[64,2,1024]{2,1,0:T(2,128)(2,1)S(1)} %get-tuple-element.27), channel_id=1, source_target_pairs={{1,0},{2,1},{3,2},{4,3},{5,4},{6,5},{7,6},{8,7},{9,8},{10,9},{11,1... | collective-permute-start | bytes 786440 | tf_op jit(solution)/shard_map/ppermute | solution.py:15
  9.9 1.9 %collective-permute-start.1 = (bf16[64,2,1024]{2,1,0:T(2,128)(2,1)S(1)}, bf16[64,2,1024]{2,1,0:T(2,128)(2,1)S(1)}, u32[]{:S(2)}, u32[]{:S(2)}) collective-permute-start(bf16[64,2,1024]{2,1,0:T(2,128)(2,1)S(1)} %get-tuple-element.28), channel_id=1, source_target_pairs={{0,1},{1,2},{2,3},{3,4},{4,5},{5,6},{6,7},{7,8},{8,9},{9,10},{10,1... | collective-permute-start | bytes 786440 | tf_op jit(solution)/shard_map/ppermute | solution.py:15
  11.9 0.7 fusion.26
  12.5 0.1 slice_subtract_fusion
  12.6 0.6 fusion.25
  13.2 0.9 %fusion.22 = (bf16[2,16,1024]{2,1,0:T(8,128)(2,1)S(1)}, bf16[2,16,1024]{2,1,0:T(8,128)(2,1)S(1)}) fusion(bf16[64,16,1024]{2,1,0:T(8,128)(2,1)} %refs_2_.1), kind=kLoop, calls=%fused_computation.78 | loop fusion | bytes 262144 | tf_op jit(solution)/shard_map/slice | solution.py:219
  14.1 0.8 %convert_multiply_fusion = f32[4,16]{1,0:T(4,128)S(1)} fusion(s32[4,16]{1,0:T(4,128)} %param.6, f32[4]{0:T(128)} %constant.46), kind=kLoop, calls=%fused_computation.52 | loop fusion | flops 128 | bytes 528 | tf_op jit(solution)/shard_map/mul | solution.py:21
  14.8 0.1 multiply_subtract_fusion
  15.0 1.3 %fusion.19 = f32[1,16]{1,0:T(1,128)S(1)} fusion(f32[1]{0:T(128)} %get-tuple-element.48, f32[1]{0:T(128)} %get-tuple-element.47), kind=kLoop, calls=%fused_computation.74 | loop fusion | flops 64 | bytes 72 | tf_op jit(solution)/shard_map/stack | solution.py:30
  16.3 0.1 add_convert_fusion.refs_1_
  16.4 0.1 pad.53.clone
  16.5 1.0 %slice_convert_fusion = (f32[4,16,1024]{2,1,0:T(8,128)S(1)}, f32[4,16,1024]{2,1,0:T(8,128)S(1)}) fusion(bf16[64,16,1024]{2,1,0:T(8,128)(2,1)} %refs_2_.1), kind=kLoop, calls=%fused_computation.5 | loop fusion | flops 131072 | bytes 786432 | tf_op jit(solution)/shard_map/convert_element_type | solution.py:217
  17.5 0.0 copy-start
  17.5 0.0 collective-permute-done
  17.5 4.2 %collective-permute-done.1 = bf16[64,2,1024]{2,1,0:T(2,128)(2,1)S(1)} collective-permute-done((bf16[64,2,1024]{2,1,0:T(2,128)(2,1)S(1)}, bf16[64,2,1024]{2,1,0:T(2,128)(2,1)S(1)}, u32[]{:S(2)}, u32[]{:S(2)}) %collective-permute-start.1) | collective-permute-done | bytes 262176 | tf_op jit(solution)/shard_map/ppermute | solution.py:15
  21.7 0.6 pad_maximum_fusion
  22.4 1.3 %collective-permute-start.3 = (bf16[2,24,1024]{2,1,0:T(8,128)(2,1)S(1)}, bf16[2,24,1024]{2,1,0:T(8,128)(2,1)S(1)}, u32[]{:S(2)}, u32[]{:S(2)}) collective-permute-start(bf16[2,24,1024]{2,1,0:T(8,128)(2,1)S(1)} %pad_maximum_fusion.3), channel_id=1, source_target_pairs={{32,0},{64,32},{96,64},{128,96},{160,128},{192,160},{224,192},{33,... | collective-permute-start | bytes 294920 | tf_op jit(solution)/shard_map/ppermute | solution.py:15
  23.7 3.0 %collective-permute-start.2 = (bf16[2,24,1024]{2,1,0:T(8,128)(2,1)S(1)}, bf16[2,24,1024]{2,1,0:T(8,128)(2,1)S(1)}, u32[]{:S(2)}, u32[]{:S(2)}) collective-permute-start(bf16[2,24,1024]{2,1,0:T(8,128)(2,1)S(1)} %pad_maximum_fusion.2), channel_id=1, source_target_pairs={{0,32},{32,64},{64,96},{96,128},{128,160},{160,192},{192,224},{1,3... | collective-permute-start | bytes 294920 | tf_op jit(solution)/shard_map/ppermute | solution.py:15
  26.8 0.0 copy-done
  26.8 30.9 %shard_map.46 = (f32[3,16,1024]{2,1,0:T(8,128)S(1)}, f32[16,1024]{1,0:T(8,128)S(1)}, f32[16,1024]{1,0:T(8,128)S(1)}) custom-call(f32[10,16]{1,0:T(8,128)S(1)} %stack.62.refs_0_, s32[4]{0:T(128)S(1)} %add_convert_fusion.refs_1_, bf16[64,16,1024]{2,1,0:T(8,128)(2,1)S(1)} %copy-done, f32[64,8,1024]{2,1,0:T(8,128)S(1)} %get-tuple-element.32.refs_3_), custom_call_target="tpu_custom_call" | custom-call | tf_op jit(solution)/shard_map/pallas_call | solution.py:192
  57.7 0.0 collective-permute-done.3
  57.8 0.0 collective-permute-done.2
  57.9 2.8 %shard_map.47 = (f32[3,16,1024]{2,1,0:T(8,128)S(1)}, f32[16,1024]{1,0:T(8,128)S(1)}) custom-call(f32[10,16]{1,0:T(8,128)S(1)} %stack.62.refs_0_, s32[4]{0:T(128)S(1)} %add_convert_fusion.refs_1_, f32[6,24,1024]{2,1,0:T(8,128)S(1)} %maximum_maximum_fusion.refs_2_, f32[6,24,1024]{2,1,0:T(8,128)S(1)} %pad_maximum_fusion.1.refs_3_, ...), custom_call_target="tpu_custom_call" | custom-call | tf_op jit(solution)/shard_map/pallas_call | solution.py:200
  60.8 12.0 %all_to_all.5 = f32[8,4,16,128]{3,2,1,0:T(8,128)S(1)} all-to-all(f32[8,4,16,128]{3,2,1,0:T(8,128)S(1)} %maximum_bitcast_fusion), channel_id=1, replica_groups=mesh['depth'=8,'tile'=32] {'depth'}, dimensions={0} | all-to-all | bytes 524288 | tf_op jit(solution)/shard_map/all_to_all | solution.py:233
  72.9 0.6 pad_maximum_fusion.4
  (27 shorter events, 0.4 us)
Async XLA Ops:
  2.0 15.5 %collective-permute-start = (bf16[64,2,1024]{2,1,0:T(2,128)(2,1)S(1)}, bf16[64,2,1024]{2,1,0:T(2,128)(2,1)S(1)}, u32[]{:S(2)}, u32[]{:S(2)}) collective-permute-start(bf16[64,2,1024]{2,1,0:T(2,128)(2,1)S(1)} %get-tuple-element.27), channel_id=1, source_target_pairs={{1,0},{2,1},{3,2},{4,3},{5,4},{6,5},{7,6},{8,7},{9,8},{10,9},{11,1... | collective-permute-start | bytes 786440 | tf_op jit(solution)/shard_map/ppermute | solution.py:15
  9.9 11.8 %collective-permute-start.1 = (bf16[64,2,1024]{2,1,0:T(2,128)(2,1)S(1)}, bf16[64,2,1024]{2,1,0:T(2,128)(2,1)S(1)}, u32[]{:S(2)}, u32[]{:S(2)}) collective-permute-start(bf16[64,2,1024]{2,1,0:T(2,128)(2,1)S(1)} %get-tuple-element.28), channel_id=1, source_target_pairs={{0,1},{1,2},{2,3},{3,4},{4,5},{5,6},{6,7},{7,8},{8,9},{9,10},{10,1... | collective-permute-start | bytes 786440 | tf_op jit(solution)/shard_map/ppermute | solution.py:15
  17.5 9.3 %copy-start = (bf16[64,16,1024]{2,1,0:T(8,128)(2,1)S(1)}, bf16[64,16,1024]{2,1,0:T(8,128)(2,1)}, u32[]{:S(2)}) copy-start(bf16[64,16,1024]{2,1,0:T(8,128)(2,1)} %refs_2_.1) | copy-start | bytes 6291460
  22.4 35.4 %collective-permute-start.3 = (bf16[2,24,1024]{2,1,0:T(8,128)(2,1)S(1)}, bf16[2,24,1024]{2,1,0:T(8,128)(2,1)S(1)}, u32[]{:S(2)}, u32[]{:S(2)}) collective-permute-start(bf16[2,24,1024]{2,1,0:T(8,128)(2,1)S(1)} %pad_maximum_fusion.3), channel_id=1, source_target_pairs={{32,0},{64,32},{96,64},{128,96},{160,128},{192,160},{224,192},{33,... | collective-permute-start | bytes 294920 | tf_op jit(solution)/shard_map/ppermute | solution.py:15
  23.7 34.1 %collective-permute-start.2 = (bf16[2,24,1024]{2,1,0:T(8,128)(2,1)S(1)}, bf16[2,24,1024]{2,1,0:T(8,128)(2,1)S(1)}, u32[]{:S(2)}, u32[]{:S(2)}) collective-permute-start(bf16[2,24,1024]{2,1,0:T(8,128)(2,1)S(1)} %pad_maximum_fusion.2), channel_id=1, source_target_pairs={{0,32},{32,64},{64,96},{96,128},{128,160},{160,192},{192,224},{1,3... | collective-permute-start | bytes 294920 | tf_op jit(solution)/shard_map/ppermute | solution.py:15

commit v11 on v10

--- a/solution.py
+++ b/solution.py
@@ -140,13 +140,13 @@
 
 def edge_kernel(table, flags, front_ref, back_ref, color_ref, depth_ref, trans_ref,
                 out_color_ref, out_depth_ref, *, segments, rows):
-    span, tall, lanes = front_ref.shape
+    tall, lanes = front_ref.shape[1:]
     keep = row_keep(flags, tall, lanes, rows)
     palette = Palette(table, segments)
 
-    def side(ref, outside):
+    def cells_of(ref, outside):
         smoothed = []
-        for i in range(1, span - 1):
+        for i in range(1, ref.shape[0] - 1):
             inside = keep & ~outside(i)
             smoothed.append(smooth_plane(ref[i - 1], ref[i], ref[i + 1], inside, rows))
         cells = []
@@ -155,16 +155,10 @@
                                       smoothed[j][1], smoothed[j][2]))
         return cells
 
-    front = side(front_ref, lambda i: (i == 1) & (flags[0] == 1))
-    back = side(back_ref, lambda i: (i == span - 2) & (flags[1] == 1))
-    mid_color = [color_ref[c] for c in range(3)]
-    mid_depth = depth_ref[...]
-    mid_trans = trans_ref[...]
-    color = [jnp.zeros((rows, lanes), jnp.float32) for c in range(3)]
-    total = jnp.zeros((rows, lanes), jnp.float32)
-    trans = jnp.ones((rows, lanes), jnp.float32)
-
-    def add_cells(cells, color, total, trans):
+    def segment(cells):
+        color = [jnp.zeros((rows, lanes), jnp.float32) for c in range(3)]
+        total = jnp.zeros((rows, lanes), jnp.float32)
+        trans = jnp.ones((rows, lanes), jnp.float32)
         for shade, chan in cells:
             fade = jnp.exp(-chan[3])
             weight = shade * (1.0 - fade) * trans
@@ -173,14 +167,28 @@
             trans = trans * fade
         return color, total, trans
 
-    color, total, trans = add_cells(front, color, total, trans)
-    color = [color[c] + trans * mid_color[c] for c in range(3)]
-    total = total + mid_depth
-    trans = trans * mid_trans
-    color, total, trans = add_cells(back, color, total, trans)
+    def join(a, b):
+        return ([a[0][c] + a[2] * b[0][c] for c in range(3)], a[1] + b[1], a[2] * b[2])
+
+    def only_if(flag, seg):
+        color, total, trans = seg
+        return ([jnp.where(flag, color[c], 0.0) for c in range(3)],
+                jnp.where(flag, total, 0.0), jnp.where(flag, trans, 1.0))
+
+    first = flags[0] == 1
+    last = flags[1] == 1
+    front = segment(cells_of(front_ref, lambda i: i == 1))
+    span = back_ref.shape[0]
+    back_cells = cells_of(back_ref, lambda i: (i >= span - 4) & last)
+    own_back = segment(back_cells[:EDGE])
+    next_front = segment(back_cells[EDGE:])
+    middle = ([color_ref[c] for c in range(3)], depth_ref[...], trans_ref[...])
+    result = join(only_if(first, front), middle)
+    result = join(result, own_back)
+    result = join(result, only_if(~last, next_front))
     for c in range(3):
-        out_color_ref[c] = color[c]
-    out_depth_ref[...] = total
+        out_color_ref[c] = result[0][c]
+    out_depth_ref[...] = result[1]
 
 
 def render_block(table, flags, volume, side, front, back, rows, segments):
@@ -217,10 +225,9 @@
     planes = lambda a, b: jnp.concatenate([volume[a:b].astype(jnp.float32), side[a:b]], axis=1)
     sides = jnp.concatenate([x_high, gap, x_low], axis=1)
     narrow = lambda a, b: jnp.concatenate([volume[a:b], sides[a:b]], axis=1)
-    z_low = shifted(narrow(depth - 2, depth), "depth", 1).astype(jnp.float32)
-    z_high = shifted(narrow(0, 2), "depth", -1).astype(jnp.float32)
-    front = jnp.concatenate([z_low, planes(0, EDGE + 2)], axis=0)
-    back = jnp.concatenate([planes(depth - EDGE - 2, depth), z_high], axis=0)
+    z_next = shifted(narrow(0, 2 * EDGE), "depth", -1).astype(jnp.float32)
+    front = jnp.concatenate([jnp.zeros_like(z_next[:2]), planes(0, EDGE + 2)], axis=0)
+    back = jnp.concatenate([planes(depth - 2 * EDGE, depth), z_next], axis=0)
     d = lax.axis_index("depth")
     t = lax.axis_index("tile")
     flags = jnp.stack([d == 0, d == depth_count - 1, t == 0, t == lax.axis_size("tile") - 1])

time: 73.9 us -> 72 us (0.974)
  starting transfers between devices: 14.2 us -> 11.2 us
  Pallas kernels: 33.7 us -> 34.7 us
  waiting for transfers between devices: 4.18 us -> 5.1 us
  local copies, waits for them, and re-layouts: 3.69 us -> 2.78 us
    ppermute x4 -> x3, starting transfers between devices: 14.2 us -> 11.2 us  [shifted(): return lax.ppermute(block, axis, pairs)]
    pallas_call x1, Pallas kernels: 2.8 us -> 3.74 us  [render_block(): pl.pallas_call(lambda *refs: edge_kernel(*refs, segments=segments, rows=r...]
    ppermute x4 -> x3, waiting for transfers between devices: 4.18 us -> 5.1 us  [shifted(): return lax.ppermute(block, axis, pairs)]
    slice x2 -> x1, local copies, waits for them, and re-layouts: 0.89 us -> 0.01 us  [body(): narrow = lambda a, b: jnp.concatenate([volume[a:b], sides[a:b]], axis=1)]
  transfers between devices with their start and end apart: 4 -> 3, of which waited for: 1 -> 1; matrix products, arithmetic and copies ran while one was open for 8% -> 7% of each run, Pallas kernels for 42% -> 43%
where the time goes in v11:
time: 72 us; the launch traced here: 71.7 us
  Pallas kernels  34.7 us (48%)
  blocking collectives  12.3 us (17%)
  starting transfers between devices  11.2 us (16%)
  other arithmetic  5.42 us (8%)
  waiting for transfers between devices  5.1 us (7%)
  local copies, waits for them, and re-layouts  2.78 us (4%)
    pallas_call x1, Pallas kernels, render_block(): pl.pallas_call(lambda *refs: middle_kernel(*refs, segments=segments, rows...  30.9 us
    all_to_all x1, blocking collectives, body(): blocks = lax.all_to_all(weighted, 'depth', 0, 0, tiled=True)  12.3 us
    ppermute x3, starting transfers between devices, shifted(): return lax.ppermute(block, axis, pairs)  11.2 us
    ppermute x3, waiting for transfers between devices, shifted(): return lax.ppermute(block, axis, pairs)  5.1 us
    pallas_call x1, Pallas kernels, render_block(): pl.pallas_call(lambda *refs: edge_kernel(*refs, segments=segments, rows=r...  3.74 us
    slice x1, local copies, waits for them, and re-layouts, body(): x_high = shifted(volume[:, :2], 'tile', -1)  1.99 us
  transfers between devices with their start and end apart: 3, of which 1 were waited for; matrix products, arithmetic and copies ran while one was open for 7% of the time, Pallas kernels for 43%

profile of v11, /device:TPU:24, one launch (start us, length us, event | category | flops | bytes accessed | tf_op | source)
XLA Modules:
  0.0 71.7 jit_solution(2593151264213272250)
XLA Ops:
  0.0 2.0 %fusion.22 = (bf16[64,2,1024]{2,1,0:T(2,128)(2,1)S(1)}, bf16[64,2,1024]{2,1,0:T(2,128)(2,1)S(1)}) fusion(bf16[64,16,1024]{2,1,0:T(8,128)(2,1)} %refs_2_.1), kind=kLoop, calls=%fused_computation.78 | loop fusion | bytes 1048576 | tf_op jit(solution)/shard_map/slice | solution.py:222
  2.0 7.9 %collective-permute-start = (bf16[64,2,1024]{2,1,0:T(2,128)(2,1)S(1)}, bf16[64,2,1024]{2,1,0:T(2,128)(2,1)S(1)}, u32[]{:S(2)}, u32[]{:S(2)}) collective-permute-start(bf16[64,2,1024]{2,1,0:T(2,128)(2,1)S(1)} %get-tuple-element.26), channel_id=1, source_target_pairs={{1,0},{2,1},{3,2},{4,3},{5,4},{6,5},{7,6},{8,7},{9,8},{10,9},{11,1... | collective-permute-start | bytes 786440 | tf_op jit(solution)/shard_map/ppermute | solution.py:15
  9.9 1.9 %collective-permute-start.1 = (bf16[64,2,1024]{2,1,0:T(2,128)(2,1)S(1)}, bf16[64,2,1024]{2,1,0:T(2,128)(2,1)S(1)}, u32[]{:S(2)}, u32[]{:S(2)}) collective-permute-start(bf16[64,2,1024]{2,1,0:T(2,128)(2,1)S(1)} %get-tuple-element.27), channel_id=1, source_target_pairs={{0,1},{1,2},{2,3},{3,4},{4,5},{5,6},{6,7},{7,8},{8,9},{9,10},{10,1... | collective-permute-start | bytes 786440 | tf_op jit(solution)/shard_map/ppermute | solution.py:15
  11.9 0.7 fusion.24
  12.5 0.1 slice_subtract_fusion
  12.6 0.6 fusion.23
  13.2 0.8 %convert_multiply_fusion = f32[4,16]{1,0:T(4,128)S(1)} fusion(s32[4,16]{1,0:T(4,128)} %param.6, f32[4]{0:T(128)} %constant.49), kind=kLoop, calls=%fused_computation.51 | loop fusion | flops 128 | bytes 528 | tf_op jit(solution)/shard_map/mul | solution.py:21
  13.9 0.1 multiply_subtract_fusion
  14.1 1.3 %fusion.19 = f32[1,16]{1,0:T(1,128)S(1)} fusion(f32[1]{0:T(128)} %get-tuple-element.45, f32[1]{0:T(128)} %get-tuple-element.44), kind=kLoop, calls=%fused_computation.73 | loop fusion | flops 64 | bytes 72 | tf_op jit(solution)/shard_map/stack | solution.py:30
  15.4 0.1 add_convert_fusion.refs_1_
  15.4 0.1 pad.51.clone
  15.6 1.0 %slice_convert_fusion = (f32[4,16,1024]{2,1,0:T(8,128)S(1)}, f32[4,16,1024]{2,1,0:T(8,128)S(1)}, bf16[4,16,1024]{2,1,0:T(8,128)(2,1)S(1)}) fusion(bf16[64,16,1024]{2,1,0:T(8,128)(2,1)} %refs_2_.1), kind=kLoop, calls=%fused_computation.7 | loop fusion | flops 131072 | bytes 917504 | tf_op jit(solution)/shard_map/convert_element_type | solution.py:225
  16.6 0.0 copy-start
  16.6 0.0 collective-permute-done
  16.6 5.1 %collective-permute-done.1 = bf16[64,2,1024]{2,1,0:T(2,128)(2,1)S(1)} collective-permute-done((bf16[64,2,1024]{2,1,0:T(2,128)(2,1)S(1)}, bf16[64,2,1024]{2,1,0:T(2,128)(2,1)S(1)}, u32[]{:S(2)}, u32[]{:S(2)}) %collective-permute-start.1) | collective-permute-done | bytes 262176 | tf_op jit(solution)/shard_map/ppermute | solution.py:15
  21.7 0.6 pad_maximum_fusion
  22.4 1.3 %collective-permute-start.2 = (bf16[4,24,1024]{2,1,0:T(8,128)(2,1)S(1)}, bf16[4,24,1024]{2,1,0:T(8,128)(2,1)S(1)}, u32[]{:S(2)}, u32[]{:S(2)}) collective-permute-start(bf16[4,24,1024]{2,1,0:T(8,128)(2,1)S(1)} %pad_maximum_fusion.2), channel_id=1, source_target_pairs={{32,0},{64,32},{96,64},{128,96},{160,128},{192,160},{224,192},{33,... | collective-permute-start | bytes 589832 | tf_op jit(solution)/shard_map/ppermute | solution.py:15
  23.7 0.0 copy-done
  23.7 30.9 %shard_map.46 = (f32[3,16,1024]{2,1,0:T(8,128)S(1)}, f32[16,1024]{1,0:T(8,128)S(1)}, f32[16,1024]{1,0:T(8,128)S(1)}) custom-call(f32[10,16]{1,0:T(8,128)S(1)} %stack.62.refs_0_, s32[4]{0:T(128)S(1)} %add_convert_fusion.refs_1_, bf16[64,16,1024]{2,1,0:T(8,128)(2,1)S(1)} %copy-done, f32[64,8,1024]{2,1,0:T(8,128)S(1)} %get-tuple-element.29.refs_3_), custom_call_target="tpu_custom_call" | custom-call | tf_op jit(solution)/shard_map/pallas_call | solution.py:200
  54.7 0.0 collective-permute-done.2
  54.8 0.1 pad_maximum_fusion.1.refs_3_
  54.9 3.7 %shard_map.47 = (f32[3,16,1024]{2,1,0:T(8,128)S(1)}, f32[16,1024]{1,0:T(8,128)S(1)}) custom-call(f32[10,16]{1,0:T(8,128)S(1)} %stack.62.refs_0_, s32[4]{0:T(128)S(1)} %add_convert_fusion.refs_1_, f32[6,24,1024]{2,1,0:T(8,128)S(1)} %select_maximum_fusion.refs_2_, f32[8,24,1024]{2,1,0:T(8,128)S(1)} %pad_maximum_fusion.1.refs_3_, ...), custom_call_target="tpu_custom_call" | custom-call | tf_op jit(solution)/shard_map/pallas_call | solution.py:208
  58.7 12.3 %all_to_all.5 = f32[8,4,16,128]{3,2,1,0:T(8,128)S(1)} all-to-all(f32[8,4,16,128]{3,2,1,0:T(8,128)S(1)} %maximum_bitcast_fusion), channel_id=1, replica_groups=mesh['depth'=8,'tile'=32] {'depth'}, dimensions={0} | all-to-all | bytes 524288 | tf_op jit(solution)/shard_map/all_to_all | solution.py:240
  71.1 0.6 pad_maximum_fusion.3
  (24 shorter events, 0.3 us)
Async XLA Ops:
  2.0 14.6 %collective-permute-start = (bf16[64,2,1024]{2,1,0:T(2,128)(2,1)S(1)}, bf16[64,2,1024]{2,1,0:T(2,128)(2,1)S(1)}, u32[]{:S(2)}, u32[]{:S(2)}) collective-permute-start(bf16[64,2,1024]{2,1,0:T(2,128)(2,1)S(1)} %get-tuple-element.26), channel_id=1, source_target_pairs={{1,0},{2,1},{3,2},{4,3},{5,4},{6,5},{7,6},{8,7},{9,8},{10,9},{11,1... | collective-permute-start | bytes 786440 | tf_op jit(solution)/shard_map/ppermute | solution.py:15
  9.9 11.8 %collective-permute-start.1 = (bf16[64,2,1024]{2,1,0:T(2,128)(2,1)S(1)}, bf16[64,2,1024]{2,1,0:T(2,128)(2,1)S(1)}, u32[]{:S(2)}, u32[]{:S(2)}) collective-permute-start(bf16[64,2,1024]{2,1,0:T(2,128)(2,1)S(1)} %get-tuple-element.27), channel_id=1, source_target_pairs={{0,1},{1,2},{2,3},{3,4},{4,5},{5,6},{6,7},{7,8},{8,9},{9,10},{10,1... | collective-permute-start | bytes 786440 | tf_op jit(solution)/shard_map/ppermute | solution.py:15
  16.6 7.1 %copy-start = (bf16[64,16,1024]{2,1,0:T(8,128)(2,1)S(1)}, bf16[64,16,1024]{2,1,0:T(8,128)(2,1)}, u32[]{:S(2)}) copy-start(bf16[64,16,1024]{2,1,0:T(8,128)(2,1)} %refs_2_.1) | copy-start | bytes 6291460
  22.4 32.3 %collective-permute-start.2 = (bf16[4,24,1024]{2,1,0:T(8,128)(2,1)S(1)}, bf16[4,24,1024]{2,1,0:T(8,128)(2,1)S(1)}, u32[]{:S(2)}, u32[]{:S(2)}) collective-permute-start(bf16[4,24,1024]{2,1,0:T(8,128)(2,1)S(1)} %pad_maximum_fusion.2), channel_id=1, source_target_pairs={{32,0},{64,32},{96,64},{128,96},{160,128},{192,160},{224,192},{33,... | collective-permute-start | bytes 589832 | tf_op jit(solution)/shard_map/ppermute | solution.py:15

commit v12 on v11

--- a/solution.py
+++ b/solution.py
@@ -91,7 +91,7 @@
 
 
 def middle_kernel(table, flags, volume_ref, side_ref, color_ref, depth_ref, trans_ref,
-                  smooth_ref, square_ref, facing_ref, *, segments, rows, width):
+                  kept_ref, terms_ref, smooth_ref, square_ref, facing_ref, *, segments, rows, width):
     depth, _, lanes = volume_ref.shape
     tall = rows + side_ref.shape[1]
     keep = row_keep(flags, tall, lanes, rows)[rows:]
@@ -107,6 +107,11 @@
         return carry
 
     lax.fori_loop(1, depth - 1, plane, 0, unroll=2)
+    for n, i in enumerate((1, 2, depth - 3, depth - 2)):
+        kept_ref[n] = smooth_ref[i]
+    for n, i in enumerate((1, depth - 2)):
+        terms_ref[2 * n] = square_ref[i]
+        terms_ref[2 * n + 1] = facing_ref[i]
     palette = Palette(table, segments)
     sub = 8
     for r0 in range(0, rows, sub):
@@ -138,22 +143,27 @@
             trans_ref[rs, cs] = trans
 
 
-def edge_kernel(table, flags, front_ref, back_ref, color_ref, depth_ref, trans_ref,
-                out_color_ref, out_depth_ref, *, segments, rows):
+def edge_kernel(table, flags, front_ref, back_ref, kept_ref, terms_ref, color_ref, depth_ref,
+                trans_ref, out_color_ref, out_depth_ref, *, segments, rows):
     tall, lanes = front_ref.shape[1:]
     keep = row_keep(flags, tall, lanes, rows)
     palette = Palette(table, segments)
-
-    def cells_of(ref, outside):
-        smoothed = []
-        for i in range(1, ref.shape[0] - 1):
-            inside = keep & ~outside(i)
-            smoothed.append(smooth_plane(ref[i - 1], ref[i], ref[i + 1], inside, rows))
-        cells = []
-        for j in range(1, len(smoothed) - 1):
-            cells.append(palette.cell(smoothed[j - 1][0], smoothed[j][0], smoothed[j + 1][0],
-                                      smoothed[j][1], smoothed[j][2]))
-        return cells
+    first = flags[0] == 1
+    last = flags[1] == 1
+    zero = jnp.zeros((rows, lanes), jnp.float32)
+    s0, q0, f0 = smooth_plane(jnp.zeros((tall, lanes), jnp.float32), front_ref[0], front_ref[1],
+                              keep, rows)
+    s1, s2, s61, s62 = [kept_ref[n] for n in range(4)]
+    q1, f1, q62, f62 = [terms_ref[n] for n in range(4)]
+    front_cells = [palette.cell(zero, s0, s1, q0, f0), palette.cell(s0, s1, s2, q1, f1)]
+    smoothed = [(s61, None, None), (s62, q62, f62)]
+    for i in range(1, back_ref.shape[0] - 1):
+        inside = keep & ~((i >= 2) & last)
+        smoothed.append(smooth_plane(back_ref[i - 1], back_ref[i], back_ref[i + 1], inside, rows))
+    back_cells = []
+    for j in range(1, len(smoothed) - 1):
+        back_cells.append(palette.cell(smoothed[j - 1][0], smoothed[j][0], smoothed[j + 1][0],
+                                       smoothed[j][1], smoothed[j][2]))
 
     def segment(cells):
         color = [jnp.zeros((rows, lanes), jnp.float32) for c in range(3)]
@@ -175,11 +185,7 @@
         return ([jnp.where(flag, color[c], 0.0) for c in range(3)],
                 jnp.where(flag, total, 0.0), jnp.where(flag, trans, 1.0))
 
-    first = flags[0] == 1
-    last = flags[1] == 1
-    front = segment(cells_of(front_ref, lambda i: i == 1))
-    span = back_ref.shape[0]
-    back_cells = cells_of(back_ref, lambda i: (i >= span - 4) & last)
+    front = segment(front_cells)
     own_back = segment(back_cells[:EDGE])
     next_front = segment(back_cells[EDGE:])
     middle = ([color_ref[c] for c in range(3)], depth_ref[...], trans_ref[...])
@@ -200,18 +206,20 @@
     middle = pl.pallas_call(
         lambda *refs: middle_kernel(*refs, segments=segments, rows=rows, width=256),
         in_specs=[smem, smem, vmem, vmem],
-        out_specs=[vmem, vmem, vmem],
-        out_shape=[color_shape, plane_shape, plane_shape],
+        out_specs=[vmem] * 5,
+        out_shape=[color_shape, plane_shape, plane_shape,
+                   jax.ShapeDtypeStruct((4, rows, lanes), jnp.float32),
+                   jax.ShapeDtypeStruct((4, rows, lanes), jnp.float32)],
         scratch_shapes=[pltpu.VMEM((depth, rows, lanes), jnp.float32) for _ in range(3)],
         compiler_params=pltpu.CompilerParams(vmem_limit_bytes=48 * 1024 * 1024),
     )(table, flags, volume, side)
     return pl.pallas_call(
         lambda *refs: edge_kernel(*refs, segments=segments, rows=rows),
-        in_specs=[smem, smem] + [vmem] * 5,
+        in_specs=[smem, smem] + [vmem] * 7,
         out_specs=[vmem, vmem],
         out_shape=[color_shape, plane_shape],
         compiler_params=pltpu.CompilerParams(vmem_limit_bytes=48 * 1024 * 1024),
-    )(table, flags, front, back, *middle)
+    )(table, flags, front, back, middle[3], middle[4], *middle[:3])
 
 
 def body(volume, knot_pos, knot_color):
@@ -226,8 +234,8 @@
     sides = jnp.concatenate([x_high, gap, x_low], axis=1)
     narrow = lambda a, b: jnp.concatenate([volume[a:b], sides[a:b]], axis=1)
     z_next = shifted(narrow(0, 2 * EDGE), "depth", -1).astype(jnp.float32)
-    front = jnp.concatenate([jnp.zeros_like(z_next[:2]), planes(0, EDGE + 2)], axis=0)
-    back = jnp.concatenate([planes(depth - 2 * EDGE, depth), z_next], axis=0)
+    front = planes(0, 2)
+    back = jnp.concatenate([planes(depth - 2, depth), z_next], axis=0)
     d = lax.axis_index("depth")
     t = lax.axis_index("tile")
     flags = jnp.stack([d == 0, d == depth_count - 1, t == 0, t == lax.axis_size("tile") - 1])

time: 72 us -> 67.8 us (0.942)
  waiting for transfers between devices: 5.1 us -> 0.64 us
    ppermute x3, waiting for transfers between devices: 5.1 us -> 0.64 us  [shifted(): return lax.ppermute(block, axis, pairs)]
  transfers between devices with their start and end apart: 3 -> 3, of which waited for: 1 -> 1; matrix products, arithmetic and copies ran while one was open for 7% -> 7% of each run, Pallas kernels for 43% -> 46%
where the time goes in v12:
time: 67.8 us; the launch traced here: 67 us
  Pallas kernels  34.3 us (51%)
  blocking collectives  12.3 us (18%)
  starting transfers between devices  11.2 us (17%)
  other arithmetic  5.42 us (8%)
  local copies, waits for them, and re-layouts  2.89 us (4%)
    pallas_call x1, Pallas kernels, render_block(): pl.pallas_call(lambda *refs: middle_kernel(*refs, segments=segments, rows...  31 us
    all_to_all x1, blocking collectives, body(): blocks = lax.all_to_all(weighted, 'depth', 0, 0, tiled=True)  12.3 us
    ppermute x3, starting transfers between devices, shifted(): return lax.ppermute(block, axis, pairs)  11.2 us
    pallas_call x1, Pallas kernels, render_block(): pl.pallas_call(lambda *refs: edge_kernel(*refs, segments=segments, rows=r...  3.35 us
    slice x1, local copies, waits for them, and re-layouts, body(): x_high = shifted(volume[:, :2], 'tile', -1)  1.99 us
    another operation x1, other arithmetic, ramp_table(): return jnp.stack(rows)  1.41 us
  transfers between devices with their start and end apart: 3, of which 1 were waited for; matrix products, arithmetic and copies ran while one was open for 7% of the time, Pallas kernels for 46%

profile of v12, /device:TPU:24, one launch (start us, length us, event | category | flops | bytes accessed | tf_op | source)
XLA Modules:
  0.0 67.0 jit_solution(167885327212046648)
XLA Ops:
  0.0 2.0 %fusion.22 = (bf16[64,2,1024]{2,1,0:T(2,128)(2,1)S(1)}, bf16[64,2,1024]{2,1,0:T(2,128)(2,1)S(1)}) fusion(bf16[64,16,1024]{2,1,0:T(8,128)(2,1)} %refs_2_.1), kind=kLoop, calls=%fused_computation.77 | loop fusion | bytes 1048576 | tf_op jit(solution)/shard_map/slice | solution.py:230
  2.0 3.8 %collective-permute-start.1 = (bf16[64,2,1024]{2,1,0:T(2,128)(2,1)S(1)}, bf16[64,2,1024]{2,1,0:T(2,128)(2,1)S(1)}, u32[]{:S(2)}, u32[]{:S(2)}) collective-permute-start(bf16[64,2,1024]{2,1,0:T(2,128)(2,1)S(1)} %get-tuple-element.30), channel_id=1, source_target_pairs={{0,1},{1,2},{2,3},{3,4},{4,5},{5,6},{6,7},{7,8},{8,9},{9,10},{10,1... | collective-permute-start | bytes 786440 | tf_op jit(solution)/shard_map/ppermute | solution.py:15
  5.8 6.0 %collective-permute-start = (bf16[64,2,1024]{2,1,0:T(2,128)(2,1)S(1)}, bf16[64,2,1024]{2,1,0:T(2,128)(2,1)S(1)}, u32[]{:S(2)}, u32[]{:S(2)}) collective-permute-start(bf16[64,2,1024]{2,1,0:T(2,128)(2,1)S(1)} %get-tuple-element.29), channel_id=1, source_target_pairs={{1,0},{2,1},{3,2},{4,3},{5,4},{6,5},{7,6},{8,7},{9,8},{10,9},{11,1... | collective-permute-start | bytes 786440 | tf_op jit(solution)/shard_map/ppermute | solution.py:15
  11.9 0.7 fusion.24
  12.5 0.1 slice_subtract_fusion
  12.6 0.7 fusion.23
  13.3 0.8 %convert_multiply_fusion = f32[4,16]{1,0:T(4,128)S(1)} fusion(s32[4,16]{1,0:T(4,128)} %param.6, f32[4]{0:T(128)} %constant.46), kind=kLoop, calls=%fused_computation.51 | loop fusion | flops 128 | bytes 528 | tf_op jit(solution)/shard_map/mul | solution.py:21
  14.0 0.1 multiply_subtract_fusion
  14.2 1.4 %fusion.19 = f32[1,16]{1,0:T(1,128)S(1)} fusion(f32[1]{0:T(128)} %get-tuple-element.48, f32[1]{0:T(128)} %get-tuple-element.47), kind=kLoop, calls=%fused_computation.73 | loop fusion | flops 64 | bytes 72 | tf_op jit(solution)/shard_map/stack | solution.py:30
  15.6 0.1 add_convert_fusion.refs_1_
  15.7 0.1 pad.50.clone
  15.8 0.0 slice-start
  15.8 0.9 %slice_convert_fusion = (f32[2,16,1024]{2,1,0:T(8,128)S(1)}, f32[2,16,1024]{2,1,0:T(8,128)S(1)}) fusion(bf16[64,16,1024]{2,1,0:T(8,128)(2,1)} %refs_2_.1), kind=kLoop, calls=%fused_computation.6 | loop fusion | flops 65536 | bytes 393216 | tf_op jit(solution)/shard_map/convert_element_type | solution.py:233
  16.8 0.0 copy-start
  16.8 0.0 collective-permute-done.1
  16.8 0.6 collective-permute-done
  17.4 0.6 pad_maximum_fusion
  18.1 0.0 slice-done
  18.1 1.3 %collective-permute-start.2 = (bf16[4,24,1024]{2,1,0:T(8,128)(2,1)S(1)}, bf16[4,24,1024]{2,1,0:T(8,128)(2,1)S(1)}, u32[]{:S(2)}, u32[]{:S(2)}) collective-permute-start(bf16[4,24,1024]{2,1,0:T(8,128)(2,1)S(1)} %pad_maximum_fusion.3), channel_id=1, source_target_pairs={{32,0},{64,32},{96,64},{128,96},{160,128},{192,160},{224,192},{33,... | collective-permute-start | bytes 589832 | tf_op jit(solution)/shard_map/ppermute | solution.py:15
  19.4 0.0 copy-done
  19.4 31.0 %shard_map.46 = (f32[3,16,1024]{2,1,0:T(8,128)S(1)}, f32[16,1024]{1,0:T(8,128)S(1)}, f32[16,1024]{1,0:T(8,128)S(1)}, f32[4,16,1024]{2,1,0:T(8,128)S(1)}, f32[4,16,1024]{2,1,0:T(8,128)S(1)}) custom-call(f32[10,16]{1,0:T(8,128)S(1)} %stack.62.refs_0_, s32[4]{0:T(128)S(1)} %add_convert_fusion.refs_1_, bf16[64,16,1024]{2,1,0:T(8,128)(2,1)S(1)} %copy-done, ...), custom_call_target="tpu_custom_call" | custom-call | tf_op jit(solution)/shard_map/pallas_call | solution.py:206
  50.5 0.0 collective-permute-done.2
  50.6 3.4 %shard_map.47 = (f32[3,16,1024]{2,1,0:T(8,128)S(1)}, f32[16,1024]{1,0:T(8,128)S(1)}) custom-call(f32[10,16]{1,0:T(8,128)S(1)} %stack.62.refs_0_, s32[4]{0:T(128)S(1)} %add_convert_fusion.refs_1_, f32[2,24,1024]{2,1,0:T(8,128)S(1)} %pad_maximum_fusion.2.refs_2_, f32[6,24,1024]{2,1,0:T(8,128)S(1)} %pad_maximum_fusion.1.refs_3_, ...), custom_call_target="tpu_custom_call" | custom-call | tf_op jit(solution)/shard_map/pallas_call | solution.py:216
  54.0 12.3 %all_to_all.5 = f32[8,4,16,128]{3,2,1,0:T(8,128)S(1)} all-to-all(f32[8,4,16,128]{3,2,1,0:T(8,128)S(1)} %maximum_bitcast_fusion), channel_id=1, replica_groups=mesh['depth'=8,'tile'=32] {'depth'}, dimensions={0} | all-to-all | bytes 524288 | tf_op jit(solution)/shard_map/all_to_all | solution.py:248
  66.4 0.6 pad_maximum_fusion.4
  (25 shorter events, 0.3 us)
Async XLA Ops:
  2.0 14.8 %collective-permute-start.1 = (bf16[64,2,1024]{2,1,0:T(2,128)(2,1)S(1)}, bf16[64,2,1024]{2,1,0:T(2,128)(2,1)S(1)}, u32[]{:S(2)}, u32[]{:S(2)}) collective-permute-start(bf16[64,2,1024]{2,1,0:T(2,128)(2,1)S(1)} %get-tuple-element.30), channel_id=1, source_target_pairs={{0,1},{1,2},{2,3},{3,4},{4,5},{5,6},{6,7},{7,8},{8,9},{9,10},{10,1... | collective-permute-start | bytes 786440 | tf_op jit(solution)/shard_map/ppermute | solution.py:15
  5.8 11.6 %collective-permute-start = (bf16[64,2,1024]{2,1,0:T(2,128)(2,1)S(1)}, bf16[64,2,1024]{2,1,0:T(2,128)(2,1)S(1)}, u32[]{:S(2)}, u32[]{:S(2)}) collective-permute-start(bf16[64,2,1024]{2,1,0:T(2,128)(2,1)S(1)} %get-tuple-element.29), channel_id=1, source_target_pairs={{1,0},{2,1},{3,2},{4,3},{5,4},{6,5},{7,6},{8,7},{9,8},{10,9},{11,1... | collective-permute-start | bytes 786440 | tf_op jit(solution)/shard_map/ppermute | solution.py:15
  15.8 2.2 %slice-start = ((bf16[64,16,1024]{2,1,0:T(8,128)(2,1)}), bf16[4,16,1024]{2,1,0:T(8,128)(2,1)S(1)}, s32[]{:S(2)}) async-start(bf16[64,16,1024]{2,1,0:T(8,128)(2,1)} %refs_2_.1), calls=%async_computation.1 | async-start | bytes 262144 | tf_op jit(solution)/shard_map/slice | solution.py:235
  16.8 2.7 %copy-start = (bf16[64,16,1024]{2,1,0:T(8,128)(2,1)S(1)}, bf16[64,16,1024]{2,1,0:T(8,128)(2,1)}, u32[]{:S(2)}) copy-start(bf16[64,16,1024]{2,1,0:T(8,128)(2,1)} %refs_2_.1) | copy-start | bytes 6291460
  18.1 32.3 %collective-permute-start.2 = (bf16[4,24,1024]{2,1,0:T(8,128)(2,1)S(1)}, bf16[4,24,1024]{2,1,0:T(8,128)(2,1)S(1)}, u32[]{:S(2)}, u32[]{:S(2)}) collective-permute-start(bf16[4,24,1024]{2,1,0:T(8,128)(2,1)S(1)} %pad_maximum_fusion.3), channel_id=1, source_target_pairs={{32,0},{64,32},{96,64},{128,96},{160,128},{192,160},{224,192},{33,... | collective-permute-start | bytes 589832 | tf_op jit(solution)/shard_map/ppermute | solution.py:15

commit v13 on v12

--- a/solution.py
+++ b/solution.py
@@ -226,8 +226,8 @@
     depth_count = lax.axis_size("depth")
     depth, rows, width = volume.shape
     sigma_scale = 4.0 / (depth * depth_count)
-    x_low = shifted(volume[:, rows - 2:], "tile", 1)
-    x_high = shifted(volume[:, :2], "tile", -1)
+    x_low = shifted(volume[:, rows - 2:].transpose(1, 0, 2), "tile", 1).transpose(1, 0, 2)
+    x_high = shifted(volume[:, :2].transpose(1, 0, 2), "tile", -1).transpose(1, 0, 2)
     gap = jnp.zeros((depth, TALL - rows - 4, width), volume.dtype)
     side = jnp.concatenate([x_high, gap, x_low], axis=1).astype(jnp.float32)
     planes = lambda a, b: jnp.concatenate([volume[a:b].astype(jnp.float32), side[a:b]], axis=1)

time: 67.8 us -> 67.8 us (level)
    slice x1 -> x0, local copies, waits for them, and re-layouts: 1.99 us -> none  [body(): x_high = shifted(volume[:, :2], 'tile', -1)]
    transpose x0 -> x1, local copies, waits for them, and re-layouts: none -> 1.99 us  [body(): volume[:, :2].transpose(1, 0, 2)]
where the time goes in v13:
time: 67.8 us; the launch traced here: 67.1 us
  Pallas kernels  34.3 us (51%)
  blocking collectives  12.3 us (18%)
  starting transfers between devices  11.2 us (17%)
  other arithmetic  5.42 us (8%)
  local copies, waits for them, and re-layouts  2.88 us (4%)
    pallas_call x1, Pallas kernels, render_block(): pl.pallas_call(lambda *refs: middle_kernel(*refs, segments=segments, rows...  31 us
    all_to_all x1, blocking collectives, body(): blocks = lax.all_to_all(weighted, 'depth', 0, 0, tiled=True)  12.3 us
    ppermute x3, starting transfers between devices, shifted(): return lax.ppermute(block, axis, pairs)  11.2 us
    pallas_call x1, Pallas kernels, render_block(): pl.pallas_call(lambda *refs: edge_kernel(*refs, segments=segments, rows=r...  3.35 us
    transpose x1, local copies, waits for them, and re-layouts, body(): volume[:, :2].transpose(1, 0, 2)  1.99 us
    another operation x1, other arithmetic, ramp_table(): return jnp.stack(rows)  1.41 us
  transfers between devices with their start and end apart: 3, of which 1 were waited for; matrix products, arithmetic and copies ran while one was open for 7% of the time, Pallas kernels for 46%

profile of v13, /device:TPU:24, one launch (start us, length us, event | category | flops | bytes accessed | tf_op | source)
XLA Modules:
  0.0 67.1 jit_solution(5458520138409291830)
XLA Ops:
  0.0 2.0 %slice_bitcast_fusion.1 = (bf16[2,64,1024]{2,0,1:T(2,128)(2,1)S(1)}, bf16[2,64,1024]{2,0,1:T(2,128)(2,1)S(1)}) fusion(bf16[64,16,1024]{2,1,0:T(8,128)(2,1)} %refs_2_.1), kind=kLoop, calls=%fused_computation.4 | loop fusion | bytes 1048576 | tf_op jit(solution)/shard_map/transpose | solution.py:230
  2.0 3.8 %collective-permute-start.1 = (bf16[2,64,1024]{2,0,1:T(2,128)(2,1)S(1)}, bf16[2,64,1024]{2,0,1:T(2,128)(2,1)S(1)}, u32[]{:S(2)}, u32[]{:S(2)}) collective-permute-start(bf16[2,64,1024]{2,0,1:T(2,128)(2,1)S(1)} %get-tuple-element.30), channel_id=1, source_target_pairs={{0,1},{1,2},{2,3},{3,4},{4,5},{5,6},{6,7},{7,8},{8,9},{9,10},{10,1... | collective-permute-start | bytes 786440 | tf_op jit(solution)/shard_map/ppermute | solution.py:15
  5.8 6.0 %collective-permute-start = (bf16[2,64,1024]{2,0,1:T(2,128)(2,1)S(1)}, bf16[2,64,1024]{2,0,1:T(2,128)(2,1)S(1)}, u32[]{:S(2)}, u32[]{:S(2)}) collective-permute-start(bf16[2,64,1024]{2,0,1:T(2,128)(2,1)S(1)} %get-tuple-element.29), channel_id=1, source_target_pairs={{1,0},{2,1},{3,2},{4,3},{5,4},{6,5},{7,6},{8,7},{9,8},{10,9},{11,1... | collective-permute-start | bytes 786440 | tf_op jit(solution)/shard_map/ppermute | solution.py:15
  11.9 0.7 fusion.23
  12.5 0.1 slice_subtract_fusion
  12.6 0.7 fusion.22
  13.3 0.8 %convert_multiply_fusion = f32[4,16]{1,0:T(4,128)S(1)} fusion(s32[4,16]{1,0:T(4,128)} %param.6, f32[4]{0:T(128)} %constant.46), kind=kLoop, calls=%fused_computation.53 | loop fusion | flops 128 | bytes 528 | tf_op jit(solution)/shard_map/mul | solution.py:21
  14.0 0.1 multiply_subtract_fusion
  14.2 1.4 %fusion.19 = f32[1,16]{1,0:T(1,128)S(1)} fusion(f32[1]{0:T(128)} %get-tuple-element.48, f32[1]{0:T(128)} %get-tuple-element.47), kind=kLoop, calls=%fused_computation.75 | loop fusion | flops 64 | bytes 72 | tf_op jit(solution)/shard_map/stack | solution.py:30
  15.6 0.1 add_convert_fusion.refs_1_
  15.7 0.1 pad.50.clone
  15.8 0.0 slice-start
  15.8 0.9 %slice_convert_fusion = (f32[2,16,1024]{2,1,0:T(8,128)S(1)}, f32[2,16,1024]{2,1,0:T(8,128)S(1)}) fusion(bf16[64,16,1024]{2,1,0:T(8,128)(2,1)} %refs_2_.1), kind=kLoop, calls=%fused_computation.8 | loop fusion | flops 65536 | bytes 393216 | tf_op jit(solution)/shard_map/convert_element_type | solution.py:233
  16.8 0.0 collective-permute-done.1
  16.8 0.6 collective-permute-done
  17.4 0.0 copy-start
  17.4 0.6 pad_maximum_fusion
  18.1 0.0 slice-done
  18.1 1.3 %collective-permute-start.2 = (bf16[4,24,1024]{2,1,0:T(8,128)(2,1)S(1)}, bf16[4,24,1024]{2,1,0:T(8,128)(2,1)S(1)}, u32[]{:S(2)}, u32[]{:S(2)}) collective-permute-start(bf16[4,24,1024]{2,1,0:T(8,128)(2,1)S(1)} %pad_maximum_fusion.3), channel_id=1, source_target_pairs={{32,0},{64,32},{96,64},{128,96},{160,128},{192,160},{224,192},{33,... | collective-permute-start | bytes 589832 | tf_op jit(solution)/shard_map/ppermute | solution.py:15
  19.4 0.0 copy-done
  19.4 31.0 %shard_map.46 = (f32[3,16,1024]{2,1,0:T(8,128)S(1)}, f32[16,1024]{1,0:T(8,128)S(1)}, f32[16,1024]{1,0:T(8,128)S(1)}, f32[4,16,1024]{2,1,0:T(8,128)S(1)}, f32[4,16,1024]{2,1,0:T(8,128)S(1)}) custom-call(f32[10,16]{1,0:T(8,128)S(1)} %stack.62.refs_0_, s32[4]{0:T(128)S(1)} %add_convert_fusion.refs_1_, bf16[64,16,1024]{2,1,0:T(8,128)(2,1)S(1)} %copy-done, ...), custom_call_target="tpu_custom_call" | custom-call | tf_op jit(solution)/shard_map/pallas_call | solution.py:206
  50.5 0.0 collective-permute-done.2
  50.6 3.4 %shard_map.47 = (f32[3,16,1024]{2,1,0:T(8,128)S(1)}, f32[16,1024]{1,0:T(8,128)S(1)}) custom-call(f32[10,16]{1,0:T(8,128)S(1)} %stack.62.refs_0_, s32[4]{0:T(128)S(1)} %add_convert_fusion.refs_1_, f32[2,24,1024]{2,1,0:T(8,128)S(1)} %pad_maximum_fusion.2.refs_2_, f32[6,24,1024]{2,1,0:T(8,128)S(1)} %pad_maximum_fusion.1.refs_3_, ...), custom_call_target="tpu_custom_call" | custom-call | tf_op jit(solution)/shard_map/pallas_call | solution.py:216
  54.0 12.3 %all_to_all.5 = f32[8,4,16,128]{3,2,1,0:T(8,128)S(1)} all-to-all(f32[8,4,16,128]{3,2,1,0:T(8,128)S(1)} %maximum_bitcast_fusion), channel_id=1, replica_groups=mesh['depth'=8,'tile'=32] {'depth'}, dimensions={0} | all-to-all | bytes 524288 | tf_op jit(solution)/shard_map/all_to_all | solution.py:248
  66.4 0.6 pad_maximum_fusion.4
  (25 shorter events, 0.3 us)
Async XLA Ops:
  2.0 14.8 %collective-permute-start.1 = (bf16[2,64,1024]{2,0,1:T(2,128)(2,1)S(1)}, bf16[2,64,1024]{2,0,1:T(2,128)(2,1)S(1)}, u32[]{:S(2)}, u32[]{:S(2)}) collective-permute-start(bf16[2,64,1024]{2,0,1:T(2,128)(2,1)S(1)} %get-tuple-element.30), channel_id=1, source_target_pairs={{0,1},{1,2},{2,3},{3,4},{4,5},{5,6},{6,7},{7,8},{8,9},{9,10},{10,1... | collective-permute-start | bytes 786440 | tf_op jit(solution)/shard_map/ppermute | solution.py:15
  5.8 11.6 %collective-permute-start = (bf16[2,64,1024]{2,0,1:T(2,128)(2,1)S(1)}, bf16[2,64,1024]{2,0,1:T(2,128)(2,1)S(1)}, u32[]{:S(2)}, u32[]{:S(2)}) collective-permute-start(bf16[2,64,1024]{2,0,1:T(2,128)(2,1)S(1)} %get-tuple-element.29), channel_id=1, source_target_pairs={{1,0},{2,1},{3,2},{4,3},{5,4},{6,5},{7,6},{8,7},{9,8},{10,9},{11,1... | collective-permute-start | bytes 786440 | tf_op jit(solution)/shard_map/ppermute | solution.py:15
  15.8 2.3 %slice-start = ((bf16[64,16,1024]{2,1,0:T(8,128)(2,1)}), bf16[4,16,1024]{2,1,0:T(8,128)(2,1)S(1)}, s32[]{:S(2)}) async-start(bf16[64,16,1024]{2,1,0:T(8,128)(2,1)} %refs_2_.1), calls=%async_computation.1 | async-start | bytes 262144 | tf_op jit(solution)/shard_map/slice | solution.py:235
  17.4 2.0 %copy-start = (bf16[64,16,1024]{2,1,0:T(8,128)(2,1)S(1)}, bf16[64,16,1024]{2,1,0:T(8,128)(2,1)}, u32[]{:S(2)}) copy-start(bf16[64,16,1024]{2,1,0:T(8,128)(2,1)} %refs_2_.1) | copy-start | bytes 6291460
  18.1 32.3 %collective-permute-start.2 = (bf16[4,24,1024]{2,1,0:T(8,128)(2,1)S(1)}, bf16[4,24,1024]{2,1,0:T(8,128)(2,1)S(1)}, u32[]{:S(2)}, u32[]{:S(2)}) collective-permute-start(bf16[4,24,1024]{2,1,0:T(8,128)(2,1)S(1)} %pad_maximum_fusion.3), channel_id=1, source_target_pairs={{32,0},{64,32},{96,64},{128,96},{160,128},{192,160},{224,192},{33,... | collective-permute-start | bytes 589832 | tf_op jit(solution)/shard_map/ppermute | solution.py:15

commit v14 on v12

--- a/solution.py
+++ b/solution.py
@@ -97,7 +97,7 @@
     keep = row_keep(flags, tall, lanes, rows)[rows:]
 
     def joined(i):
-        return jnp.concatenate([volume_ref[i].astype(jnp.float32), side_ref[i]], axis=0)
+        return jnp.concatenate([volume_ref[i], side_ref[i]], axis=0)
 
     def plane(i, carry):
         center, square, facing = smooth_plane(joined(i - 1), joined(i), joined(i + 1), keep, rows)
@@ -212,7 +212,7 @@
                    jax.ShapeDtypeStruct((4, rows, lanes), jnp.float32)],
         scratch_shapes=[pltpu.VMEM((depth, rows, lanes), jnp.float32) for _ in range(3)],
         compiler_params=pltpu.CompilerParams(vmem_limit_bytes=48 * 1024 * 1024),
-    )(table, flags, volume, side)
+    )(table, flags, volume.astype(jnp.float32), side)
     return pl.pallas_call(
         lambda *refs: edge_kernel(*refs, segments=segments, rows=rows),
         in_specs=[smem, smem] + [vmem] * 7,

time: 67.8 us -> 75.9 us (1.12)
  Pallas kernels: 34.3 us -> 38.5 us
  other arithmetic: 5.42 us -> 8.71 us
  waiting for transfers between devices: 0.64 us -> 1.65 us
    pallas_call x1, Pallas kernels: 31 us -> 35.2 us  [render_block(): pl.pallas_call(lambda *refs: middle_kernel(*refs, segments=segments, rows...]
    convert_element_type x0 -> x1, other arithmetic: none -> 4.2 us  [render_block(): volume.astype(jnp.float32)]
    ppermute x3, waiting for transfers between devices: 0.64 us -> 1.65 us  [shifted(): return lax.ppermute(block, axis, pairs)]
    convert_element_type x1, other arithmetic: 0.93 us -> 0.02 us  [body(): volume[a:b].astype(jnp.float32)]
  transfers between devices with their start and end apart: 3 -> 3, of which waited for: 1 -> 1; matrix products, arithmetic and copies ran while one was open for 7% -> 11% of each run, Pallas kernels for 46% -> 47%
where the time goes in v14:
time: 75.9 us; the launch traced here: 75.5 us
  Pallas kernels  38.5 us (51%)
  blocking collectives  12.3 us (16%)
  starting transfers between devices  11.2 us (15%)
  other arithmetic  8.71 us (11%)
  local copies, waits for them, and re-layouts  2.88 us (4%)
  waiting for transfers between devices  1.65 us (2%)
    pallas_call x1, Pallas kernels, render_block(): pl.pallas_call(lambda *refs: middle_kernel(*refs, segments=segments, rows...  35.2 us
    all_to_all x1, blocking collectives, body(): blocks = lax.all_to_all(weighted, 'depth', 0, 0, tiled=True)  12.3 us
    ppermute x3, starting transfers between devices, shifted(): return lax.ppermute(block, axis, pairs)  11.2 us
    convert_element_type x1, other arithmetic, render_block(): volume.astype(jnp.float32)  4.2 us
    pallas_call x1, Pallas kernels, render_block(): pl.pallas_call(lambda *refs: edge_kernel(*refs, segments=segments, rows=r...  3.35 us
    slice x1, local copies, waits for them, and re-layouts, body(): x_high = shifted(volume[:, :2], 'tile', -1)  1.99 us
    ppermute x3, waiting for transfers between devices, shifted(): return lax.ppermute(block, axis, pairs)  1.65 us
  transfers between devices with their start and end apart: 3, of which 1 were waited for; matrix products, arithmetic and copies ran while one was open for 11% of the time, Pallas kernels for 47%

profile of v14, /device:TPU:24, one launch (start us, length us, event | category | flops | bytes accessed | tf_op | source)
XLA Modules:
  0.0 75.5 jit_solution(16167444930014221567)
XLA Ops:
  0.0 2.0 %fusion.22 = (bf16[64,2,1024]{2,1,0:T(2,128)(2,1)S(1)}, bf16[64,2,1024]{2,1,0:T(2,128)(2,1)S(1)}) fusion(bf16[64,16,1024]{2,1,0:T(8,128)(2,1)} %param.4), kind=kLoop, calls=%fused_computation.77 | loop fusion | bytes 1048576 | tf_op jit(solution)/shard_map/slice | solution.py:230
  2.0 7.9 %collective-permute-start = (bf16[64,2,1024]{2,1,0:T(2,128)(2,1)S(1)}, bf16[64,2,1024]{2,1,0:T(2,128)(2,1)S(1)}, u32[]{:S(2)}, u32[]{:S(2)}) collective-permute-start(bf16[64,2,1024]{2,1,0:T(2,128)(2,1)S(1)} %get-tuple-element.29), channel_id=1, source_target_pairs={{1,0},{2,1},{3,2},{4,3},{5,4},{6,5},{7,6},{8,7},{9,8},{10,9},{11,1... | collective-permute-start | bytes 786440 | tf_op jit(solution)/shard_map/ppermute | solution.py:15
  9.9 1.9 %collective-permute-start.1 = (bf16[64,2,1024]{2,1,0:T(2,128)(2,1)S(1)}, bf16[64,2,1024]{2,1,0:T(2,128)(2,1)S(1)}, u32[]{:S(2)}, u32[]{:S(2)}) collective-permute-start(bf16[64,2,1024]{2,1,0:T(2,128)(2,1)S(1)} %get-tuple-element.30), channel_id=1, source_target_pairs={{0,1},{1,2},{2,3},{3,4},{4,5},{5,6},{6,7},{7,8},{8,9},{9,10},{10,1... | collective-permute-start | bytes 786440 | tf_op jit(solution)/shard_map/ppermute | solution.py:15
  11.9 0.7 fusion.24
  12.5 0.1 slice_subtract_fusion
  12.6 0.7 fusion.23
  13.3 0.8 convert_multiply_fusion
  14.0 0.1 multiply_subtract_fusion
  14.2 1.4 %fusion.19 = f32[1,16]{1,0:T(1,128)S(1)} fusion(f32[1]{0:T(128)} %get-tuple-element.48, f32[1]{0:T(128)} %get-tuple-element.47), kind=kLoop, calls=%fused_computation.73 | loop fusion | flops 64 | bytes 72 | tf_op jit(solution)/shard_map/stack | solution.py:30
  15.6 0.1 add_convert_fusion.refs_1_
  15.7 0.0 copy-start
  15.7 4.2 %convert_element_type.42.refs_2_ = f32[64,16,1024]{2,1,0:T(8,128)} convert(bf16[64,16,1024]{2,1,0:T(8,128)(2,1)} %param.4) | non-fusion elementwise | flops 1048576 | bytes 6291456 | tf_op jit(solution)/shard_map/convert_element_type | solution.py:215
  19.9 0.1 pad.50.clone
  20.0 0.0 copy-done
  20.0 0.0 slice-start
  20.1 0.0 collective-permute-done
  20.1 1.6 %collective-permute-done.1 = bf16[64,2,1024]{2,1,0:T(2,128)(2,1)S(1)} collective-permute-done((bf16[64,2,1024]{2,1,0:T(2,128)(2,1)S(1)}, bf16[64,2,1024]{2,1,0:T(2,128)(2,1)S(1)}, u32[]{:S(2)}, u32[]{:S(2)}) %collective-permute-start.1) | collective-permute-done | bytes 262176 | tf_op jit(solution)/shard_map/ppermute | solution.py:15
  21.7 0.6 pad_maximum_fusion
  22.4 0.0 slice-done
  22.4 1.3 %collective-permute-start.2 = (bf16[4,24,1024]{2,1,0:T(8,128)(2,1)S(1)}, bf16[4,24,1024]{2,1,0:T(8,128)(2,1)S(1)}, u32[]{:S(2)}, u32[]{:S(2)}) collective-permute-start(bf16[4,24,1024]{2,1,0:T(8,128)(2,1)S(1)} %pad_maximum_fusion.3), channel_id=1, source_target_pairs={{32,0},{64,32},{96,64},{128,96},{160,128},{192,160},{224,192},{33,... | collective-permute-start | bytes 589832 | tf_op jit(solution)/shard_map/ppermute | solution.py:15
  23.7 35.2 %shard_map.46 = (f32[3,16,1024]{2,1,0:T(8,128)S(1)}, f32[16,1024]{1,0:T(8,128)S(1)}, f32[16,1024]{1,0:T(8,128)S(1)}, f32[4,16,1024]{2,1,0:T(8,128)S(1)}, f32[4,16,1024]{2,1,0:T(8,128)S(1)}) custom-call(f32[10,16]{1,0:T(8,128)S(1)} %stack.62.refs_0_, s32[4]{0:T(128)S(1)} %add_convert_fusion.refs_1_, f32[64,16,1024]{2,1,0:T(8,128)} %convert_element_type.42.refs_2_, ...), custom_call_target="tpu_custom_call" | custom-call | tf_op jit(solution)/shard_map/pallas_call | solution.py:206
  58.9 0.0 collective-permute-done.2
  59.0 3.4 %shard_map.47 = (f32[3,16,1024]{2,1,0:T(8,128)S(1)}, f32[16,1024]{1,0:T(8,128)S(1)}) custom-call(f32[10,16]{1,0:T(8,128)S(1)} %stack.62.refs_0_, s32[4]{0:T(128)S(1)} %add_convert_fusion.refs_1_, f32[2,24,1024]{2,1,0:T(8,128)S(1)} %pad_maximum_fusion.2.refs_2_, f32[6,24,1024]{2,1,0:T(8,128)S(1)} %pad_maximum_fusion.1.refs_3_, ...), custom_call_target="tpu_custom_call" | custom-call | tf_op jit(solution)/shard_map/pallas_call | solution.py:216
  62.5 12.3 %all_to_all.5 = f32[8,4,16,128]{3,2,1,0:T(8,128)S(1)} all-to-all(f32[8,4,16,128]{3,2,1,0:T(8,128)S(1)} %maximum_bitcast_fusion), channel_id=1, replica_groups=mesh['depth'=8,'tile'=32] {'depth'}, dimensions={0} | all-to-all | bytes 524288 | tf_op jit(solution)/shard_map/all_to_all | solution.py:248
  74.9 0.6 pad_maximum_fusion.4
  (26 shorter events, 0.4 us)
Async XLA Ops:
  2.0 18.1 %collective-permute-start = (bf16[64,2,1024]{2,1,0:T(2,128)(2,1)S(1)}, bf16[64,2,1024]{2,1,0:T(2,128)(2,1)S(1)}, u32[]{:S(2)}, u32[]{:S(2)}) collective-permute-start(bf16[64,2,1024]{2,1,0:T(2,128)(2,1)S(1)} %get-tuple-element.29), channel_id=1, source_target_pairs={{1,0},{2,1},{3,2},{4,3},{5,4},{6,5},{7,6},{8,7},{9,8},{10,9},{11,1... | collective-permute-start | bytes 786440 | tf_op jit(solution)/shard_map/ppermute | solution.py:15
  9.9 11.8 %collective-permute-start.1 = (bf16[64,2,1024]{2,1,0:T(2,128)(2,1)S(1)}, bf16[64,2,1024]{2,1,0:T(2,128)(2,1)S(1)}, u32[]{:S(2)}, u32[]{:S(2)}) collective-permute-start(bf16[64,2,1024]{2,1,0:T(2,128)(2,1)S(1)} %get-tuple-element.30), channel_id=1, source_target_pairs={{0,1},{1,2},{2,3},{3,4},{4,5},{5,6},{6,7},{7,8},{8,9},{9,10},{10,1... | collective-permute-start | bytes 786440 | tf_op jit(solution)/shard_map/ppermute | solution.py:15
  15.7 4.3 %copy-start = (bf16[64,16,1024]{2,1,0:T(8,128)(2,1)S(1)}, bf16[64,16,1024]{2,1,0:T(8,128)(2,1)}, u32[]{:S(2)}) copy-start(bf16[64,16,1024]{2,1,0:T(8,128)(2,1)} %param.4) | copy-start | bytes 6291460
  20.0 2.3 %slice-start = ((bf16[64,16,1024]{2,1,0:T(8,128)(2,1)}), bf16[4,16,1024]{2,1,0:T(8,128)(2,1)S(1)}, s32[]{:S(2)}) async-start(bf16[64,16,1024]{2,1,0:T(8,128)(2,1)} %param.4), calls=%async_computation.1 | async-start | bytes 262144 | tf_op jit(solution)/shard_map/slice | solution.py:235
  22.4 36.5 %collective-permute-start.2 = (bf16[4,24,1024]{2,1,0:T(8,128)(2,1)S(1)}, bf16[4,24,1024]{2,1,0:T(8,128)(2,1)S(1)}, u32[]{:S(2)}, u32[]{:S(2)}) collective-permute-start(bf16[4,24,1024]{2,1,0:T(8,128)(2,1)S(1)} %pad_maximum_fusion.3), channel_id=1, source_target_pairs={{32,0},{64,32},{96,64},{128,96},{160,128},{192,160},{224,192},{33,... | collective-permute-start | bytes 589832 | tf_op jit(solution)/shard_map/ppermute | solution.py:15

commit v15 on v12

--- a/solution.py
+++ b/solution.py
@@ -106,7 +106,7 @@
         facing_ref[i] = facing
         return carry
 
-    lax.fori_loop(1, depth - 1, plane, 0, unroll=2)
+    lax.fori_loop(1, depth - 1, plane, 0, unroll=4)
     for n, i in enumerate((1, 2, depth - 3, depth - 2)):
         kept_ref[n] = smooth_ref[i]
     for n, i in enumerate((1, depth - 2)):

time: 67.8 us -> 69.2 us (1.021)
  Pallas kernels: 34.3 us -> 35.8 us
    pallas_call x1, Pallas kernels: 31 us -> 32.4 us  [render_block(): pl.pallas_call(lambda *refs: middle_kernel(*refs, segments=segments, rows...]
  transfers between devices with their start and end apart: 3 -> 3, of which waited for: 1 -> 1; matrix products, arithmetic and copies ran while one was open for 7% -> 7% of each run, Pallas kernels for 46% -> 47%
where the time goes in v15:
time: 69.2 us; the launch traced here: 68.5 us
  Pallas kernels  35.8 us (52%)
  blocking collectives  12.3 us (18%)
  starting transfers between devices  11.2 us (16%)
  other arithmetic  5.42 us (8%)
  local copies, waits for them, and re-layouts  2.89 us (4%)
    pallas_call x1, Pallas kernels, render_block(): pl.pallas_call(lambda *refs: middle_kernel(*refs, segments=segments, rows...  32.4 us
    all_to_all x1, blocking collectives, body(): blocks = lax.all_to_all(weighted, 'depth', 0, 0, tiled=True)  12.3 us
    ppermute x3, starting transfers between devices, shifted(): return lax.ppermute(block, axis, pairs)  11.2 us
    pallas_call x1, Pallas kernels, render_block(): pl.pallas_call(lambda *refs: edge_kernel(*refs, segments=segments, rows=r...  3.35 us
    slice x1, local copies, waits for them, and re-layouts, body(): x_high = shifted(volume[:, :2], 'tile', -1)  1.99 us
    another operation x1, other arithmetic, ramp_table(): return jnp.stack(rows)  1.41 us
  transfers between devices with their start and end apart: 3, of which 1 were waited for; matrix products, arithmetic and copies ran while one was open for 7% of the time, Pallas kernels for 47%

profile of v15, /device:TPU:24, one launch (start us, length us, event | category | flops | bytes accessed | tf_op | source)
XLA Modules:
  0.0 68.5 jit_solution(9729818807194161072)
XLA Ops:
  0.0 2.0 %fusion.22 = (bf16[64,2,1024]{2,1,0:T(2,128)(2,1)S(1)}, bf16[64,2,1024]{2,1,0:T(2,128)(2,1)S(1)}) fusion(bf16[64,16,1024]{2,1,0:T(8,128)(2,1)} %refs_2_.1), kind=kLoop, calls=%fused_computation.77 | loop fusion | bytes 1048576 | tf_op jit(solution)/shard_map/slice | solution.py:230
  2.0 3.8 %collective-permute-start.1 = (bf16[64,2,1024]{2,1,0:T(2,128)(2,1)S(1)}, bf16[64,2,1024]{2,1,0:T(2,128)(2,1)S(1)}, u32[]{:S(2)}, u32[]{:S(2)}) collective-permute-start(bf16[64,2,1024]{2,1,0:T(2,128)(2,1)S(1)} %get-tuple-element.30), channel_id=1, source_target_pairs={{0,1},{1,2},{2,3},{3,4},{4,5},{5,6},{6,7},{7,8},{8,9},{9,10},{10,1... | collective-permute-start | bytes 786440 | tf_op jit(solution)/shard_map/ppermute | solution.py:15
  5.8 6.0 %collective-permute-start = (bf16[64,2,1024]{2,1,0:T(2,128)(2,1)S(1)}, bf16[64,2,1024]{2,1,0:T(2,128)(2,1)S(1)}, u32[]{:S(2)}, u32[]{:S(2)}) collective-permute-start(bf16[64,2,1024]{2,1,0:T(2,128)(2,1)S(1)} %get-tuple-element.29), channel_id=1, source_target_pairs={{1,0},{2,1},{3,2},{4,3},{5,4},{6,5},{7,6},{8,7},{9,8},{10,9},{11,1... | collective-permute-start | bytes 786440 | tf_op jit(solution)/shard_map/ppermute | solution.py:15
  11.9 0.7 fusion.24
  12.5 0.1 slice_subtract_fusion
  12.6 0.7 fusion.23
  13.3 0.8 %convert_multiply_fusion = f32[4,16]{1,0:T(4,128)S(1)} fusion(s32[4,16]{1,0:T(4,128)} %param.6, f32[4]{0:T(128)} %constant.46), kind=kLoop, calls=%fused_computation.51 | loop fusion | flops 128 | bytes 528 | tf_op jit(solution)/shard_map/mul | solution.py:21
  14.0 0.1 multiply_subtract_fusion
  14.2 1.4 %fusion.19 = f32[1,16]{1,0:T(1,128)S(1)} fusion(f32[1]{0:T(128)} %get-tuple-element.48, f32[1]{0:T(128)} %get-tuple-element.47), kind=kLoop, calls=%fused_computation.73 | loop fusion | flops 64 | bytes 72 | tf_op jit(solution)/shard_map/stack | solution.py:30
  15.6 0.1 add_convert_fusion.refs_1_
  15.7 0.1 pad.50.clone
  15.8 0.0 slice-start
  15.8 0.9 %slice_convert_fusion = (f32[2,16,1024]{2,1,0:T(8,128)S(1)}, f32[2,16,1024]{2,1,0:T(8,128)S(1)}) fusion(bf16[64,16,1024]{2,1,0:T(8,128)(2,1)} %refs_2_.1), kind=kLoop, calls=%fused_computation.6 | loop fusion | flops 65536 | bytes 393216 | tf_op jit(solution)/shard_map/convert_element_type | solution.py:233
  16.8 0.0 copy-start
  16.8 0.0 collective-permute-done.1
  16.8 0.6 collective-permute-done
  17.4 0.6 pad_maximum_fusion
  18.1 0.0 slice-done
  18.1 1.3 %collective-permute-start.2 = (bf16[4,24,1024]{2,1,0:T(8,128)(2,1)S(1)}, bf16[4,24,1024]{2,1,0:T(8,128)(2,1)S(1)}, u32[]{:S(2)}, u32[]{:S(2)}) collective-permute-start(bf16[4,24,1024]{2,1,0:T(8,128)(2,1)S(1)} %pad_maximum_fusion.3), channel_id=1, source_target_pairs={{32,0},{64,32},{96,64},{128,96},{160,128},{192,160},{224,192},{33,... | collective-permute-start | bytes 589832 | tf_op jit(solution)/shard_map/ppermute | solution.py:15
  19.4 0.0 copy-done
  19.4 32.4 %shard_map.46 = (f32[3,16,1024]{2,1,0:T(8,128)S(1)}, f32[16,1024]{1,0:T(8,128)S(1)}, f32[16,1024]{1,0:T(8,128)S(1)}, f32[4,16,1024]{2,1,0:T(8,128)S(1)}, f32[4,16,1024]{2,1,0:T(8,128)S(1)}) custom-call(f32[10,16]{1,0:T(8,128)S(1)} %stack.62.refs_0_, s32[4]{0:T(128)S(1)} %add_convert_fusion.refs_1_, bf16[64,16,1024]{2,1,0:T(8,128)(2,1)S(1)} %copy-done, ...), custom_call_target="tpu_custom_call" | custom-call | tf_op jit(solution)/shard_map/pallas_call | solution.py:206
  51.9 0.0 collective-permute-done.2
  52.0 3.4 %shard_map.47 = (f32[3,16,1024]{2,1,0:T(8,128)S(1)}, f32[16,1024]{1,0:T(8,128)S(1)}) custom-call(f32[10,16]{1,0:T(8,128)S(1)} %stack.62.refs_0_, s32[4]{0:T(128)S(1)} %add_convert_fusion.refs_1_, f32[2,24,1024]{2,1,0:T(8,128)S(1)} %pad_maximum_fusion.2.refs_2_, f32[6,24,1024]{2,1,0:T(8,128)S(1)} %pad_maximum_fusion.1.refs_3_, ...), custom_call_target="tpu_custom_call" | custom-call | tf_op jit(solution)/shard_map/pallas_call | solution.py:216
  55.4 12.3 %all_to_all.5 = f32[8,4,16,128]{3,2,1,0:T(8,128)S(1)} all-to-all(f32[8,4,16,128]{3,2,1,0:T(8,128)S(1)} %maximum_bitcast_fusion), channel_id=1, replica_groups=mesh['depth'=8,'tile'=32] {'depth'}, dimensions={0} | all-to-all | bytes 524288 | tf_op jit(solution)/shard_map/all_to_all | solution.py:248
  67.9 0.6 pad_maximum_fusion.4
  (25 shorter events, 0.3 us)
Async XLA Ops:
  2.0 14.8 %collective-permute-start.1 = (bf16[64,2,1024]{2,1,0:T(2,128)(2,1)S(1)}, bf16[64,2,1024]{2,1,0:T(2,128)(2,1)S(1)}, u32[]{:S(2)}, u32[]{:S(2)}) collective-permute-start(bf16[64,2,1024]{2,1,0:T(2,128)(2,1)S(1)} %get-tuple-element.30), channel_id=1, source_target_pairs={{0,1},{1,2},{2,3},{3,4},{4,5},{5,6},{6,7},{7,8},{8,9},{9,10},{10,1... | collective-permute-start | bytes 786440 | tf_op jit(solution)/shard_map/ppermute | solution.py:15
  5.8 11.6 %collective-permute-start = (bf16[64,2,1024]{2,1,0:T(2,128)(2,1)S(1)}, bf16[64,2,1024]{2,1,0:T(2,128)(2,1)S(1)}, u32[]{:S(2)}, u32[]{:S(2)}) collective-permute-start(bf16[64,2,1024]{2,1,0:T(2,128)(2,1)S(1)} %get-tuple-element.29), channel_id=1, source_target_pairs={{1,0},{2,1},{3,2},{4,3},{5,4},{6,5},{7,6},{8,7},{9,8},{10,9},{11,1... | collective-permute-start | bytes 786440 | tf_op jit(solution)/shard_map/ppermute | solution.py:15
  15.8 2.2 %slice-start = ((bf16[64,16,1024]{2,1,0:T(8,128)(2,1)}), bf16[4,16,1024]{2,1,0:T(8,128)(2,1)S(1)}, s32[]{:S(2)}) async-start(bf16[64,16,1024]{2,1,0:T(8,128)(2,1)} %refs_2_.1), calls=%async_computation.1 | async-start | bytes 262144 | tf_op jit(solution)/shard_map/slice | solution.py:235
  16.8 2.7 %copy-start = (bf16[64,16,1024]{2,1,0:T(8,128)(2,1)S(1)}, bf16[64,16,1024]{2,1,0:T(8,128)(2,1)}, u32[]{:S(2)}) copy-start(bf16[64,16,1024]{2,1,0:T(8,128)(2,1)} %refs_2_.1) | copy-start | bytes 6291460
  18.1 33.8 %collective-permute-start.2 = (bf16[4,24,1024]{2,1,0:T(8,128)(2,1)S(1)}, bf16[4,24,1024]{2,1,0:T(8,128)(2,1)S(1)}, u32[]{:S(2)}, u32[]{:S(2)}) collective-permute-start(bf16[4,24,1024]{2,1,0:T(8,128)(2,1)S(1)} %pad_maximum_fusion.3), channel_id=1, source_target_pairs={{32,0},{64,32},{96,64},{128,96},{160,128},{192,160},{224,192},{33,... | collective-permute-start | bytes 589832 | tf_op jit(solution)/shard_map/ppermute | solution.py:15

commit v16 on v12

--- a/solution.py
+++ b/solution.py
@@ -57,7 +57,7 @@
     center = smooth[:rows]
     slope_x = 0.5 * (pltpu.roll(smooth, tall - 1, 0)[:rows] - pltpu.roll(smooth, 1, 0)[:rows])
     slope_y = 0.5 * (y_next(center) - y_prev(center))
-    return center, slope_x * slope_x + slope_y * slope_y, 0.8 * slope_x
+    return center, slope_x * slope_x + slope_y * slope_y + 0.1, 0.56 * slope_x
 
 
 class Palette:
@@ -70,10 +70,10 @@
         self.segments = segments
 
     def cell(self, before, center, after, square, facing):
-        slope_z = 0.5 * (after - before)
-        facing = jnp.abs(0.6 * slope_z + facing)
-        norm = slope_z * slope_z + square + 0.1
-        shade = 0.3 + 0.7 * facing * lax.rsqrt(norm)
+        step = after - before
+        facing = jnp.abs(0.21 * step + facing)
+        norm = 0.25 * (step * step) + square
+        shade = 0.3 + facing * lax.rsqrt(norm)
         lookup = jnp.clip(127.5 + 70.0 * center, self.lo, self.hi)
         offset = [jnp.full_like(lookup, self.offsets[c][0]) for c in range(4)]
         slope = [jnp.full_like(lookup, self.slopes[c][0]) for c in range(4)]

time: 67.8 us -> 67.9 us (level)
  no operation moved by 1% of the time
where the time goes in v16:
time: 67.9 us; the launch traced here: 67.2 us
  Pallas kernels  34.5 us (51%)
  blocking collectives  12.3 us (18%)
  starting transfers between devices  11.2 us (16%)
  other arithmetic  5.42 us (8%)
  local copies, waits for them, and re-layouts  2.89 us (4%)
    pallas_call x1, Pallas kernels, render_block(): pl.pallas_call(lambda *refs: middle_kernel(*refs, segments=segments, rows...  31.1 us
    all_to_all x1, blocking collectives, body(): blocks = lax.all_to_all(weighted, 'depth', 0, 0, tiled=True)  12.3 us
    ppermute x3, starting transfers between devices, shifted(): return lax.ppermute(block, axis, pairs)  11.2 us
    pallas_call x1, Pallas kernels, render_block(): pl.pallas_call(lambda *refs: edge_kernel(*refs, segments=segments, rows=r...  3.34 us
    slice x1, local copies, waits for them, and re-layouts, body(): x_high = shifted(volume[:, :2], 'tile', -1)  1.99 us
    another operation x1, other arithmetic, ramp_table(): return jnp.stack(rows)  1.41 us
  transfers between devices with their start and end apart: 3, of which 1 were waited for; matrix products, arithmetic and copies ran while one was open for 7% of the time, Pallas kernels for 46%

profile of v16, /device:TPU:24, one launch (start us, length us, event | category | flops | bytes accessed | tf_op | source)
XLA Modules:
  0.0 67.2 jit_solution(6575671975095970241)
XLA Ops:
  0.0 2.0 %fusion.22 = (bf16[64,2,1024]{2,1,0:T(2,128)(2,1)S(1)}, bf16[64,2,1024]{2,1,0:T(2,128)(2,1)S(1)}) fusion(bf16[64,16,1024]{2,1,0:T(8,128)(2,1)} %refs_2_.1), kind=kLoop, calls=%fused_computation.77 | loop fusion | bytes 1048576 | tf_op jit(solution)/shard_map/slice | solution.py:230
  2.0 3.8 %collective-permute-start.1 = (bf16[64,2,1024]{2,1,0:T(2,128)(2,1)S(1)}, bf16[64,2,1024]{2,1,0:T(2,128)(2,1)S(1)}, u32[]{:S(2)}, u32[]{:S(2)}) collective-permute-start(bf16[64,2,1024]{2,1,0:T(2,128)(2,1)S(1)} %get-tuple-element.30), channel_id=1, source_target_pairs={{0,1},{1,2},{2,3},{3,4},{4,5},{5,6},{6,7},{7,8},{8,9},{9,10},{10,1... | collective-permute-start | bytes 786440 | tf_op jit(solution)/shard_map/ppermute | solution.py:15
  5.8 6.0 %collective-permute-start = (bf16[64,2,1024]{2,1,0:T(2,128)(2,1)S(1)}, bf16[64,2,1024]{2,1,0:T(2,128)(2,1)S(1)}, u32[]{:S(2)}, u32[]{:S(2)}) collective-permute-start(bf16[64,2,1024]{2,1,0:T(2,128)(2,1)S(1)} %get-tuple-element.29), channel_id=1, source_target_pairs={{1,0},{2,1},{3,2},{4,3},{5,4},{6,5},{7,6},{8,7},{9,8},{10,9},{11,1... | collective-permute-start | bytes 786440 | tf_op jit(solution)/shard_map/ppermute | solution.py:15
  11.9 0.7 fusion.24
  12.5 0.1 slice_subtract_fusion
  12.6 0.7 fusion.23
  13.3 0.8 %convert_multiply_fusion = f32[4,16]{1,0:T(4,128)S(1)} fusion(s32[4,16]{1,0:T(4,128)} %param.6, f32[4]{0:T(128)} %constant.46), kind=kLoop, calls=%fused_computation.51 | loop fusion | flops 128 | bytes 528 | tf_op jit(solution)/shard_map/mul | solution.py:21
  14.0 0.1 multiply_subtract_fusion
  14.2 1.4 %fusion.19 = f32[1,16]{1,0:T(1,128)S(1)} fusion(f32[1]{0:T(128)} %get-tuple-element.48, f32[1]{0:T(128)} %get-tuple-element.47), kind=kLoop, calls=%fused_computation.73 | loop fusion | flops 64 | bytes 72 | tf_op jit(solution)/shard_map/stack | solution.py:30
  15.6 0.1 add_convert_fusion.refs_1_
  15.7 0.1 pad.50.clone
  15.8 0.0 slice-start
  15.8 0.9 %slice_convert_fusion = (f32[2,16,1024]{2,1,0:T(8,128)S(1)}, f32[2,16,1024]{2,1,0:T(8,128)S(1)}) fusion(bf16[64,16,1024]{2,1,0:T(8,128)(2,1)} %refs_2_.1), kind=kLoop, calls=%fused_computation.6 | loop fusion | flops 65536 | bytes 393216 | tf_op jit(solution)/shard_map/convert_element_type | solution.py:233
  16.8 0.0 copy-start
  16.8 0.0 collective-permute-done.1
  16.8 0.6 collective-permute-done
  17.4 0.6 pad_maximum_fusion
  18.1 0.0 slice-done
  18.1 1.3 %collective-permute-start.2 = (bf16[4,24,1024]{2,1,0:T(8,128)(2,1)S(1)}, bf16[4,24,1024]{2,1,0:T(8,128)(2,1)S(1)}, u32[]{:S(2)}, u32[]{:S(2)}) collective-permute-start(bf16[4,24,1024]{2,1,0:T(8,128)(2,1)S(1)} %pad_maximum_fusion.3), channel_id=1, source_target_pairs={{32,0},{64,32},{96,64},{128,96},{160,128},{192,160},{224,192},{33,... | collective-permute-start | bytes 589832 | tf_op jit(solution)/shard_map/ppermute | solution.py:15
  19.4 0.0 copy-done
  19.4 31.1 %shard_map.46 = (f32[3,16,1024]{2,1,0:T(8,128)S(1)}, f32[16,1024]{1,0:T(8,128)S(1)}, f32[16,1024]{1,0:T(8,128)S(1)}, f32[4,16,1024]{2,1,0:T(8,128)S(1)}, f32[4,16,1024]{2,1,0:T(8,128)S(1)}) custom-call(f32[10,16]{1,0:T(8,128)S(1)} %stack.62.refs_0_, s32[4]{0:T(128)S(1)} %add_convert_fusion.refs_1_, bf16[64,16,1024]{2,1,0:T(8,128)(2,1)S(1)} %copy-done, ...), custom_call_target="tpu_custom_call" | custom-call | tf_op jit(solution)/shard_map/pallas_call | solution.py:206
  50.6 0.0 collective-permute-done.2
  50.7 3.3 %shard_map.47 = (f32[3,16,1024]{2,1,0:T(8,128)S(1)}, f32[16,1024]{1,0:T(8,128)S(1)}) custom-call(f32[10,16]{1,0:T(8,128)S(1)} %stack.62.refs_0_, s32[4]{0:T(128)S(1)} %add_convert_fusion.refs_1_, f32[2,24,1024]{2,1,0:T(8,128)S(1)} %pad_maximum_fusion.2.refs_2_, f32[6,24,1024]{2,1,0:T(8,128)S(1)} %pad_maximum_fusion.1.refs_3_, ...), custom_call_target="tpu_custom_call" | custom-call | tf_op jit(solution)/shard_map/pallas_call | solution.py:216
  54.1 12.3 %all_to_all.5 = f32[8,4,16,128]{3,2,1,0:T(8,128)S(1)} all-to-all(f32[8,4,16,128]{3,2,1,0:T(8,128)S(1)} %maximum_bitcast_fusion), channel_id=1, replica_groups=mesh['depth'=8,'tile'=32] {'depth'}, dimensions={0} | all-to-all | bytes 524288 | tf_op jit(solution)/shard_map/all_to_all | solution.py:248
  66.5 0.6 pad_maximum_fusion.4
  (25 shorter events, 0.3 us)
Async XLA Ops:
  2.0 14.8 %collective-permute-start.1 = (bf16[64,2,1024]{2,1,0:T(2,128)(2,1)S(1)}, bf16[64,2,1024]{2,1,0:T(2,128)(2,1)S(1)}, u32[]{:S(2)}, u32[]{:S(2)}) collective-permute-start(bf16[64,2,1024]{2,1,0:T(2,128)(2,1)S(1)} %get-tuple-element.30), channel_id=1, source_target_pairs={{0,1},{1,2},{2,3},{3,4},{4,5},{5,6},{6,7},{7,8},{8,9},{9,10},{10,1... | collective-permute-start | bytes 786440 | tf_op jit(solution)/shard_map/ppermute | solution.py:15
  5.8 11.6 %collective-permute-start = (bf16[64,2,1024]{2,1,0:T(2,128)(2,1)S(1)}, bf16[64,2,1024]{2,1,0:T(2,128)(2,1)S(1)}, u32[]{:S(2)}, u32[]{:S(2)}) collective-permute-start(bf16[64,2,1024]{2,1,0:T(2,128)(2,1)S(1)} %get-tuple-element.29), channel_id=1, source_target_pairs={{1,0},{2,1},{3,2},{4,3},{5,4},{6,5},{7,6},{8,7},{9,8},{10,9},{11,1... | collective-permute-start | bytes 786440 | tf_op jit(solution)/shard_map/ppermute | solution.py:15
  15.8 2.2 %slice-start = ((bf16[64,16,1024]{2,1,0:T(8,128)(2,1)}), bf16[4,16,1024]{2,1,0:T(8,128)(2,1)S(1)}, s32[]{:S(2)}) async-start(bf16[64,16,1024]{2,1,0:T(8,128)(2,1)} %refs_2_.1), calls=%async_computation.1 | async-start | bytes 262144 | tf_op jit(solution)/shard_map/slice | solution.py:235
  16.8 2.7 %copy-start = (bf16[64,16,1024]{2,1,0:T(8,128)(2,1)S(1)}, bf16[64,16,1024]{2,1,0:T(8,128)(2,1)}, u32[]{:S(2)}) copy-start(bf16[64,16,1024]{2,1,0:T(8,128)(2,1)} %refs_2_.1) | copy-start | bytes 6291460
  18.1 32.5 %collective-permute-start.2 = (bf16[4,24,1024]{2,1,0:T(8,128)(2,1)S(1)}, bf16[4,24,1024]{2,1,0:T(8,128)(2,1)S(1)}, u32[]{:S(2)}, u32[]{:S(2)}) collective-permute-start(bf16[4,24,1024]{2,1,0:T(8,128)(2,1)S(1)} %pad_maximum_fusion.3), channel_id=1, source_target_pairs={{32,0},{64,32},{96,64},{128,96},{160,128},{192,160},{224,192},{33,... | collective-permute-start | bytes 589832 | tf_op jit(solution)/shard_map/ppermute | solution.py:15

commit v17 on v12

--- a/solution.py
+++ b/solution.py
@@ -144,31 +144,38 @@
 
 
 def edge_kernel(table, flags, front_ref, back_ref, kept_ref, terms_ref, color_ref, depth_ref,
-                trans_ref, out_color_ref, out_depth_ref, *, segments, rows):
+                trans_ref, out_color_ref, out_depth_ref, stash_ref, *, segments, rows):
     tall, lanes = front_ref.shape[1:]
     keep = row_keep(flags, tall, lanes, rows)
     palette = Palette(table, segments)
     first = flags[0] == 1
     last = flags[1] == 1
-    zero = jnp.zeros((rows, lanes), jnp.float32)
     s0, q0, f0 = smooth_plane(jnp.zeros((tall, lanes), jnp.float32), front_ref[0], front_ref[1],
                               keep, rows)
-    s1, s2, s61, s62 = [kept_ref[n] for n in range(4)]
-    q1, f1, q62, f62 = [terms_ref[n] for n in range(4)]
-    front_cells = [palette.cell(zero, s0, s1, q0, f0), palette.cell(s0, s1, s2, q1, f1)]
-    smoothed = [(s61, None, None), (s62, q62, f62)]
+    stash_ref[0] = jnp.zeros((rows, lanes), jnp.float32)
+    stash_ref[1] = s0
+    stash_ref[2] = kept_ref[0]
+    stash_ref[3] = kept_ref[1]
+    stash_ref[4] = q0
+    stash_ref[5] = f0
+    stash_ref[6] = terms_ref[0]
+    stash_ref[7] = terms_ref[1]
+    stash_ref[8] = kept_ref[2]
+    stash_ref[9] = kept_ref[3]
+    stash_ref[14] = terms_ref[2]
+    stash_ref[18] = terms_ref[3]
     for i in range(1, back_ref.shape[0] - 1):
         inside = keep & ~((i >= 2) & last)
-        smoothed.append(smooth_plane(back_ref[i - 1], back_ref[i], back_ref[i + 1], inside, rows))
-    back_cells = []
-    for j in range(1, len(smoothed) - 1):
-        back_cells.append(palette.cell(smoothed[j - 1][0], smoothed[j][0], smoothed[j + 1][0],
-                                       smoothed[j][1], smoothed[j][2]))
-
-    def segment(cells):
-        color = [jnp.zeros((rows, lanes), jnp.float32) for c in range(3)]
-        total = jnp.zeros((rows, lanes), jnp.float32)
-        trans = jnp.ones((rows, lanes), jnp.float32)
+        s, q, f = smooth_plane(back_ref[i - 1], back_ref[i], back_ref[i + 1], inside, rows)
+        stash_ref[9 + i] = s
+        if i < 4:
+            stash_ref[14 + i] = q
+            stash_ref[18 + i] = f
+
+    def segment(cells, shape):
+        color = [jnp.zeros(shape, jnp.float32) for c in range(3)]
+        total = jnp.zeros(shape, jnp.float32)
+        trans = jnp.ones(shape, jnp.float32)
         for shade, chan in cells:
             fade = jnp.exp(-chan[3])
             weight = shade * (1.0 - fade) * trans
@@ -185,16 +192,27 @@
         return ([jnp.where(flag, color[c], 0.0) for c in range(3)],
                 jnp.where(flag, total, 0.0), jnp.where(flag, trans, 1.0))
 
-    front = segment(front_cells)
-    own_back = segment(back_cells[:EDGE])
-    next_front = segment(back_cells[EDGE:])
-    middle = ([color_ref[c] for c in range(3)], depth_ref[...], trans_ref[...])
-    result = join(only_if(first, front), middle)
-    result = join(result, own_back)
-    result = join(result, only_if(~last, next_front))
-    for c in range(3):
-        out_color_ref[c] = result[0][c]
-    out_depth_ref[...] = result[1]
+    sub, width = 8, 256
+    for r0 in range(0, rows, sub):
+        for c0 in range(0, lanes, width):
+            rs = pl.ds(r0, sub)
+            cs = pl.ds(c0, width)
+            get = lambda n: stash_ref[n, rs, cs]
+            front_cells = [palette.cell(get(0), get(1), get(2), get(4), get(5)),
+                           palette.cell(get(1), get(2), get(3), get(6), get(7))]
+            back_cells = [palette.cell(get(7 + j), get(8 + j), get(9 + j), get(14 + j - 1),
+                                       get(18 + j - 1)) for j in range(1, 5)]
+            shape = (sub, width)
+            front = segment(front_cells, shape)
+            own_back = segment(back_cells[:EDGE], shape)
+            next_front = segment(back_cells[EDGE:], shape)
+            middle = ([color_ref[c, rs, cs] for c in range(3)], depth_ref[rs, cs], trans_ref[rs, cs])
+            result = join(only_if(first, front), middle)
+            result = join(result, own_back)
+            result = join(result, only_if(~last, next_front))
+            for c in range(3):
+                out_color_ref[c, rs, cs] = result[0][c]
+            out_depth_ref[rs, cs] = result[1]
 
 
 def render_block(table, flags, volume, side, front, back, rows, segments):
@@ -218,6 +236,7 @@
         in_specs=[smem, smem] + [vmem] * 7,
         out_specs=[vmem, vmem],
         out_shape=[color_shape, plane_shape],
+        scratch_shapes=[pltpu.VMEM((22, rows, lanes), jnp.float32)],
         compiler_params=pltpu.CompilerParams(vmem_limit_bytes=48 * 1024 * 1024),
     )(table, flags, front, back, middle[3], middle[4], *middle[:3])
 

time: 67.8 us -> 68 us (level)
  no operation moved by 1% of the time
where the time goes in v17:
time: 68 us; the launch traced here: 67.2 us
  Pallas kernels  34.5 us (51%)
  blocking collectives  12.3 us (18%)
  starting transfers between devices  11.2 us (16%)
  other arithmetic  5.42 us (8%)
  local copies, waits for them, and re-layouts  2.89 us (4%)
    pallas_call x1, Pallas kernels, render_block(): pl.pallas_call(lambda *refs: middle_kernel(*refs, segments=segments, rows...  31 us
    all_to_all x1, blocking collectives, body(): blocks = lax.all_to_all(weighted, 'depth', 0, 0, tiled=True)  12.3 us
    ppermute x3, starting transfers between devices, shifted(): return lax.ppermute(block, axis, pairs)  11.2 us
    pallas_call x1, Pallas kernels, render_block(): pl.pallas_call(lambda *refs: edge_kernel(*refs, segments=segments, rows=r...  3.55 us
    slice x1, local copies, waits for them, and re-layouts, body(): x_high = shifted(volume[:, :2], 'tile', -1)  1.99 us
    another operation x1, other arithmetic, ramp_table(): return jnp.stack(rows)  1.41 us
  transfers between devices with their start and end apart: 3, of which 1 were waited for; matrix products, arithmetic and copies ran while one was open for 7% of the time, Pallas kernels for 46%

profile of v17, /device:TPU:24, one launch (start us, length us, event | category | flops | bytes accessed | tf_op | source)
XLA Modules:
  0.0 67.2 jit_solution(6652121526798921913)
XLA Ops:
  0.0 2.0 %fusion.22 = (bf16[64,2,1024]{2,1,0:T(2,128)(2,1)S(1)}, bf16[64,2,1024]{2,1,0:T(2,128)(2,1)S(1)}) fusion(bf16[64,16,1024]{2,1,0:T(8,128)(2,1)} %refs_2_.1), kind=kLoop, calls=%fused_computation.77 | loop fusion | bytes 1048576 | tf_op jit(solution)/shard_map/slice | solution.py:249
  2.0 3.8 %collective-permute-start.1 = (bf16[64,2,1024]{2,1,0:T(2,128)(2,1)S(1)}, bf16[64,2,1024]{2,1,0:T(2,128)(2,1)S(1)}, u32[]{:S(2)}, u32[]{:S(2)}) collective-permute-start(bf16[64,2,1024]{2,1,0:T(2,128)(2,1)S(1)} %get-tuple-element.30), channel_id=1, source_target_pairs={{0,1},{1,2},{2,3},{3,4},{4,5},{5,6},{6,7},{7,8},{8,9},{9,10},{10,1... | collective-permute-start | bytes 786440 | tf_op jit(solution)/shard_map/ppermute | solution.py:15
  5.8 6.0 %collective-permute-start = (bf16[64,2,1024]{2,1,0:T(2,128)(2,1)S(1)}, bf16[64,2,1024]{2,1,0:T(2,128)(2,1)S(1)}, u32[]{:S(2)}, u32[]{:S(2)}) collective-permute-start(bf16[64,2,1024]{2,1,0:T(2,128)(2,1)S(1)} %get-tuple-element.29), channel_id=1, source_target_pairs={{1,0},{2,1},{3,2},{4,3},{5,4},{6,5},{7,6},{8,7},{9,8},{10,9},{11,1... | collective-permute-start | bytes 786440 | tf_op jit(solution)/shard_map/ppermute | solution.py:15
  11.9 0.7 fusion.24
  12.5 0.1 slice_subtract_fusion
  12.6 0.7 fusion.23
  13.3 0.8 %convert_multiply_fusion = f32[4,16]{1,0:T(4,128)S(1)} fusion(s32[4,16]{1,0:T(4,128)} %param.6, f32[4]{0:T(128)} %constant.46), kind=kLoop, calls=%fused_computation.51 | loop fusion | flops 128 | bytes 528 | tf_op jit(solution)/shard_map/mul | solution.py:21
  14.0 0.1 multiply_subtract_fusion
  14.2 1.4 %fusion.19 = f32[1,16]{1,0:T(1,128)S(1)} fusion(f32[1]{0:T(128)} %get-tuple-element.48, f32[1]{0:T(128)} %get-tuple-element.47), kind=kLoop, calls=%fused_computation.73 | loop fusion | flops 64 | bytes 72 | tf_op jit(solution)/shard_map/stack | solution.py:30
  15.6 0.1 add_convert_fusion.refs_1_
  15.7 0.1 pad.50.clone
  15.8 0.0 slice-start
  15.8 0.9 %slice_convert_fusion = (f32[2,16,1024]{2,1,0:T(8,128)S(1)}, f32[2,16,1024]{2,1,0:T(8,128)S(1)}) fusion(bf16[64,16,1024]{2,1,0:T(8,128)(2,1)} %refs_2_.1), kind=kLoop, calls=%fused_computation.6 | loop fusion | flops 65536 | bytes 393216 | tf_op jit(solution)/shard_map/convert_element_type | solution.py:252
  16.8 0.0 copy-start
  16.8 0.0 collective-permute-done.1
  16.8 0.6 collective-permute-done
  17.4 0.6 pad_maximum_fusion
  18.1 0.0 slice-done
  18.1 1.3 %collective-permute-start.2 = (bf16[4,24,1024]{2,1,0:T(8,128)(2,1)S(1)}, bf16[4,24,1024]{2,1,0:T(8,128)(2,1)S(1)}, u32[]{:S(2)}, u32[]{:S(2)}) collective-permute-start(bf16[4,24,1024]{2,1,0:T(8,128)(2,1)S(1)} %pad_maximum_fusion.3), channel_id=1, source_target_pairs={{32,0},{64,32},{96,64},{128,96},{160,128},{192,160},{224,192},{33,... | collective-permute-start | bytes 589832 | tf_op jit(solution)/shard_map/ppermute | solution.py:15
  19.4 0.0 copy-done
  19.4 31.0 %shard_map.46 = (f32[3,16,1024]{2,1,0:T(8,128)S(1)}, f32[16,1024]{1,0:T(8,128)S(1)}, f32[16,1024]{1,0:T(8,128)S(1)}, f32[4,16,1024]{2,1,0:T(8,128)S(1)}, f32[4,16,1024]{2,1,0:T(8,128)S(1)}) custom-call(f32[10,16]{1,0:T(8,128)S(1)} %stack.62.refs_0_, s32[4]{0:T(128)S(1)} %add_convert_fusion.refs_1_, bf16[64,16,1024]{2,1,0:T(8,128)(2,1)S(1)} %copy-done, ...), custom_call_target="tpu_custom_call" | custom-call | tf_op jit(solution)/shard_map/pallas_call | solution.py:224
  50.5 0.0 collective-permute-done.2
  50.6 3.5 %shard_map.47 = (f32[3,16,1024]{2,1,0:T(8,128)S(1)}, f32[16,1024]{1,0:T(8,128)S(1)}) custom-call(f32[10,16]{1,0:T(8,128)S(1)} %stack.62.refs_0_, s32[4]{0:T(128)S(1)} %add_convert_fusion.refs_1_, f32[2,24,1024]{2,1,0:T(8,128)S(1)} %pad_maximum_fusion.2.refs_2_, f32[6,24,1024]{2,1,0:T(8,128)S(1)} %pad_maximum_fusion.1.refs_3_, ...), custom_call_target="tpu_custom_call" | custom-call | tf_op jit(solution)/shard_map/pallas_call | solution.py:234
  54.2 12.3 %all_to_all.5 = f32[8,4,16,128]{3,2,1,0:T(8,128)S(1)} all-to-all(f32[8,4,16,128]{3,2,1,0:T(8,128)S(1)} %maximum_bitcast_fusion), channel_id=1, replica_groups=mesh['depth'=8,'tile'=32] {'depth'}, dimensions={0} | all-to-all | bytes 524288 | tf_op jit(solution)/shard_map/all_to_all | solution.py:267
  66.6 0.6 pad_maximum_fusion.4
  (25 shorter events, 0.3 us)
Async XLA Ops:
  2.0 14.8 %collective-permute-start.1 = (bf16[64,2,1024]{2,1,0:T(2,128)(2,1)S(1)}, bf16[64,2,1024]{2,1,0:T(2,128)(2,1)S(1)}, u32[]{:S(2)}, u32[]{:S(2)}) collective-permute-start(bf16[64,2,1024]{2,1,0:T(2,128)(2,1)S(1)} %get-tuple-element.30), channel_id=1, source_target_pairs={{0,1},{1,2},{2,3},{3,4},{4,5},{5,6},{6,7},{7,8},{8,9},{9,10},{10,1... | collective-permute-start | bytes 786440 | tf_op jit(solution)/shard_map/ppermute | solution.py:15
  5.8 11.6 %collective-permute-start = (bf16[64,2,1024]{2,1,0:T(2,128)(2,1)S(1)}, bf16[64,2,1024]{2,1,0:T(2,128)(2,1)S(1)}, u32[]{:S(2)}, u32[]{:S(2)}) collective-permute-start(bf16[64,2,1024]{2,1,0:T(2,128)(2,1)S(1)} %get-tuple-element.29), channel_id=1, source_target_pairs={{1,0},{2,1},{3,2},{4,3},{5,4},{6,5},{7,6},{8,7},{9,8},{10,9},{11,1... | collective-permute-start | bytes 786440 | tf_op jit(solution)/shard_map/ppermute | solution.py:15
  15.8 2.2 %slice-start = ((bf16[64,16,1024]{2,1,0:T(8,128)(2,1)}), bf16[4,16,1024]{2,1,0:T(8,128)(2,1)S(1)}, s32[]{:S(2)}) async-start(bf16[64,16,1024]{2,1,0:T(8,128)(2,1)} %refs_2_.1), calls=%async_computation.1 | async-start | bytes 262144 | tf_op jit(solution)/shard_map/slice | solution.py:254
  16.8 2.7 %copy-start = (bf16[64,16,1024]{2,1,0:T(8,128)(2,1)S(1)}, bf16[64,16,1024]{2,1,0:T(8,128)(2,1)}, u32[]{:S(2)}) copy-start(bf16[64,16,1024]{2,1,0:T(8,128)(2,1)} %refs_2_.1) | copy-start | bytes 6291460
  18.1 32.3 %collective-permute-start.2 = (bf16[4,24,1024]{2,1,0:T(8,128)(2,1)S(1)}, bf16[4,24,1024]{2,1,0:T(8,128)(2,1)S(1)}, u32[]{:S(2)}, u32[]{:S(2)}) collective-permute-start(bf16[4,24,1024]{2,1,0:T(8,128)(2,1)S(1)} %pad_maximum_fusion.3), channel_id=1, source_target_pairs={{32,0},{64,32},{96,64},{128,96},{160,128},{192,160},{224,192},{33,... | collective-permute-start | bytes 589832 | tf_op jit(solution)/shard_map/ppermute | solution.py:15

commit v18 on v12

--- a/solution.py
+++ b/solution.py
@@ -135,7 +135,7 @@
             zeros = jnp.zeros((sub, width), jnp.float32)
             init = (jnp.ones((sub, width), jnp.float32), zeros, zeros, zeros, zeros)
             trans, acc0, acc1, acc2, total = lax.fori_loop(
-                EDGE, depth - EDGE, step, init, unroll=2)
+                EDGE, depth - EDGE, step, init, unroll=4)
             color_ref[0, rs, cs] = acc0
             color_ref[1, rs, cs] = acc1
             color_ref[2, rs, cs] = acc2

time: 67.8 us -> 67.1 us (0.990)
  Pallas kernels: 34.3 us -> 33.6 us
    pallas_call x1, Pallas kernels: 31 us -> 30.2 us  [render_block(): pl.pallas_call(lambda *refs: middle_kernel(*refs, segments=segments, rows...]
where the time goes in v18:
time: 67.1 us; the launch traced here: 66.3 us
  Pallas kernels  33.6 us (50%)
  blocking collectives  12.3 us (18%)
  starting transfers between devices  11.2 us (17%)
  other arithmetic  5.42 us (8%)
  local copies, waits for them, and re-layouts  2.89 us (4%)
    pallas_call x1, Pallas kernels, render_block(): pl.pallas_call(lambda *refs: middle_kernel(*refs, segments=segments, rows...  30.2 us
    all_to_all x1, blocking collectives, body(): blocks = lax.all_to_all(weighted, 'depth', 0, 0, tiled=True)  12.3 us
    ppermute x3, starting transfers between devices, shifted(): return lax.ppermute(block, axis, pairs)  11.2 us
    pallas_call x1, Pallas kernels, render_block(): pl.pallas_call(lambda *refs: edge_kernel(*refs, segments=segments, rows=r...  3.35 us
    slice x1, local copies, waits for them, and re-layouts, body(): x_high = shifted(volume[:, :2], 'tile', -1)  1.99 us
    another operation x1, other arithmetic, ramp_table(): return jnp.stack(rows)  1.41 us
  transfers between devices with their start and end apart: 3, of which 1 were waited for; matrix products, arithmetic and copies ran while one was open for 7% of the time, Pallas kernels for 46%

profile of v18, /device:TPU:24, one launch (start us, length us, event | category | flops | bytes accessed | tf_op | source)
XLA Modules:
  0.0 66.3 jit_solution(1204857003697186185)
XLA Ops:
  0.0 2.0 %fusion.22 = (bf16[64,2,1024]{2,1,0:T(2,128)(2,1)S(1)}, bf16[64,2,1024]{2,1,0:T(2,128)(2,1)S(1)}) fusion(bf16[64,16,1024]{2,1,0:T(8,128)(2,1)} %refs_2_.1), kind=kLoop, calls=%fused_computation.77 | loop fusion | bytes 1048576 | tf_op jit(solution)/shard_map/slice | solution.py:230
  2.0 3.8 %collective-permute-start.1 = (bf16[64,2,1024]{2,1,0:T(2,128)(2,1)S(1)}, bf16[64,2,1024]{2,1,0:T(2,128)(2,1)S(1)}, u32[]{:S(2)}, u32[]{:S(2)}) collective-permute-start(bf16[64,2,1024]{2,1,0:T(2,128)(2,1)S(1)} %get-tuple-element.30), channel_id=1, source_target_pairs={{0,1},{1,2},{2,3},{3,4},{4,5},{5,6},{6,7},{7,8},{8,9},{9,10},{10,1... | collective-permute-start | bytes 786440 | tf_op jit(solution)/shard_map/ppermute | solution.py:15
  5.8 6.0 %collective-permute-start = (bf16[64,2,1024]{2,1,0:T(2,128)(2,1)S(1)}, bf16[64,2,1024]{2,1,0:T(2,128)(2,1)S(1)}, u32[]{:S(2)}, u32[]{:S(2)}) collective-permute-start(bf16[64,2,1024]{2,1,0:T(2,128)(2,1)S(1)} %get-tuple-element.29), channel_id=1, source_target_pairs={{1,0},{2,1},{3,2},{4,3},{5,4},{6,5},{7,6},{8,7},{9,8},{10,9},{11,1... | collective-permute-start | bytes 786440 | tf_op jit(solution)/shard_map/ppermute | solution.py:15
  11.9 0.7 fusion.24
  12.5 0.1 slice_subtract_fusion
  12.6 0.7 fusion.23
  13.3 0.8 %convert_multiply_fusion = f32[4,16]{1,0:T(4,128)S(1)} fusion(s32[4,16]{1,0:T(4,128)} %param.6, f32[4]{0:T(128)} %constant.46), kind=kLoop, calls=%fused_computation.51 | loop fusion | flops 128 | bytes 528 | tf_op jit(solution)/shard_map/mul | solution.py:21
  14.0 0.1 multiply_subtract_fusion
  14.2 1.4 %fusion.19 = f32[1,16]{1,0:T(1,128)S(1)} fusion(f32[1]{0:T(128)} %get-tuple-element.48, f32[1]{0:T(128)} %get-tuple-element.47), kind=kLoop, calls=%fused_computation.73 | loop fusion | flops 64 | bytes 72 | tf_op jit(solution)/shard_map/stack | solution.py:30
  15.6 0.1 add_convert_fusion.refs_1_
  15.7 0.1 pad.50.clone
  15.8 0.0 slice-start
  15.8 0.9 %slice_convert_fusion = (f32[2,16,1024]{2,1,0:T(8,128)S(1)}, f32[2,16,1024]{2,1,0:T(8,128)S(1)}) fusion(bf16[64,16,1024]{2,1,0:T(8,128)(2,1)} %refs_2_.1), kind=kLoop, calls=%fused_computation.6 | loop fusion | flops 65536 | bytes 393216 | tf_op jit(solution)/shard_map/convert_element_type | solution.py:233
  16.8 0.0 copy-start
  16.8 0.0 collective-permute-done.1
  16.8 0.6 collective-permute-done
  17.4 0.6 pad_maximum_fusion
  18.1 0.0 slice-done
  18.1 1.3 %collective-permute-start.2 = (bf16[4,24,1024]{2,1,0:T(8,128)(2,1)S(1)}, bf16[4,24,1024]{2,1,0:T(8,128)(2,1)S(1)}, u32[]{:S(2)}, u32[]{:S(2)}) collective-permute-start(bf16[4,24,1024]{2,1,0:T(8,128)(2,1)S(1)} %pad_maximum_fusion.3), channel_id=1, source_target_pairs={{32,0},{64,32},{96,64},{128,96},{160,128},{192,160},{224,192},{33,... | collective-permute-start | bytes 589832 | tf_op jit(solution)/shard_map/ppermute | solution.py:15
  19.4 0.0 copy-done
  19.4 30.2 %shard_map.46 = (f32[3,16,1024]{2,1,0:T(8,128)S(1)}, f32[16,1024]{1,0:T(8,128)S(1)}, f32[16,1024]{1,0:T(8,128)S(1)}, f32[4,16,1024]{2,1,0:T(8,128)S(1)}, f32[4,16,1024]{2,1,0:T(8,128)S(1)}) custom-call(f32[10,16]{1,0:T(8,128)S(1)} %stack.62.refs_0_, s32[4]{0:T(128)S(1)} %add_convert_fusion.refs_1_, bf16[64,16,1024]{2,1,0:T(8,128)(2,1)S(1)} %copy-done, ...), custom_call_target="tpu_custom_call" | custom-call | tf_op jit(solution)/shard_map/pallas_call | solution.py:206
  49.7 0.0 collective-permute-done.2
  49.8 3.4 %shard_map.47 = (f32[3,16,1024]{2,1,0:T(8,128)S(1)}, f32[16,1024]{1,0:T(8,128)S(1)}) custom-call(f32[10,16]{1,0:T(8,128)S(1)} %stack.62.refs_0_, s32[4]{0:T(128)S(1)} %add_convert_fusion.refs_1_, f32[2,24,1024]{2,1,0:T(8,128)S(1)} %pad_maximum_fusion.2.refs_2_, f32[6,24,1024]{2,1,0:T(8,128)S(1)} %pad_maximum_fusion.1.refs_3_, ...), custom_call_target="tpu_custom_call" | custom-call | tf_op jit(solution)/shard_map/pallas_call | solution.py:216
  53.2 12.3 %all_to_all.5 = f32[8,4,16,128]{3,2,1,0:T(8,128)S(1)} all-to-all(f32[8,4,16,128]{3,2,1,0:T(8,128)S(1)} %maximum_bitcast_fusion), channel_id=1, replica_groups=mesh['depth'=8,'tile'=32] {'depth'}, dimensions={0} | all-to-all | bytes 524288 | tf_op jit(solution)/shard_map/all_to_all | solution.py:248
  65.7 0.6 pad_maximum_fusion.4
  (25 shorter events, 0.3 us)
Async XLA Ops:
  2.0 14.8 %collective-permute-start.1 = (bf16[64,2,1024]{2,1,0:T(2,128)(2,1)S(1)}, bf16[64,2,1024]{2,1,0:T(2,128)(2,1)S(1)}, u32[]{:S(2)}, u32[]{:S(2)}) collective-permute-start(bf16[64,2,1024]{2,1,0:T(2,128)(2,1)S(1)} %get-tuple-element.30), channel_id=1, source_target_pairs={{0,1},{1,2},{2,3},{3,4},{4,5},{5,6},{6,7},{7,8},{8,9},{9,10},{10,1... | collective-permute-start | bytes 786440 | tf_op jit(solution)/shard_map/ppermute | solution.py:15
  5.8 11.6 %collective-permute-start = (bf16[64,2,1024]{2,1,0:T(2,128)(2,1)S(1)}, bf16[64,2,1024]{2,1,0:T(2,128)(2,1)S(1)}, u32[]{:S(2)}, u32[]{:S(2)}) collective-permute-start(bf16[64,2,1024]{2,1,0:T(2,128)(2,1)S(1)} %get-tuple-element.29), channel_id=1, source_target_pairs={{1,0},{2,1},{3,2},{4,3},{5,4},{6,5},{7,6},{8,7},{9,8},{10,9},{11,1... | collective-permute-start | bytes 786440 | tf_op jit(solution)/shard_map/ppermute | solution.py:15
  15.8 2.2 %slice-start = ((bf16[64,16,1024]{2,1,0:T(8,128)(2,1)}), bf16[4,16,1024]{2,1,0:T(8,128)(2,1)S(1)}, s32[]{:S(2)}) async-start(bf16[64,16,1024]{2,1,0:T(8,128)(2,1)} %refs_2_.1), calls=%async_computation.1 | async-start | bytes 262144 | tf_op jit(solution)/shard_map/slice | solution.py:235
  16.8 2.7 %copy-start = (bf16[64,16,1024]{2,1,0:T(8,128)(2,1)S(1)}, bf16[64,16,1024]{2,1,0:T(8,128)(2,1)}, u32[]{:S(2)}) copy-start(bf16[64,16,1024]{2,1,0:T(8,128)(2,1)} %refs_2_.1) | copy-start | bytes 6291460
  18.1 31.6 %collective-permute-start.2 = (bf16[4,24,1024]{2,1,0:T(8,128)(2,1)S(1)}, bf16[4,24,1024]{2,1,0:T(8,128)(2,1)S(1)}, u32[]{:S(2)}, u32[]{:S(2)}) collective-permute-start(bf16[4,24,1024]{2,1,0:T(8,128)(2,1)S(1)} %pad_maximum_fusion.3), channel_id=1, source_target_pairs={{32,0},{64,32},{96,64},{128,96},{160,128},{192,160},{224,192},{33,... | collective-permute-start | bytes 589832 | tf_op jit(solution)/shard_map/ppermute | solution.py:15
